TPU v7x, 128 devices: a whole 4x4x4 slice. The times are simulated.
128 devices in a mesh: iface: 4 (over x), sub: 32 (over y, z, core).
Axes of the slice: x: 4, y: 4, z: 4, core: 2. Of those that a mesh axis runs over, the one named last changes fastest.
Arguments:
- schur_blocks: bfloat16 [2048, 512, 512], P('sub', 'iface'), as said below
- noise_field: float32 [32, 2048, 512], P(None, 'sub', 'iface')
- peer_device: int32 [2048, 512], P('sub', 'iface'), may hold values from 0 to 127, as said below
- partner_slot: int32 [2048, 512], P('sub', 'iface'), may hold values from 0 to 8191, as said below
- pivot_rows: int32 [32], replicated, may hold values from 0 to 1048575
Outputs:
- constraints: float32 [32, 2048, 512], P(None, 'sub', 'iface')
Inputs may be any that keep to these rules, and one draw needn't show every extreme that they name: `schur_blocks`: each block is exactly symmetric and positive definite. Devices are numbered iface index times the size of sub plus sub index; a device's dofs are numbered local subdomain * 128 + dof within its group. If peer_device names the holding device, the partner is that device's dof number partner_slot. Otherwise the partner is the dof of device peer_device that names this device with the same partner_slot, which is then below 64. Two devices share at most 64 pairs, and exactly 64 in every draw for some two devices. The relation is symmetric. `partner_slot`: see peer_device.
All inputs are finite; a program needn't handle non-finite values.
Results may differ from a plain program's by a relative error of at most 0.0071.
Values may be sent and summed in bfloat16 or wider, within the bound.
No kernel may reach another device: no remote copies, remote signals or barrier semaphores. Data moves between devices by JAX's collectives and lax.ppermute only.
A program may use at most 128 MiB of HBM per device.

v0:
```python
import math

import jax
import jax.numpy as jnp
from jax import lax
from jax.experimental import pallas as pl
from jax.experimental.pallas import tpu as pltpu
from jax.sharding import PartitionSpec as P

UNROLL = 16


def _pack_kernel(slot_ref, x_ref, o_ref, buf):
    rows = x_ref.shape[0]
    buf[...] = jnp.zeros_like(buf)
    def body(j, carry):
        for u in range(UNROLL):
            i = j * UNROLL + u
            buf[pl.ds(slot_ref[i], 1), :] = x_ref[pl.ds(i, 1), :]
        return carry
    lax.fori_loop(0, rows // UNROLL, body, 0)
    width = x_ref.shape[1]
    per = o_ref.shape[1] // width
    n = o_ref.shape[0]
    lane = lax.broadcasted_iota(jnp.int32, (n, o_ref.shape[1]), 1) // width
    acc = jnp.zeros((n, o_ref.shape[1]), jnp.float32)
    for t in range(per):
        piece = buf[pl.ds(t, n, stride=per), :]
        wide = jnp.concatenate([piece] + [jnp.zeros_like(piece)] * (per - 1), axis=1)
        if t:
            wide = pltpu.roll(wide, shift=width * t, axis=1)
        acc = jnp.where(lane == t, wide, acc)
    o_ref[...] = acc

def _unpack_kernel(src_ref, v_ref, inc_ref, o_ref, joined, picked):
    rows, width = v_ref.shape
    n, lanes = inc_ref.shape
    per = lanes // width
    joined[pl.ds(0, rows), :] = v_ref[...]
    inc = inc_ref[...]
    for t in range(per):
        part = inc if t == 0 else pltpu.roll(inc, shift=lanes - width * t, axis=1)
        joined[pl.ds(rows + t, n, stride=per), :] = part[:, :width]
    def body(j, carry):
        for u in range(UNROLL):
            q = j * UNROLL + u
            picked[pl.ds(q, 1), :] = joined[pl.ds(src_ref[q], 1), :]
        return carry
    lax.fori_loop(0, rows // UNROLL, body, 0)
    o_ref[...] = v_ref[...] - picked[...]

def pack_rows(x, send_pos):
    rows, width = x.shape
    return pl.pallas_call(_pack_kernel,
        in_specs=[pl.BlockSpec(memory_space=pltpu.SMEM), pl.BlockSpec(memory_space=pltpu.VMEM)],
        out_specs=pl.BlockSpec(memory_space=pltpu.VMEM),
        out_shape=jax.ShapeDtypeStruct((rows * width // 128, 128), x.dtype),
        scratch_shapes=[pltpu.VMEM((rows + 8, width), x.dtype)],
        compiler_params=pltpu.CompilerParams(vmem_limit_bytes=48 * 1024 * 1024))(send_pos, x)

def unpack_jump(v, incoming, source):
    rows, width = v.shape
    return pl.pallas_call(_unpack_kernel,
        in_specs=[pl.BlockSpec(memory_space=pltpu.SMEM), pl.BlockSpec(memory_space=pltpu.VMEM), pl.BlockSpec(memory_space=pltpu.VMEM)],
        out_specs=pl.BlockSpec(memory_space=pltpu.VMEM),
        out_shape=jax.ShapeDtypeStruct((rows, width), v.dtype),
        scratch_shapes=[pltpu.VMEM((2 * rows, width), v.dtype), pltpu.VMEM((rows, width), v.dtype)],
        compiler_params=pltpu.CompilerParams(vmem_limit_bytes=48 * 1024 * 1024))(source, v, incoming)


def partner_jump(rows_in, routing, device_count):
    send_pos, source = routing
    outgoing = pack_rows(rows_in, send_pos)
    incoming = lax.all_to_all(outgoing, ("iface", "sub"), split_axis=0, concat_axis=0, tiled=True)
    return unpack_jump(rows_in, incoming, source)


def apply_blocks(jump_rows, schur_blocks, sub_local, group):
    width = jump_rows.shape[1]
    half = jump_rows.astype(jnp.bfloat16).reshape(sub_local, group, width).transpose(2, 0, 1)
    gathered = lax.all_gather(half, "iface", axis=2, tiled=True)
    result = jnp.einsum("src,ksc->srk", schur_blocks, gathered, preferred_element_type=jnp.float32)
    return result.reshape(sub_local * group, width)


def combine_weights(gram_matrix, picked, total_rows, sample_count):
    lower = jnp.linalg.cholesky(gram_matrix)
    solved = jax.scipy.linalg.cho_solve((lower, True), picked)
    coupling = jnp.dot(picked.T, solved, precision=lax.Precision.HIGHEST) * (
        total_rows / sample_count
    ) + jnp.eye(sample_count, dtype=jnp.float32)
    lower_two = jnp.linalg.cholesky(coupling)
    return jax.scipy.linalg.cho_solve((lower_two, True), solved.T) * (
        total_rows / math.sqrt(sample_count)
    )


def shards(schur_blocks, noise_field, peer_device, partner_slot, pivot_rows):
    sample_count, sub_local, group = noise_field.shape
    row_count = sub_local * group
    iface_count = lax.axis_size("iface")
    sub_count = lax.axis_size("sub")
    device_count = iface_count * sub_count
    capacity = row_count // device_count
    full_width = group * iface_count
    iface_place = lax.axis_index("iface")
    sub_place = lax.axis_index("sub")
    device_self = iface_place * sub_count + sub_place
    peer_flat = peer_device.reshape(row_count)
    slot_flat = partner_slot.reshape(row_count)
    crossing = peer_flat != device_self
    send_pos = jnp.clip(
        jnp.where(crossing, peer_flat * capacity + slot_flat, row_count), 0, row_count
    ).astype(jnp.int32)
    source = jnp.clip(
        jnp.where(crossing, row_count + peer_flat * capacity + slot_flat, slot_flat),
        0,
        2 * row_count - 1,
    ).astype(jnp.int32)
    routing = (send_pos, source)
    noise_rows = noise_field.transpose(1, 2, 0).reshape(row_count, sample_count)
    first_jump = partner_jump(noise_rows, routing, device_count)
    response_one = apply_blocks(first_jump, schur_blocks, sub_local, group)
    second_jump = partner_jump(response_one, routing, device_count)
    response_two = apply_blocks(second_jump, schur_blocks, sub_local, group)
    samples = partner_jump(response_two, routing, device_count)
    gram_part = lax.dot_general(
        samples,
        samples,
        (((0,), (0,)), ((), ())),
        precision=lax.Precision.HIGHEST,
        preferred_element_type=jnp.float32,
    )
    pivot_sub = pivot_rows // full_width
    pivot_dof = pivot_rows % full_width
    holder = (pivot_sub // sub_local == sub_place) & (pivot_dof // group == iface_place)
    local_row = pivot_sub % sub_local * group + pivot_dof % group
    picked_part = jnp.take(samples, local_row, axis=0, mode="clip").T * holder[None, :].astype(
        jnp.float32
    )
    partial = jnp.concatenate((gram_part, picked_part), axis=1)[None]
    over_sub = jnp.sum(lax.all_gather(partial, "sub", axis=0, tiled=True), axis=0, keepdims=True)
    total = jnp.sum(lax.all_gather(over_sub, "iface", axis=0, tiled=True), axis=0)
    gram_matrix = total[:, :sample_count]
    picked = total[:, sample_count:]
    total_rows = float(sub_local * sub_count * full_width)
    coefficients = combine_weights(gram_matrix, picked, total_rows, sample_count)
    constraint_rows = lax.dot_general(
        coefficients,
        samples,
        (((1,), (1,)), ((), ())),
        precision=lax.Precision.HIGHEST,
        preferred_element_type=jnp.float32,
    )
    return constraint_rows.reshape(sample_count, sub_local, group)


def solution(mesh):
    placed = (
        P("sub", "iface", None),
        P(None, "sub", "iface"),
        P("sub", "iface"),
        P("sub", "iface"),
        P(),
    )
    return jax.shard_map(
        shards, mesh=mesh, in_specs=placed, out_specs=P(None, "sub", "iface"), check_vma=False
    )
```

profile of v0, /device:TPU:0, one launch (start us, length us, event | category | flops | bytes accessed | tf_op | source)
XLA Modules:
  0.0 333.6 jit_solution(7257344214639847070)
XLA Ops:
  6.5 3.6 %copy.15 = f32[64,128,32]{2,1,0:T(8,128)} copy(f32[64,128,32]{1,0,2:T(8,128)} %bitcast.93) | data formatting | bytes 2097152 | tf_op jit(solution)/shard_map/transpose | solution.py:121
  10.2 2.2 copy-done.2
  12.4 11.1 %shard_map.55 = f32[2048,128]{1,0:T(8,128)S(1)} custom-call(s32[8192]{0:T(1024)S(1)} %get-tuple-element.9.slot_ref, f32[8192,32]{1,0:T(8,128)S(1)} %bitcast.80), custom_call_target="tpu_custom_call" | custom-call | tf_op jit(solution)/shard_map/pallas_call | solution.py:54
  23.5 30.3 %all_to_all.33 = f32[128,16,128]{2,1,0:T(8,128)S(1)} all-to-all(f32[128,16,128]{2,1,0:T(8,128)S(1)} %bitcast.86), channel_id=1, replica_groups=mesh['iface'=4,'sub'=32] {'iface','sub'}, dimensions={0} | all-to-all | bytes 2097152 | tf_op jit(solution)/shard_map/all_to_all | solution.py:74
  53.8 12.6 %shard_map.56 = f32[8192,32]{1,0:T(8,128)S(1)} custom-call(s32[8192]{0:T(1024)S(1)} %get-tuple-element.10.src_ref, f32[8192,32]{1,0:T(8,128)} %bitcast.79, f32[2048,128]{1,0:T(8,128)S(1)} %bitcast.84), custom_call_target="tpu_custom_call" | custom-call | tf_op jit(solution)/shard_map/pallas_call | solution.py:63
  66.6 1.5 copy.16
  68.2 29.7 %all-gather.5.cloned.1.call-done = bf16[32,64,512]{2,0,1:T(8,128)(2,1)} async-done(((bf16[32,64,128]{2,0,1:T(8,128)(2,1)}), bf16[32,64,512]{2,0,1:T(8,128)(2,1)}) %all-gather.5.cloned.1.call-update) | async-done | bytes 2097168 | tf_op jit(solution)/shard_map/all_gather | solution.py:81
  97.9 6.9 %convolution_bitcast_fusion.2 = f32[64,128,32]{1,2,0:T(8,128)S(1)} fusion(bf16[32,64,512]{2,0,1:T(8,128)(2,1)} %all-gather.5.cloned.1.call-done, bf16[64,128,512]{2,1,0:T(8,128)(2,1)} %param.8), kind=kOutput, calls=%fused_computation.3 | convolution fusion | flops 268435456 | bytes 11534336 | tf_op jit(solution)/shard_map/src,ksc->srk/dot_general | solution.py:82
  104.8 2.6 copy.17
  107.4 2.2 copy-done.3
  109.6 11.1 %shard_map.57 = f32[2048,128]{1,0:T(8,128)S(1)} custom-call(s32[8192]{0:T(1024)S(1)} %get-tuple-element.9.slot_ref, f32[8192,32]{1,0:T(8,128)S(1)} %bitcast.82), custom_call_target="tpu_custom_call" | custom-call | tf_op jit(solution)/shard_map/pallas_call | solution.py:54
  120.8 28.8 %all_to_all.34 = f32[128,16,128]{2,1,0:T(8,128)S(1)} all-to-all(f32[128,16,128]{2,1,0:T(8,128)S(1)} %bitcast.87), channel_id=1, replica_groups=mesh['iface'=4,'sub'=32] {'iface','sub'}, dimensions={0} | all-to-all | bytes 2097152 | tf_op jit(solution)/shard_map/all_to_all | solution.py:74
  149.6 12.6 %shard_map.58 = f32[8192,32]{1,0:T(8,128)S(1)} custom-call(s32[8192]{0:T(1024)S(1)} %get-tuple-element.10.src_ref, f32[8192,32]{1,0:T(8,128)} %bitcast.81, f32[2048,128]{1,0:T(8,128)S(1)} %bitcast.85), custom_call_target="tpu_custom_call" | custom-call | tf_op jit(solution)/shard_map/pallas_call | solution.py:63
  162.3 1.5 copy.18
  163.9 29.8 %all-gather.7.cloned.1.call-done = bf16[32,64,512]{2,0,1:T(8,128)(2,1)} async-done(((bf16[32,64,128]{2,0,1:T(8,128)(2,1)}), bf16[32,64,512]{2,0,1:T(8,128)(2,1)}) %all-gather.7.cloned.1.call-update) | async-done | bytes 2097168 | tf_op jit(solution)/shard_map/all_gather | solution.py:81
  193.6 6.9 %convolution_bitcast_fusion.1 = f32[64,128,32]{1,2,0:T(8,128)S(1)} fusion(bf16[32,64,512]{2,0,1:T(8,128)(2,1)} %all-gather.7.cloned.1.call-done, bf16[64,128,512]{2,1,0:T(8,128)(2,1)} %param.8), kind=kOutput, calls=%fused_computation.2 | convolution fusion | flops 268435456 | bytes 11534336 | tf_op jit(solution)/shard_map/src,ksc->srk/dot_general | solution.py:82
  200.5 2.6 copy.19
  203.2 2.2 copy-done.1
  205.4 12.1 %shard_map.59 = f32[2048,128]{1,0:T(8,128)} custom-call(s32[8192]{0:T(1024)S(1)} %get-tuple-element.9.slot_ref, f32[8192,32]{1,0:T(8,128)S(1)} %bitcast.78), custom_call_target="tpu_custom_call" | custom-call | tf_op jit(solution)/shard_map/pallas_call | solution.py:54
  217.5 9.9 %all-to-all-start.2 = ((f32[128,16,128]{2,1,0:T(8,128)}), f32[128,16,128]{2,1,0:T(8,128)S(1)}, u32[]{:S(2)}, u32[]{:S(2)}) async-start(f32[128,16,128]{2,1,0:T(8,128)} %bitcast.17), calls=%async_computation.2 | async-start | bytes 2097152 | tf_op jit(solution)/shard_map/all_to_all | solution.py:74
  227.4 19.1 %all-to-all-done.2 = f32[128,16,128]{2,1,0:T(8,128)S(1)} async-done(((f32[128,16,128]{2,1,0:T(8,128)}), f32[128,16,128]{2,1,0:T(8,128)S(1)}, u32[]{:S(2)}, u32[]{:S(2)}) %all-to-all-start.2) | async-done | bytes 1048608 | tf_op jit(solution)/shard_map/all_to_all | solution.py:74
  246.5 12.6 %shard_map.60 = f32[8192,32]{1,0:T(8,128)S(1)} custom-call(s32[8192]{0:T(1024)S(1)} %get-tuple-element.10.src_ref, f32[8192,32]{1,0:T(8,128)} %bitcast.77, f32[2048,128]{1,0:T(8,128)S(1)} %bitcast.83), custom_call_target="tpu_custom_call" | custom-call | tf_op jit(solution)/shard_map/pallas_call | solution.py:63
  259.0 1.9 copy-done
  260.9 6.7 %fusion.22 = f32[32,32]{1,0:T(8,128)S(1)} fusion(f32[8192,32]{1,0:T(8,128)S(1)} %shard_map.60), kind=kOutput, calls=%fused_computation.61 | convolution fusion | flops 100663296 | bytes 1052672 | tf_op jit(solution)/shard_map/dot_general | solution.py:127
  267.6 2.8 gather_fusion
  270.6 22.3 %all-gather = f32[1024,64]{1,0:T(8,128)S(1)} all-gather(f32[32,64]{1,0:T(8,128)S(1)} %pad_maximum_fusion), channel_id=2, replica_groups=mesh['iface'=4,'sub'=32] {'sub'}, dimensions={0}, use_global_device_ids=true | all-gather | bytes 270336 | tf_op jit(solution)/shard_map/all_gather | solution.py:142
  292.9 12.1 %all-gather.1 = f32[128,64]{1,0:T(8,128)S(1)} all-gather(f32[32,64]{1,0:T(8,128)S(1)} %reduce_sum.18), channel_id=3, replica_groups=mesh['iface'=4,'sub'=32] {'iface'}, dimensions={0}, use_global_device_ids=true | all-gather | bytes 40960 | tf_op jit(solution)/shard_map/all_gather | solution.py:143
  305.1 2.9 cholesky.44
  309.4 2.4 custom-call.8
  312.5 2.9 cholesky.55
  316.8 2.4 custom-call.9
  319.6 6.0 %convolution_bitcast_fusion = f32[4,8,64,128]{3,1,2,0:T(8,128)S(1)} fusion(f32[32,32]{1,0:T(8,128)S(1)} %convolution_multiply_fusion, f32[8192,32]{1,0:T(8,128)} %copy-done), kind=kOutput, calls=%fused_computation.1 | convolution fusion | flops 100663296 | bytes 2101248 | tf_op jit(solution)/shard_map/dot_general | solution.py:148
  (41 shorter events, 5.8 us)
Async XLA Ops:
  6.5 3.6 %copy-start.5 = (s32[64,128]{1,0:T(8,128)S(1)}, s32[64,128]{1,0:T(8,128)}, u32[]{:S(2)}) copy-start(s32[64,128]{1,0:T(8,128)} %param.10) | copy-start | bytes 98308
  6.5 3.6 %copy-start.4 = (s32[64,128]{1,0:T(8,128)S(1)}, s32[64,128]{1,0:T(8,128)}, u32[]{:S(2)}) copy-start(s32[64,128]{1,0:T(8,128)} %param.11) | copy-start | bytes 98308
  6.5 91.4 %all-gather.5.cloned.1.call-start = ((), (), s32[]{:S(2)}) async-start(), calls=%async_computation.3 | async-start | bytes 2621440 | tf_op jit(solution)/shard_map/all_gather | solution.py:81
  10.2 2.2 copy-start.2
  68.1 125.5 %all-gather.7.cloned.1.call-start = ((), (), s32[]{:S(2)}) async-start(), calls=%async_computation.4 | async-start | bytes 2621440 | tf_op jit(solution)/shard_map/all_gather | solution.py:81
  107.4 2.2 copy-start.3
  203.1 24.2 %copy-start.6 = (s32[32]{0:T(128)S(1)}, s32[32]{0:T(128)}, u32[]{:S(2)}) copy-start(s32[32]{0:T(128)} %param.12) | copy-start | bytes 388
  203.2 2.2 copy-start.1
  217.5 29.0 %all-to-all-start.2 = ((f32[128,16,128]{2,1,0:T(8,128)}), f32[128,16,128]{2,1,0:T(8,128)S(1)}, u32[]{:S(2)}, u32[]{:S(2)}) async-start(f32[128,16,128]{2,1,0:T(8,128)} %bitcast.17), calls=%async_computation.2 | async-start | bytes 2097152 | tf_op jit(solution)/shard_map/all_to_all | solution.py:74
  259.0 1.9 copy-start
Sparse Core Ops, SparseCore 0:
  68.3 29.6 all-gather.4
  164.0 29.6 all-gather.6
where the time goes:
time: 334 us
  blocking collectives  93.5 us (28%)
  waiting for transfers between devices  78.6 us (24%)
  Pallas kernels  72 us (22%)
  matrix products  27.5 us (8%)
  local copies, waits for them, and re-layouts  24.5 us (7%)
  other arithmetic  14 us (4%)
  between operations  13.6 us (4%)
  starting transfers between devices  9.91 us (3%)
    all_gather x2, waiting for transfers between devices, apply_blocks(): gathered = lax.all_gather(half, 'iface', axis=2, tiled=True)  59.5 us
    all_to_all x2, blocking collectives, partner_jump(): lax.all_to_all(outgoing, ('iface', 'sub'), split_axis=0, concat_axis=0, t...  59.1 us
    pallas_call x3, Pallas kernels, unpack_jump(): pl.pallas_call(_unpack_kernel, in_specs=[pl.BlockSpec(memory_space=pltpu....  37.7 us
    pallas_call x3, Pallas kernels, pack_rows(): pl.pallas_call(_pack_kernel, in_specs=[pl.BlockSpec(memory_space=pltpu.SM...  34.4 us
    all_gather x1, blocking collectives, shards(): lax.all_gather(partial, 'sub', axis=0, tiled=True)  22.3 us
    all_to_all x1, waiting for transfers between devices, partner_jump(): lax.all_to_all(outgoing, ('iface', 'sub'), split_axis=0, concat_axis=0, t...  19.1 us
    dot_general x2, matrix products, apply_blocks(): jnp.einsum('src,ksc->srk', schur_blocks, gathered, preferred_element_type...  13.8 us
    all_gather x1, blocking collectives, shards(): lax.all_gather(over_sub, 'iface', axis=0, tiled=True)  12.1 us
  transfers between devices with their start and end apart: 3, of which 3 were waited for; matrix products, arithmetic and copies ran while one was open for 0% of the time, Pallas kernels for 0%

commit v1 on v0

--- a/solution.py
+++ b/solution.py
@@ -1,3 +1,4 @@
+import functools
 import math
 
 import jax
@@ -7,23 +8,28 @@
 from jax.experimental.pallas import tpu as pltpu
 from jax.sharding import PartitionSpec as P
 
-UNROLL = 16
-
-
-def _pack_kernel(slot_ref, x_ref, o_ref, buf):
-    rows = x_ref.shape[0]
+UNROLL = 32
+PIECES = 2
+
+
+def _pack_kernel(slot_ref, *refs):
+    x_refs, o_ref, buf = refs[:-2], refs[-2], refs[-1]
     buf[...] = jnp.zeros_like(buf)
-    def body(j, carry):
-        for u in range(UNROLL):
-            i = j * UNROLL + u
-            buf[pl.ds(slot_ref[i], 1), :] = x_ref[pl.ds(i, 1), :]
-        return carry
-    lax.fori_loop(0, rows // UNROLL, body, 0)
-    width = x_ref.shape[1]
-    per = o_ref.shape[1] // width
-    n = o_ref.shape[0]
-    lane = lax.broadcasted_iota(jnp.int32, (n, o_ref.shape[1]), 1) // width
-    acc = jnp.zeros((n, o_ref.shape[1]), jnp.float32)
+    offset = 0
+    for x_ref in x_refs:
+        def body(j, carry, x_ref=x_ref, offset=offset):
+            base = pl.multiple_of(j * UNROLL, UNROLL)
+            for u in range(UNROLL):
+                buf[pl.ds(slot_ref[offset + base + u], 1), :] = x_ref[pl.ds(base + u, 1), :]
+            return carry
+
+        lax.fori_loop(0, x_ref.shape[0] // UNROLL, body, 0)
+        offset += x_ref.shape[0]
+    width = buf.shape[1]
+    n, lanes = o_ref.shape
+    per = lanes // width
+    lane = lax.broadcasted_iota(jnp.int32, (n, lanes), 1) // width
+    acc = jnp.zeros((n, lanes), jnp.float32)
     for t in range(per):
         piece = buf[pl.ds(t, n, stride=per), :]
         wide = jnp.concatenate([piece] + [jnp.zeros_like(piece)] * (per - 1), axis=1)
@@ -32,55 +38,98 @@
         acc = jnp.where(lane == t, wide, acc)
     o_ref[...] = acc
 
-def _unpack_kernel(src_ref, v_ref, inc_ref, o_ref, joined, picked):
-    rows, width = v_ref.shape
+
+def _unpack_kernel(first, count, src_ref, *refs):
+    v_refs, inc_ref, o_ref, joined, picked = refs[:-4], refs[-4], refs[-3], refs[-2], refs[-1]
+    rows = sum(v_ref.shape[0] for v_ref in v_refs)
+    width = v_refs[0].shape[1]
     n, lanes = inc_ref.shape
     per = lanes // width
-    joined[pl.ds(0, rows), :] = v_ref[...]
+    offset = 0
+    for v_ref in v_refs:
+        joined[pl.ds(offset, v_ref.shape[0]), :] = v_ref[...]
+        offset += v_ref.shape[0]
     inc = inc_ref[...]
     for t in range(per):
         part = inc if t == 0 else pltpu.roll(inc, shift=lanes - width * t, axis=1)
         joined[pl.ds(rows + t, n, stride=per), :] = part[:, :width]
+
     def body(j, carry):
+        base = pl.multiple_of(j * UNROLL, UNROLL)
         for u in range(UNROLL):
-            q = j * UNROLL + u
-            picked[pl.ds(q, 1), :] = joined[pl.ds(src_ref[q], 1), :]
+            picked[pl.ds(base + u, 1), :] = joined[pl.ds(src_ref[first + base + u], 1), :]
         return carry
-    lax.fori_loop(0, rows // UNROLL, body, 0)
-    o_ref[...] = v_ref[...] - picked[...]
-
-def pack_rows(x, send_pos):
-    rows, width = x.shape
-    return pl.pallas_call(_pack_kernel,
-        in_specs=[pl.BlockSpec(memory_space=pltpu.SMEM), pl.BlockSpec(memory_space=pltpu.VMEM)],
+
+    lax.fori_loop(0, count // UNROLL, body, 0)
+    offset = 0
+    for v_ref in v_refs:
+        low = max(offset, first)
+        high = min(offset + v_ref.shape[0], first + count)
+        if low < high:
+            o_ref[pl.ds(low - first, high - low), :] = (
+                v_ref[pl.ds(low - offset, high - low), :] - picked[pl.ds(low - first, high - low), :]
+            )
+        offset += v_ref.shape[0]
+
+
+def pack_rows(xs, send_pos):
+    rows = sum(x.shape[0] for x in xs)
+    width = xs[0].shape[1]
+    return pl.pallas_call(
+        _pack_kernel,
+        in_specs=[pl.BlockSpec(memory_space=pltpu.SMEM)]
+        + [pl.BlockSpec(memory_space=pltpu.VMEM)] * len(xs),
         out_specs=pl.BlockSpec(memory_space=pltpu.VMEM),
-        out_shape=jax.ShapeDtypeStruct((rows * width // 128, 128), x.dtype),
-        scratch_shapes=[pltpu.VMEM((rows + 8, width), x.dtype)],
-        compiler_params=pltpu.CompilerParams(vmem_limit_bytes=48 * 1024 * 1024))(send_pos, x)
-
-def unpack_jump(v, incoming, source):
-    rows, width = v.shape
-    return pl.pallas_call(_unpack_kernel,
-        in_specs=[pl.BlockSpec(memory_space=pltpu.SMEM), pl.BlockSpec(memory_space=pltpu.VMEM), pl.BlockSpec(memory_space=pltpu.VMEM)],
+        out_shape=jax.ShapeDtypeStruct((rows * width // 128, 128), xs[0].dtype),
+        scratch_shapes=[pltpu.VMEM((rows + 8, width), xs[0].dtype)],
+        compiler_params=pltpu.CompilerParams(vmem_limit_bytes=48 * 1024 * 1024),
+    )(send_pos, *xs)
+
+
+def unpack_jump(vs, incoming, source, first, count):
+    rows = sum(v.shape[0] for v in vs)
+    width = vs[0].shape[1]
+    return pl.pallas_call(
+        functools.partial(_unpack_kernel, first, count),
+        in_specs=[pl.BlockSpec(memory_space=pltpu.SMEM)]
+        + [pl.BlockSpec(memory_space=pltpu.VMEM)] * (len(vs) + 1),
         out_specs=pl.BlockSpec(memory_space=pltpu.VMEM),
-        out_shape=jax.ShapeDtypeStruct((rows, width), v.dtype),
-        scratch_shapes=[pltpu.VMEM((2 * rows, width), v.dtype), pltpu.VMEM((rows, width), v.dtype)],
-        compiler_params=pltpu.CompilerParams(vmem_limit_bytes=48 * 1024 * 1024))(source, v, incoming)
-
-
-def partner_jump(rows_in, routing, device_count):
-    send_pos, source = routing
-    outgoing = pack_rows(rows_in, send_pos)
-    incoming = lax.all_to_all(outgoing, ("iface", "sub"), split_axis=0, concat_axis=0, tiled=True)
-    return unpack_jump(rows_in, incoming, source)
+        out_shape=jax.ShapeDtypeStruct((count, width), vs[0].dtype),
+        scratch_shapes=[
+            pltpu.VMEM((2 * rows, width), vs[0].dtype),
+            pltpu.VMEM((count, width), vs[0].dtype),
+        ],
+        compiler_params=pltpu.CompilerParams(vmem_limit_bytes=48 * 1024 * 1024),
+    )(source, *vs, incoming)
+
+
+def exchange(parts, send_pos):
+    outgoing = pack_rows(parts, send_pos)
+    return lax.all_to_all(outgoing, ("iface", "sub"), split_axis=0, concat_axis=0, tiled=True)
 
 
 def apply_blocks(jump_rows, schur_blocks, sub_local, group):
     width = jump_rows.shape[1]
-    half = jump_rows.astype(jnp.bfloat16).reshape(sub_local, group, width).transpose(2, 0, 1)
+    count = jump_rows.shape[0] // group
+    half = jump_rows.astype(jnp.bfloat16).reshape(count, group, width).transpose(2, 0, 1)
     gathered = lax.all_gather(half, "iface", axis=2, tiled=True)
     result = jnp.einsum("src,ksc->srk", schur_blocks, gathered, preferred_element_type=jnp.float32)
-    return result.reshape(sub_local * group, width)
+    return result.reshape(count * group, width)
+
+
+def jump_and_apply(parts, routing, schur_blocks, sub_local, group, pieces):
+    send_pos, source = routing
+    incoming = exchange(parts, send_pos)
+    rows = sum(part.shape[0] for part in parts)
+    step = rows // pieces
+    sub_step = sub_local // pieces
+    out = []
+    for h in range(pieces):
+        jumped = unpack_jump(parts, incoming, source, h * step, step)
+        out.append(
+            apply_blocks(jumped, schur_blocks[h * sub_step:(h + 1) * sub_step], sub_step, group)
+        )
+    return out
 
 
 def combine_weights(gram_matrix, picked, total_rows, sample_count):
@@ -119,11 +168,10 @@
     ).astype(jnp.int32)
     routing = (send_pos, source)
     noise_rows = noise_field.transpose(1, 2, 0).reshape(row_count, sample_count)
-    first_jump = partner_jump(noise_rows, routing, device_count)
-    response_one = apply_blocks(first_jump, schur_blocks, sub_local, group)
-    second_jump = partner_jump(response_one, routing, device_count)
-    response_two = apply_blocks(second_jump, schur_blocks, sub_local, group)
-    samples = partner_jump(response_two, routing, device_count)
+    response_one = jump_and_apply([noise_rows], routing, schur_blocks, sub_local, group, PIECES)
+    response_two = jump_and_apply(response_one, routing, schur_blocks, sub_local, group, PIECES)
+    incoming = exchange(response_two, send_pos)
+    samples = unpack_jump(response_two, incoming, source, 0, row_count)
     gram_part = lax.dot_general(
         samples,
         samples,

time: 334 us -> 353 us (1.057)
  waiting for transfers between devices: 78.6 us -> 91.4 us
  matrix products: 27.5 us -> 33.1 us
    all_gather x2 -> x4, waiting for transfers between devices: 59.5 us -> 72.3 us  [apply_blocks(): gathered = lax.all_gather(half, 'iface', axis=2, tiled=True)]
    pallas_call x3, Pallas kernels: 34.4 us -> 29.5 us  [pack_rows(): pl.pallas_call(_pack_kernel, in_specs=[pl.BlockSpec(memory_space=pltpu.SM...]
    pallas_call x3 -> x5, Pallas kernels: 37.7 us -> 40.6 us  [unpack_jump(): pl.pallas_call(functools.partial(_unpack_kernel, first, count), in_specs=...]
    dot_general x2 -> x4, matrix products: 13.8 us -> 16 us  [apply_blocks(): jnp.einsum('src,ksc->srk', schur_blocks, gathered, preferred_element_type...]
    unnamed x16 -> x22, local copies, waits for them, and re-layouts: 9.73 us -> 9.18 us
  transfers between devices with their start and end apart: 3 -> 5, of which waited for: 3 -> 5; matrix products, arithmetic and copies ran while one was open for 0% -> 3% of each run, Pallas kernels for 0% -> 4%
where the time goes in v1:
time: 353 us
  blocking collectives  93.5 us (26%)
  waiting for transfers between devices  91.4 us (26%)
  Pallas kernels  70 us (20%)
  matrix products  33.1 us (9%)
  local copies, waits for them, and re-layouts  26.2 us (7%)
  other arithmetic  15 us (4%)
  between operations  13.4 us (4%)
  starting transfers between devices  9.99 us (3%)
    all_gather x4, waiting for transfers between devices, apply_blocks(): gathered = lax.all_gather(half, 'iface', axis=2, tiled=True)  72.3 us
    all_to_all x2, blocking collectives, exchange(): lax.all_to_all(outgoing, ('iface', 'sub'), split_axis=0, concat_axis=0, t...  59.1 us
    pallas_call x5, Pallas kernels, unpack_jump(): pl.pallas_call(functools.partial(_unpack_kernel, first, count), in_specs=...  40.6 us
    pallas_call x3, Pallas kernels, pack_rows(): pl.pallas_call(_pack_kernel, in_specs=[pl.BlockSpec(memory_space=pltpu.SM...  29.5 us
    all_gather x1, blocking collectives, shards(): lax.all_gather(partial, 'sub', axis=0, tiled=True)  22.3 us
    all_to_all x1, waiting for transfers between devices, exchange(): lax.all_to_all(outgoing, ('iface', 'sub'), split_axis=0, concat_axis=0, t...  19.1 us
    dot_general x4, matrix products, apply_blocks(): jnp.einsum('src,ksc->srk', schur_blocks, gathered, preferred_element_type...  16 us
    all_gather x1, blocking collectives, shards(): lax.all_gather(over_sub, 'iface', axis=0, tiled=True)  12.1 us
  transfers between devices with their start and end apart: 5, of which 5 were waited for; matrix products, arithmetic and copies ran while one was open for 3% of the time, Pallas kernels for 4%

profile of v1, /device:TPU:0, one launch (start us, length us, event | category | flops | bytes accessed | tf_op | source)
XLA Modules:
  0.0 352.7 jit_solution(9237013542745903471)
XLA Ops:
  6.5 3.6 %copy.19 = f32[64,128,32]{2,1,0:T(8,128)} copy(f32[64,128,32]{1,0,2:T(8,128)} %bitcast.113) | data formatting | bytes 2097152 | tf_op jit(solution)/shard_map/transpose | solution.py:170
  10.2 2.2 copy-done
  12.4 9.9 %shard_map.55 = f32[2048,128]{1,0:T(8,128)S(1)} custom-call(s32[8192]{0:T(1024)S(1)} %get-tuple-element.9.slot_ref, f32[8192,32]{1,0:T(8,128)S(1)} %bitcast.89), custom_call_target="tpu_custom_call" | custom-call | tf_op jit(solution)/shard_map/pallas_call | solution.py:78
  22.3 30.3 %all_to_all.33 = f32[128,16,128]{2,1,0:T(8,128)S(1)} all-to-all(f32[128,16,128]{2,1,0:T(8,128)S(1)} %bitcast.106), channel_id=1, replica_groups=mesh['iface'=4,'sub'=32] {'iface','sub'}, dimensions={0} | all-to-all | bytes 2097152 | tf_op jit(solution)/shard_map/all_to_all | solution.py:108
  52.6 7.5 %shard_map.57 = f32[4096,32]{1,0:T(8,128)S(1)} custom-call(s32[8192]{0:T(1024)S(1)} %get-tuple-element.10.src_ref, f32[8192,32]{1,0:T(8,128)} %bitcast.87, f32[2048,128]{1,0:T(8,128)S(1)} %bitcast.100), custom_call_target="tpu_custom_call" | custom-call | tf_op jit(solution)/shard_map/pallas_call | solution.py:92
  61.4 7.5 %shard_map.56 = f32[4096,32]{1,0:T(8,128)S(1)} custom-call(s32[8192]{0:T(1024)S(1)} %get-tuple-element.10.src_ref, f32[8192,32]{1,0:T(8,128)} %bitcast.88, f32[2048,128]{1,0:T(8,128)S(1)} %bitcast.101), custom_call_target="tpu_custom_call" | custom-call | tf_op jit(solution)/shard_map/pallas_call | solution.py:92
  70.1 12.4 %all-gather.9.cloned.1.call-done = bf16[32,32,512]{2,0,1:T(8,128)(2,1)} async-done(((bf16[32,32,128]{2,0,1:T(8,128)(2,1)}), bf16[32,32,512]{2,0,1:T(8,128)(2,1)}) %all-gather.9.cloned.1.call-update) | async-done | bytes 1048592 | tf_op jit(solution)/shard_map/all_gather | solution.py:115
  82.5 4.0 %fusion.14 = f32[32,128,32]{1,2,0:T(8,128)S(1)} fusion(bf16[32,32,512]{2,0,1:T(8,128)(2,1)} %all-gather.9.cloned.1.call-done, bf16[64,128,512]{2,1,0:T(8,128)(2,1)} %param.8), kind=kOutput, calls=%fused_computation.12 | convolution fusion | flops 134217728 | bytes 5767168 | tf_op jit(solution)/shard_map/src,ksc->srk/dot_general | solution.py:116
  87.2 23.4 %all-gather.7.cloned.1.call-done = bf16[32,32,512]{2,0,1:T(8,128)(2,1)} async-done(((bf16[32,32,128]{2,0,1:T(8,128)(2,1)}), bf16[32,32,512]{2,0,1:T(8,128)(2,1)}) %all-gather.7.cloned.1.call-update) | async-done | bytes 1048592 | tf_op jit(solution)/shard_map/all_gather | solution.py:115
  110.5 4.0 %fusion.8 = f32[32,128,32]{1,2,0:T(8,128)S(1)} fusion(bf16[32,32,512]{2,0,1:T(8,128)(2,1)} %all-gather.7.cloned.1.call-done, bf16[64,128,512]{2,1,0:T(8,128)(2,1)} %param.8), kind=kOutput, calls=%fused_computation.10 | convolution fusion | flops 134217728 | bytes 5767168 | tf_op jit(solution)/shard_map/src,ksc->srk/dot_general | solution.py:116
  118.1 9.8 %shard_map.58 = f32[2048,128]{1,0:T(8,128)S(1)} custom-call(s32[8192]{0:T(1024)S(1)} %get-tuple-element.9.slot_ref, f32[4096,32]{1,0:T(8,128)S(1)} %bitcast.93, f32[4096,32]{1,0:T(8,128)S(1)} %bitcast.90), custom_call_target="tpu_custom_call" | custom-call | tf_op jit(solution)/shard_map/pallas_call | solution.py:78
  127.8 28.8 %all_to_all.34 = f32[128,16,128]{2,1,0:T(8,128)S(1)} all-to-all(f32[128,16,128]{2,1,0:T(8,128)S(1)} %bitcast.107), channel_id=1, replica_groups=mesh['iface'=4,'sub'=32] {'iface','sub'}, dimensions={0} | all-to-all | bytes 2097152 | tf_op jit(solution)/shard_map/all_to_all | solution.py:108
  156.6 6.7 %shard_map.60 = f32[4096,32]{1,0:T(8,128)S(1)} custom-call(s32[8192]{0:T(1024)S(1)} %get-tuple-element.10.src_ref, f32[4096,32]{1,0:T(8,128)S(1)} %bitcast.94, f32[4096,32]{1,0:T(8,128)} %bitcast.91, f32[2048,128]{1,0:T(8,128)S(1)} %bitcast.102), custom_call_target="tpu_custom_call" | custom-call | tf_op jit(solution)/shard_map/pallas_call | solution.py:92
  164.5 2.3 copy.26
  166.8 6.7 %shard_map.59 = f32[4096,32]{1,0:T(8,128)S(1)} custom-call(s32[8192]{0:T(1024)S(1)} %get-tuple-element.10.src_ref, f32[4096,32]{1,0:T(8,128)S(1)} %bitcast.95, f32[4096,32]{1,0:T(8,128)} %bitcast.92, f32[2048,128]{1,0:T(8,128)S(1)} %bitcast.103), custom_call_target="tpu_custom_call" | custom-call | tf_op jit(solution)/shard_map/pallas_call | solution.py:92
  174.7 13.2 %all-gather.13.cloned.1.call-done = bf16[32,32,512]{2,0,1:T(8,128)(2,1)} async-done(((bf16[32,32,128]{2,0,1:T(8,128)(2,1)}), bf16[32,32,512]{2,0,1:T(8,128)(2,1)}) %all-gather.13.cloned.1.call-update) | async-done | bytes 1048592 | tf_op jit(solution)/shard_map/all_gather | solution.py:115
  188.0 4.0 %fusion.17 = f32[32,128,32]{1,2,0:T(8,128)S(1)} fusion(bf16[32,32,512]{2,0,1:T(8,128)(2,1)} %all-gather.13.cloned.1.call-done, bf16[64,128,512]{2,1,0:T(8,128)(2,1)} %param.8), kind=kOutput, calls=%fused_computation.13 | convolution fusion | flops 134217728 | bytes 5767168 | tf_op jit(solution)/shard_map/src,ksc->srk/dot_general | solution.py:116
  192.6 23.2 %all-gather.11.cloned.1.call-done = bf16[32,32,512]{2,0,1:T(8,128)(2,1)} async-done(((bf16[32,32,128]{2,0,1:T(8,128)(2,1)}), bf16[32,32,512]{2,0,1:T(8,128)(2,1)}) %all-gather.11.cloned.1.call-update) | async-done | bytes 1048592 | tf_op jit(solution)/shard_map/all_gather | solution.py:115
  215.8 4.0 %fusion.11 = f32[32,128,32]{1,2,0:T(8,128)S(1)} fusion(bf16[32,32,512]{2,0,1:T(8,128)(2,1)} %all-gather.11.cloned.1.call-done, bf16[64,128,512]{2,1,0:T(8,128)(2,1)} %param.8), kind=kOutput, calls=%fused_computation.11 | convolution fusion | flops 134217728 | bytes 5767168 | tf_op jit(solution)/shard_map/src,ksc->srk/dot_general | solution.py:116
  223.4 9.8 %shard_map.61 = f32[2048,128]{1,0:T(8,128)S(1)} custom-call(s32[8192]{0:T(1024)S(1)} %get-tuple-element.9.slot_ref, f32[4096,32]{1,0:T(8,128)S(1)} %bitcast.98, f32[4096,32]{1,0:T(8,128)S(1)} %bitcast.96), custom_call_target="tpu_custom_call" | custom-call | tf_op jit(solution)/shard_map/pallas_call | solution.py:78
  234.2 9.9 %all-to-all-start.2 = ((f32[128,16,128]{2,1,0:T(8,128)}), f32[128,16,128]{2,1,0:T(8,128)S(1)}, u32[]{:S(2)}, u32[]{:S(2)}) async-start(f32[128,16,128]{2,1,0:T(8,128)} %bitcast.105), calls=%async_computation.2 | async-start | bytes 2097152 | tf_op jit(solution)/shard_map/all_to_all | solution.py:108
  244.1 19.1 %all-to-all-done.2 = f32[128,16,128]{2,1,0:T(8,128)S(1)} async-done(((f32[128,16,128]{2,1,0:T(8,128)}), f32[128,16,128]{2,1,0:T(8,128)S(1)}, u32[]{:S(2)}, u32[]{:S(2)}) %all-to-all-start.2) | async-done | bytes 1048608 | tf_op jit(solution)/shard_map/all_to_all | solution.py:108
  264.7 12.1 %shard_map.62 = f32[8192,32]{1,0:T(8,128)} custom-call(s32[8192]{0:T(1024)S(1)} %get-tuple-element.10.src_ref, f32[4096,32]{1,0:T(8,128)S(1)} %bitcast.99, f32[4096,32]{1,0:T(8,128)S(1)} %bitcast.97, f32[2048,128]{1,0:T(8,128)S(1)} %bitcast.104), custom_call_target="tpu_custom_call" | custom-call | tf_op jit(solution)/shard_map/pallas_call | solution.py:92
  276.9 10.1 %fusion.42 = f32[32,32]{1,0:T(8,128)S(1)} fusion(f32[8192,32]{1,0:T(8,128)} %shard_map.62), kind=kOutput, calls=%fused_computation.71 | convolution fusion | flops 100663296 | bytes 1052672 | tf_op jit(solution)/shard_map/dot_general | solution.py:175
  287.0 2.8 gather_fusion
  289.9 22.3 %all-gather = f32[1024,64]{1,0:T(8,128)S(1)} all-gather(f32[32,64]{1,0:T(8,128)S(1)} %pad_maximum_fusion), channel_id=2, replica_groups=mesh['iface'=4,'sub'=32] {'sub'}, dimensions={0}, use_global_device_ids=true | all-gather | bytes 270336 | tf_op jit(solution)/shard_map/all_gather | solution.py:190
  312.2 12.1 %all-gather.1 = f32[128,64]{1,0:T(8,128)S(1)} all-gather(f32[32,64]{1,0:T(8,128)S(1)} %reduce_sum.18), channel_id=3, replica_groups=mesh['iface'=4,'sub'=32] {'iface'}, dimensions={0}, use_global_device_ids=true | all-gather | bytes 40960 | tf_op jit(solution)/shard_map/all_gather | solution.py:191
  324.5 2.9 cholesky.44
  328.7 2.4 custom-call.8
  331.9 2.9 cholesky.55
  336.2 2.4 custom-call.9
  339.0 6.0 %convolution_bitcast_fusion = f32[4,8,64,128]{3,1,2,0:T(8,128)S(1)} fusion(f32[32,32]{1,0:T(8,128)S(1)} %convolution_multiply_fusion, f32[8192,32]{1,0:T(8,128)} %shard_map.62), kind=kOutput, calls=%fused_computation.9 | convolution fusion | flops 100663296 | bytes 2101248 | tf_op jit(solution)/shard_map/dot_general | solution.py:196
  (63 shorter events, 20.9 us)
Async XLA Ops:
  6.5 3.6 %copy-start.8 = (s32[64,128]{1,0:T(8,128)S(1)}, s32[64,128]{1,0:T(8,128)}, u32[]{:S(2)}) copy-start(s32[64,128]{1,0:T(8,128)} %param.10) | copy-start | bytes 98308
  6.5 3.6 %copy-start.7 = (s32[64,128]{1,0:T(8,128)S(1)}, s32[64,128]{1,0:T(8,128)}, u32[]{:S(2)}) copy-start(s32[64,128]{1,0:T(8,128)} %param.11) | copy-start | bytes 98308
  6.5 76.0 %all-gather.9.cloned.1.call-start = ((), (), s32[]{:S(2)}) async-start(), calls=%async_computation.4 | async-start | bytes 1310720 | tf_op jit(solution)/shard_map/all_gather | solution.py:115
  10.2 2.2 copy-start
  61.3 49.2 %all-gather.7.cloned.1.call-start = ((), (), s32[]{:S(2)}) async-start(), calls=%async_computation.3 | async-start | bytes 1310720 | tf_op jit(solution)/shard_map/all_gather | solution.py:115
  70.0 117.9 %all-gather.13.cloned.1.call-start = ((), (), s32[]{:S(2)}) async-start(), calls=%async_computation.6 | async-start | bytes 1310720 | tf_op jit(solution)/shard_map/all_gather | solution.py:115
  87.2 29.3 %copy-start.1 = (f32[32,128,32]{2,1,0:T(8,128)}, f32[32,128,32]{2,1,0:T(8,128)S(1)}, u32[]{:S(2)}) copy-start(f32[32,128,32]{2,1,0:T(8,128)S(1)} %copy.23) | copy-start | bytes 1572868
  116.5 1.6 copy-start.2
  163.4 3.4 copy-start.3
  166.8 49.1 %all-gather.11.cloned.1.call-start = ((), (), s32[]{:S(2)}) async-start(), calls=%async_computation.5 | async-start | bytes 1310720 | tf_op jit(solution)/shard_map/all_gather | solution.py:115
  221.8 22.2 %copy-start.9 = (s32[32]{0:T(128)S(1)}, s32[32]{0:T(128)}, u32[]{:S(2)}) copy-start(s32[32]{0:T(128)} %param.12) | copy-start | bytes 388
  221.8 1.6 copy-start.4
  233.2 1.0 copy-start.6
  234.2 29.0 %all-to-all-start.2 = ((f32[128,16,128]{2,1,0:T(8,128)}), f32[128,16,128]{2,1,0:T(8,128)S(1)}, u32[]{:S(2)}, u32[]{:S(2)}) async-start(f32[128,16,128]{2,1,0:T(8,128)} %bitcast.105), calls=%async_computation.2 | async-start | bytes 2097152 | tf_op jit(solution)/shard_map/all_to_all | solution.py:108
  263.1 1.6 copy-start.5
Sparse Core Ops, SparseCore 0:
  61.5 21.0 all-gather.8
  84.2 26.2 all-gather.6
  166.9 21.0 all-gather.12
  189.5 26.2 all-gather.10

commit v2 on v1

--- a/solution.py
+++ b/solution.py
@@ -9,7 +9,6 @@
 from jax.sharding import PartitionSpec as P
 
 UNROLL = 32
-PIECES = 2
 
 
 def _pack_kernel(slot_ref, *refs):
@@ -110,26 +109,20 @@
 
 def apply_blocks(jump_rows, schur_blocks, sub_local, group):
     width = jump_rows.shape[1]
-    count = jump_rows.shape[0] // group
-    half = jump_rows.astype(jnp.bfloat16).reshape(count, group, width).transpose(2, 0, 1)
-    gathered = lax.all_gather(half, "iface", axis=2, tiled=True)
-    result = jnp.einsum("src,ksc->srk", schur_blocks, gathered, preferred_element_type=jnp.float32)
-    return result.reshape(count * group, width)
-
-
-def jump_and_apply(parts, routing, schur_blocks, sub_local, group, pieces):
-    send_pos, source = routing
-    incoming = exchange(parts, send_pos)
-    rows = sum(part.shape[0] for part in parts)
-    step = rows // pieces
-    sub_step = sub_local // pieces
-    out = []
-    for h in range(pieces):
-        jumped = unpack_jump(parts, incoming, source, h * step, step)
-        out.append(
-            apply_blocks(jumped, schur_blocks[h * sub_step:(h + 1) * sub_step], sub_step, group)
-        )
-    return out
+    half = jump_rows.astype(jnp.bfloat16).reshape(sub_local, group, width).transpose(2, 0, 1)
+    ring = lax.axis_size("iface")
+    here = lax.axis_index("iface")
+    total = None
+    for shift in range(ring):
+        if shift:
+            block = lax.ppermute(half, "iface", [(i, (i + shift) % ring) for i in range(ring)])
+        else:
+            block = half
+        owner = (here - shift) % ring
+        columns = lax.dynamic_slice_in_dim(schur_blocks, owner * group, group, axis=2)
+        part = jnp.einsum("src,ksc->srk", columns, block, preferred_element_type=jnp.float32)
+        total = part if total is None else total + part
+    return total.reshape(sub_local * group, width)
 
 
 def combine_weights(gram_matrix, picked, total_rows, sample_count):
@@ -168,10 +161,13 @@
     ).astype(jnp.int32)
     routing = (send_pos, source)
     noise_rows = noise_field.transpose(1, 2, 0).reshape(row_count, sample_count)
-    response_one = jump_and_apply([noise_rows], routing, schur_blocks, sub_local, group, PIECES)
-    response_two = jump_and_apply(response_one, routing, schur_blocks, sub_local, group, PIECES)
-    incoming = exchange(response_two, send_pos)
-    samples = unpack_jump(response_two, incoming, source, 0, row_count)
+    field = [noise_rows]
+    for _ in range(2):
+        incoming = exchange(field, send_pos)
+        jumped = unpack_jump(field, incoming, source, 0, row_count)
+        field = [apply_blocks(jumped, schur_blocks, sub_local, group)]
+    incoming = exchange(field, send_pos)
+    samples = unpack_jump(field, incoming, source, 0, row_count)
     gram_part = lax.dot_general(
         samples,
         samples,

time: 353 us -> 293 us (0.83)
  waiting for transfers between devices: 91.4 us -> 50.1 us
  between operations: 13.4 us -> 0.21 us
  Pallas kernels: 70 us -> 65.1 us
    all_gather x4 -> x0, waiting for transfers between devices: 72.3 us -> none  [apply_blocks(): gathered = lax.all_gather(half, 'iface', axis=2, tiled=True)]
    ppermute x0 -> x6, waiting for transfers between devices: none -> 31.1 us  [apply_blocks(): lax.ppermute(half, 'iface', [(i, (i + shift) % ring) for i in range(ring)])]
    ppermute x0 -> x6, starting transfers between devices: none -> 6.67 us  [apply_blocks(): lax.ppermute(half, 'iface', [(i, (i + shift) % ring) for i in range(ring)])]
    dot_general x4 -> x8, matrix products: 16 us -> 22.3 us  [apply_blocks(): jnp.einsum('src,ksc->srk', columns, block, preferred_element_type=jnp.flo...]
    pallas_call x5 -> x3, Pallas kernels: 40.6 us -> 34.4 us  [unpack_jump(): pl.pallas_call(functools.partial(_unpack_kernel, first, count), in_specs=...]
    add x0 -> x2, local copies, waits for them, and re-layouts: none -> 5.27 us  [apply_blocks(): total = part if total is None else total + part]
    dot_general x4 -> x0, local copies, waits for them, and re-layouts: 5.13 us -> none  [apply_blocks(): jnp.einsum('src,ksc->srk', schur_blocks, gathered, preferred_element_type...]
    reshape x4 -> x2, local copies, waits for them, and re-layouts: 5.37 us -> 1.73 us  [apply_blocks(): jump_rows.astype(jnp.bfloat16).reshape(sub_local, group, width)]
  transfers between devices with their start and end apart: 5 -> 7, of which waited for: 5 -> 5; matrix products, arithmetic and copies ran while one was open for 3% -> 6% of each run, Pallas kernels for 4% -> 0%
where the time goes in v2:
time: 293 us; the launch traced here: 292 us
  blocking collectives  90.1 us (31%)
  Pallas kernels  65.1 us (22%)
  waiting for transfers between devices  50.1 us (17%)
  matrix products  36 us (12%)
  local copies, waits for them, and re-layouts  23.2 us (8%)
  other arithmetic  14 us (5%)
  starting transfers between devices  13.1 us (4%)
    all_to_all x2, blocking collectives, exchange(): lax.all_to_all(outgoing, ('iface', 'sub'), split_axis=0, concat_axis=0, t...  55.7 us
    pallas_call x3, Pallas kernels, unpack_jump(): pl.pallas_call(functools.partial(_unpack_kernel, first, count), in_specs=...  34.4 us
    ppermute x6, waiting for transfers between devices, apply_blocks(): lax.ppermute(half, 'iface', [(i, (i + shift) % ring) for i in range(ring)])  31.1 us
    pallas_call x3, Pallas kernels, pack_rows(): pl.pallas_call(_pack_kernel, in_specs=[pl.BlockSpec(memory_space=pltpu.SM...  30.7 us
    dot_general x8, matrix products, apply_blocks(): jnp.einsum('src,ksc->srk', columns, block, preferred_element_type=jnp.flo...  22.3 us
    all_gather x1, blocking collectives, shards(): lax.all_gather(partial, 'sub', axis=0, tiled=True)  22.3 us
    all_to_all x1, waiting for transfers between devices, exchange(): lax.all_to_all(outgoing, ('iface', 'sub'), split_axis=0, concat_axis=0, t...  19.1 us
    all_gather x1, blocking collectives, shards(): lax.all_gather(over_sub, 'iface', axis=0, tiled=True)  12.1 us
  transfers between devices with their start and end apart: 7, of which 5 were waited for; matrix products, arithmetic and copies ran while one was open for 6% of the time, Pallas kernels for 0%

profile of v2, /device:TPU:0, one launch (start us, length us, event | category | flops | bytes accessed | tf_op | source)
XLA Modules:
  0.0 291.9 jit_solution(4630035983200042910)
XLA Ops:
  0.0 3.6 %copy.15 = f32[64,128,32]{2,1,0:T(8,128)} copy(f32[64,128,32]{1,0,2:T(8,128)} %bitcast.99) | data formatting | bytes 2097152 | tf_op jit(solution)/shard_map/transpose | solution.py:163
  5.8 9.9 %shard_map.55 = f32[2048,128]{1,0:T(8,128)S(1)} custom-call(s32[8192]{0:T(1024)S(1)} %get-tuple-element.9.slot_ref, f32[8192,32]{1,0:T(8,128)S(1)} %bitcast.82), custom_call_target="tpu_custom_call" | custom-call | tf_op jit(solution)/shard_map/pallas_call | solution.py:77
  15.8 30.3 %all_to_all.33 = f32[128,16,128]{2,1,0:T(8,128)S(1)} all-to-all(f32[128,16,128]{2,1,0:T(8,128)S(1)} %bitcast.88), channel_id=1, replica_groups=mesh['iface'=4,'sub'=32] {'iface','sub'}, dimensions={0} | all-to-all | bytes 2097152 | tf_op jit(solution)/shard_map/all_to_all | solution.py:107
  46.1 11.5 %shard_map.56 = f32[8192,32]{1,0:T(8,128)S(1)} custom-call(s32[8192]{0:T(1024)S(1)} %get-tuple-element.10.src_ref, f32[8192,32]{1,0:T(8,128)} %bitcast.81, f32[2048,128]{1,0:T(8,128)S(1)} %bitcast.86), custom_call_target="tpu_custom_call" | custom-call | tf_op jit(solution)/shard_map/pallas_call | solution.py:91
  62.0 2.8 fusion.14
  64.8 10.3 %collective-permute-done.1 = bf16[32,64,128]{2,0,1:T(8,128)(2,1)S(1)} collective-permute-done((bf16[32,64,128]{2,0,1:T(8,128)(2,1)S(1)}, bf16[32,64,128]{2,0,1:T(8,128)(2,1)S(1)}, u32[]{:S(2)}, u32[]{:S(2)}) %collective-permute-start.1) | collective-permute-done | bytes 524320 | tf_op jit(solution)/shard_map/ppermute | solution.py:118
  75.1 2.8 fusion.6
  77.9 5.2 %collective-permute-done.2 = bf16[32,64,128]{2,0,1:T(8,128)(2,1)S(1)} collective-permute-done((bf16[32,64,128]{2,0,1:T(8,128)(2,1)S(1)}, bf16[32,64,128]{2,0,1:T(8,128)(2,1)S(1)}, u32[]{:S(2)}, u32[]{:S(2)}) %collective-permute-start.2) | collective-permute-done | bytes 524320 | tf_op jit(solution)/shard_map/ppermute | solution.py:118
  83.1 2.8 fusion.2
  85.9 2.8 fusion.31
  88.7 2.6 copy.17
  93.5 9.9 %shard_map.57 = f32[2048,128]{1,0:T(8,128)S(1)} custom-call(s32[8192]{0:T(1024)S(1)} %get-tuple-element.9.slot_ref, f32[8192,32]{1,0:T(8,128)S(1)} %bitcast.84), custom_call_target="tpu_custom_call" | custom-call | tf_op jit(solution)/shard_map/pallas_call | solution.py:77
  103.4 25.4 %all_to_all.34 = f32[128,16,128]{2,1,0:T(8,128)S(1)} all-to-all(f32[128,16,128]{2,1,0:T(8,128)S(1)} %bitcast.89), channel_id=1, replica_groups=mesh['iface'=4,'sub'=32] {'iface','sub'}, dimensions={0} | all-to-all | bytes 2097152 | tf_op jit(solution)/shard_map/all_to_all | solution.py:107
  128.8 11.5 %shard_map.58 = f32[8192,32]{1,0:T(8,128)S(1)} custom-call(s32[8192]{0:T(1024)S(1)} %get-tuple-element.10.src_ref, f32[8192,32]{1,0:T(8,128)} %bitcast.83, f32[2048,128]{1,0:T(8,128)S(1)} %bitcast.87), custom_call_target="tpu_custom_call" | custom-call | tf_op jit(solution)/shard_map/pallas_call | solution.py:91
  144.7 2.8 fusion.12
  147.5 10.3 %collective-permute-done.4 = bf16[32,64,128]{2,0,1:T(8,128)(2,1)S(1)} collective-permute-done((bf16[32,64,128]{2,0,1:T(8,128)(2,1)S(1)}, bf16[32,64,128]{2,0,1:T(8,128)(2,1)S(1)}, u32[]{:S(2)}, u32[]{:S(2)}) %collective-permute-start.4) | collective-permute-done | bytes 524320 | tf_op jit(solution)/shard_map/ppermute | solution.py:118
  157.8 2.8 fusion.4
  160.6 5.2 %collective-permute-done.5 = bf16[32,64,128]{2,0,1:T(8,128)(2,1)S(1)} collective-permute-done((bf16[32,64,128]{2,0,1:T(8,128)(2,1)S(1)}, bf16[32,64,128]{2,0,1:T(8,128)(2,1)S(1)}, u32[]{:S(2)}, u32[]{:S(2)}) %collective-permute-start.5) | collective-permute-done | bytes 524320 | tf_op jit(solution)/shard_map/ppermute | solution.py:118
  165.8 2.8 fusion
  168.6 2.8 fusion.28
  171.4 2.6 copy.19
  176.2 10.9 %shard_map.59 = f32[2048,128]{1,0:T(8,128)} custom-call(s32[8192]{0:T(1024)S(1)} %get-tuple-element.9.slot_ref, f32[8192,32]{1,0:T(8,128)S(1)} %bitcast.80), custom_call_target="tpu_custom_call" | custom-call | tf_op jit(solution)/shard_map/pallas_call | solution.py:77
  187.1 6.4 %all-to-all-start.2 = ((f32[128,16,128]{2,1,0:T(8,128)}), f32[128,16,128]{2,1,0:T(8,128)S(1)}, u32[]{:S(2)}, u32[]{:S(2)}) async-start(f32[128,16,128]{2,1,0:T(8,128)} %bitcast.15), calls=%async_computation.2 | async-start | bytes 2097152 | tf_op jit(solution)/shard_map/all_to_all | solution.py:107
  193.6 19.1 %all-to-all-done.2 = f32[128,16,128]{2,1,0:T(8,128)S(1)} async-done(((f32[128,16,128]{2,1,0:T(8,128)}), f32[128,16,128]{2,1,0:T(8,128)S(1)}, u32[]{:S(2)}, u32[]{:S(2)}) %all-to-all-start.2) | async-done | bytes 1048608 | tf_op jit(solution)/shard_map/all_to_all | solution.py:107
  212.7 11.5 %shard_map.60 = f32[8192,32]{1,0:T(8,128)S(1)} custom-call(s32[8192]{0:T(1024)S(1)} %get-tuple-element.10.src_ref, f32[8192,32]{1,0:T(8,128)} %bitcast.79, f32[2048,128]{1,0:T(8,128)S(1)} %bitcast.85), custom_call_target="tpu_custom_call" | custom-call | tf_op jit(solution)/shard_map/pallas_call | solution.py:91
  226.1 6.7 %fusion.66 = f32[32,32]{1,0:T(8,128)S(1)} fusion(f32[8192,32]{1,0:T(8,128)S(1)} %shard_map.60), kind=kOutput, calls=%fused_computation.91 | convolution fusion | flops 100663296 | bytes 1052672 | tf_op jit(solution)/shard_map/dot_general | solution.py:171
  232.8 2.8 gather_fusion
  235.7 22.3 %all-gather = f32[1024,64]{1,0:T(8,128)S(1)} all-gather(f32[32,64]{1,0:T(8,128)S(1)} %pad_maximum_fusion), channel_id=2, replica_groups=mesh['iface'=4,'sub'=32] {'sub'}, dimensions={0}, use_global_device_ids=true | all-gather | bytes 270336 | tf_op jit(solution)/shard_map/all_gather | solution.py:186
  258.0 12.1 %all-gather.1 = f32[128,64]{1,0:T(8,128)S(1)} all-gather(f32[32,64]{1,0:T(8,128)S(1)} %reduce_sum.18), channel_id=3, replica_groups=mesh['iface'=4,'sub'=32] {'iface'}, dimensions={0}, use_global_device_ids=true | all-gather | bytes 40960 | tf_op jit(solution)/shard_map/all_gather | solution.py:187
  270.3 2.9 %cholesky.44 = f32[32,32]{1,0:T(8,128)S(1)} custom-call(f32[32,32]{1,0:T(8,128)S(1)} %fusion.49), custom_call_target="Cholesky" | custom-call | tf_op jit(solution)/shard_map/jit(cholesky)/cholesky | solution.py:129
  277.7 2.9 %cholesky.55 = f32[32,32]{1,0:T(8,128)S(1)} custom-call(f32[32,32]{1,0:T(8,128)S(1)} %fusion.44), custom_call_target="Cholesky" | custom-call | tf_op jit(solution)/shard_map/jit(cholesky)/cholesky | solution.py:134
  284.8 6.0 %convolution_bitcast_fusion = f32[4,8,64,128]{3,1,2,0:T(8,128)S(1)} fusion(f32[32,32]{1,0:T(8,128)S(1)} %convolution_multiply_fusion, f32[8192,32]{1,0:T(8,128)} %copy-done), kind=kOutput, calls=%fused_computation.17 | convolution fusion | flops 100663296 | bytes 2101248 | tf_op jit(solution)/shard_map/dot_general | solution.py:192
  (53 shorter events, 27.5 us)
Async XLA Ops:
  0.0 3.6 %copy-start.5 = (s32[64,128]{1,0:T(8,128)S(1)}, s32[64,128]{1,0:T(8,128)}, u32[]{:S(2)}) copy-start(s32[64,128]{1,0:T(8,128)} %param.10) | copy-start | bytes 98308
  0.0 3.6 %copy-start.4 = (s32[64,128]{1,0:T(8,128)S(1)}, s32[64,128]{1,0:T(8,128)}, u32[]{:S(2)}) copy-start(s32[64,128]{1,0:T(8,128)} %param.11) | copy-start | bytes 98308
  3.6 2.2 copy-start.2
  58.7 16.4 %collective-permute-start.1 = (bf16[32,64,128]{2,0,1:T(8,128)(2,1)S(1)}, bf16[32,64,128]{2,0,1:T(8,128)(2,1)S(1)}, u32[]{:S(2)}, u32[]{:S(2)}) collective-permute-start(bf16[32,64,128]{2,0,1:T(8,128)(2,1)S(1)} %bitcast.92), channel_id=1, source_target_pairs={{0,64},{32,96},{64,0},{96,32},{1,65},{33,97},{65,1},{97,33},{2,66}... | collective-permute-start | bytes 1572872 | tf_op jit(solution)/shard_map/ppermute | solution.py:118
  59.4 23.7 %collective-permute-start.2 = (bf16[32,64,128]{2,0,1:T(8,128)(2,1)S(1)}, bf16[32,64,128]{2,0,1:T(8,128)(2,1)S(1)}, u32[]{:S(2)}, u32[]{:S(2)}) collective-permute-start(bf16[32,64,128]{2,0,1:T(8,128)(2,1)S(1)} %bitcast.93), channel_id=1, source_target_pairs={{0,96},{32,0},{64,32},{96,64},{1,97},{33,1},{65,33},{97,65},{2,98}... | collective-permute-start | bytes 1572872 | tf_op jit(solution)/shard_map/ppermute | solution.py:118
  62.0 23.9 %collective-permute-start = (bf16[32,64,128]{2,0,1:T(8,128)(2,1)S(1)}, bf16[32,64,128]{2,0,1:T(8,128)(2,1)S(1)}, u32[]{:S(2)}, u32[]{:S(2)}) collective-permute-start(bf16[32,64,128]{2,0,1:T(8,128)(2,1)S(1)} %bitcast.94), channel_id=1, source_target_pairs={{0,32},{32,64},{64,96},{96,0},{1,33},{33,65},{65,97},{97,1},{2,34}... | collective-permute-start | bytes 1572872 | tf_op jit(solution)/shard_map/ppermute | solution.py:118
  91.3 2.2 copy-start.3
  141.4 16.4 %collective-permute-start.4 = (bf16[32,64,128]{2,0,1:T(8,128)(2,1)S(1)}, bf16[32,64,128]{2,0,1:T(8,128)(2,1)S(1)}, u32[]{:S(2)}, u32[]{:S(2)}) collective-permute-start(bf16[32,64,128]{2,0,1:T(8,128)(2,1)S(1)} %bitcast.95), channel_id=1, source_target_pairs={{0,64},{32,96},{64,0},{96,32},{1,65},{33,97},{65,1},{97,33},{2,66}... | collective-permute-start | bytes 1572872 | tf_op jit(solution)/shard_map/ppermute | solution.py:118
  142.1 23.7 %collective-permute-start.5 = (bf16[32,64,128]{2,0,1:T(8,128)(2,1)S(1)}, bf16[32,64,128]{2,0,1:T(8,128)(2,1)S(1)}, u32[]{:S(2)}, u32[]{:S(2)}) collective-permute-start(bf16[32,64,128]{2,0,1:T(8,128)(2,1)S(1)} %bitcast.96), channel_id=1, source_target_pairs={{0,96},{32,0},{64,32},{96,64},{1,97},{33,1},{65,33},{97,65},{2,98}... | collective-permute-start | bytes 1572872 | tf_op jit(solution)/shard_map/ppermute | solution.py:118
  144.7 23.9 %collective-permute-start.3 = (bf16[32,64,128]{2,0,1:T(8,128)(2,1)S(1)}, bf16[32,64,128]{2,0,1:T(8,128)(2,1)S(1)}, u32[]{:S(2)}, u32[]{:S(2)}) collective-permute-start(bf16[32,64,128]{2,0,1:T(8,128)(2,1)S(1)} %bitcast.97), channel_id=1, source_target_pairs={{0,32},{32,64},{64,96},{96,0},{1,33},{33,65},{65,97},{97,1},{2,34}... | collective-permute-start | bytes 1572872 | tf_op jit(solution)/shard_map/ppermute | solution.py:118
  174.0 19.5 %copy-start.6 = (s32[32]{0:T(128)S(1)}, s32[32]{0:T(128)}, u32[]{:S(2)}) copy-start(s32[32]{0:T(128)} %param.12) | copy-start | bytes 388
  174.0 2.2 copy-start.1
  187.1 25.6 %all-to-all-start.2 = ((f32[128,16,128]{2,1,0:T(8,128)}), f32[128,16,128]{2,1,0:T(8,128)S(1)}, u32[]{:S(2)}, u32[]{:S(2)}) async-start(f32[128,16,128]{2,1,0:T(8,128)} %bitcast.15), calls=%async_computation.2 | async-start | bytes 2097152 | tf_op jit(solution)/shard_map/all_to_all | solution.py:107
  224.2 1.9 copy-start

commit v3 on v2

--- a/solution.py
+++ b/solution.py
@@ -8,7 +8,7 @@
 from jax.experimental.pallas import tpu as pltpu
 from jax.sharding import PartitionSpec as P
 
-UNROLL = 32
+UNROLL = 64
 
 
 def _pack_kernel(slot_ref, *refs):
@@ -183,8 +183,16 @@
         jnp.float32
     )
     partial = jnp.concatenate((gram_part, picked_part), axis=1)[None]
-    over_sub = jnp.sum(lax.all_gather(partial, "sub", axis=0, tiled=True), axis=0, keepdims=True)
-    total = jnp.sum(lax.all_gather(over_sub, "iface", axis=0, tiled=True), axis=0)
+    over_sub = jnp.sum(lax.all_gather(partial, "sub", axis=0, tiled=True), axis=0)
+    arrived = [over_sub] + [
+        lax.ppermute(over_sub, "iface", [(i, (i + shift) % iface_count) for i in range(iface_count)])
+        for shift in range(1, iface_count)
+    ]
+    stacked = jnp.stack(arrived)
+    total = None
+    for owner in range(iface_count):
+        term = stacked[(iface_place - owner) % iface_count]
+        total = term if total is None else total + term
     gram_matrix = total[:, :sample_count]
     picked = total[:, sample_count:]
     total_rows = float(sub_local * sub_count * full_width)

time: 293 us -> 284 us (0.969)
  blocking collectives: 90.1 us -> 78 us
  starting transfers between devices: 13.1 us -> 16.9 us
  Pallas kernels: 65.1 us -> 61.7 us
    all_gather x1 -> x0, blocking collectives: 12.1 us -> none  [shards(): lax.all_gather(over_sub, 'iface', axis=0, tiled=True)]
    ppermute x0 -> x3, starting transfers between devices: none -> 3.78 us  [shards(): lax.ppermute(over_sub, 'iface', [(i, (i + shift) % iface_count) for i in...]
    unnamed x16 -> x15, local copies, waits for them, and re-layouts: 9.73 us -> 9.66 us
  transfers between devices with their start and end apart: 7 -> 10, of which waited for: 5 -> 8; matrix products, arithmetic and copies ran while one was open for 6% -> 6% of each run, Pallas kernels for 0% -> 0%
where the time goes in v3:
time: 284 us; the launch traced here: 283 us
  blocking collectives  78 us (27%)
  Pallas kernels  61.7 us (22%)
  waiting for transfers between devices  53 us (19%)
  matrix products  36 us (13%)
  local copies, waits for them, and re-layouts  23.4 us (8%)
  starting transfers between devices  16.9 us (6%)
  other arithmetic  14 us (5%)
    all_to_all x2, blocking collectives, exchange(): lax.all_to_all(outgoing, ('iface', 'sub'), split_axis=0, concat_axis=0, t...  55.7 us
    pallas_call x3, Pallas kernels, unpack_jump(): pl.pallas_call(functools.partial(_unpack_kernel, first, count), in_specs=...  32.8 us
    ppermute x6, waiting for transfers between devices, apply_blocks(): lax.ppermute(half, 'iface', [(i, (i + shift) % ring) for i in range(ring)])  31.1 us
    pallas_call x3, Pallas kernels, pack_rows(): pl.pallas_call(_pack_kernel, in_specs=[pl.BlockSpec(memory_space=pltpu.SM...  28.9 us
    dot_general x8, matrix products, apply_blocks(): jnp.einsum('src,ksc->srk', columns, block, preferred_element_type=jnp.flo...  22.3 us
    all_gather x1, blocking collectives, shards(): lax.all_gather(partial, 'sub', axis=0, tiled=True)  22.3 us
    all_to_all x1, waiting for transfers between devices, exchange(): lax.all_to_all(outgoing, ('iface', 'sub'), split_axis=0, concat_axis=0, t...  19.1 us
    unnamed x15, local copies, waits for them, and re-layouts  9.66 us
  transfers between devices with their start and end apart: 10, of which 8 were waited for; matrix products, arithmetic and copies ran while one was open for 6% of the time, Pallas kernels for 0%

profile of v3, /device:TPU:0, one launch (start us, length us, event | category | flops | bytes accessed | tf_op | source)
XLA Modules:
  0.0 283.1 jit_solution(14262675612559910375)
XLA Ops:
  0.0 3.6 %copy.15 = f32[64,128,32]{2,1,0:T(8,128)} copy(f32[64,128,32]{1,0,2:T(8,128)} %bitcast.103) | data formatting | bytes 2097152 | tf_op jit(solution)/shard_map/transpose | solution.py:163
  5.8 9.3 %shard_map.55 = f32[2048,128]{1,0:T(8,128)S(1)} custom-call(s32[8192]{0:T(1024)S(1)} %get-tuple-element.9.slot_ref, f32[8192,32]{1,0:T(8,128)S(1)} %bitcast.86), custom_call_target="tpu_custom_call" | custom-call | tf_op jit(solution)/shard_map/pallas_call | solution.py:77
  15.2 30.3 %all_to_all.33 = f32[128,16,128]{2,1,0:T(8,128)S(1)} all-to-all(f32[128,16,128]{2,1,0:T(8,128)S(1)} %bitcast.92), channel_id=1, replica_groups=mesh['iface'=4,'sub'=32] {'iface','sub'}, dimensions={0} | all-to-all | bytes 2097152 | tf_op jit(solution)/shard_map/all_to_all | solution.py:107
  45.5 10.9 %shard_map.56 = f32[8192,32]{1,0:T(8,128)S(1)} custom-call(s32[8192]{0:T(1024)S(1)} %get-tuple-element.10.src_ref, f32[8192,32]{1,0:T(8,128)} %bitcast.85, f32[2048,128]{1,0:T(8,128)S(1)} %bitcast.90), custom_call_target="tpu_custom_call" | custom-call | tf_op jit(solution)/shard_map/pallas_call | solution.py:91
  58.2 2.6 collective-permute-start.2
  60.9 2.8 fusion.14
  63.6 10.3 %collective-permute-done.1 = bf16[32,64,128]{2,0,1:T(8,128)(2,1)S(1)} collective-permute-done((bf16[32,64,128]{2,0,1:T(8,128)(2,1)S(1)}, bf16[32,64,128]{2,0,1:T(8,128)(2,1)S(1)}, u32[]{:S(2)}, u32[]{:S(2)}) %collective-permute-start.1) | collective-permute-done | bytes 524320 | tf_op jit(solution)/shard_map/ppermute | solution.py:118
  73.9 2.8 fusion.6
  76.7 5.2 %collective-permute-done.2 = bf16[32,64,128]{2,0,1:T(8,128)(2,1)S(1)} collective-permute-done((bf16[32,64,128]{2,0,1:T(8,128)(2,1)S(1)}, bf16[32,64,128]{2,0,1:T(8,128)(2,1)S(1)}, u32[]{:S(2)}, u32[]{:S(2)}) %collective-permute-start.2) | collective-permute-done | bytes 524320 | tf_op jit(solution)/shard_map/ppermute | solution.py:118
  81.9 2.8 fusion.2
  84.7 2.8 fusion.31
  87.5 2.6 copy.17
  92.4 9.3 %shard_map.57 = f32[2048,128]{1,0:T(8,128)S(1)} custom-call(s32[8192]{0:T(1024)S(1)} %get-tuple-element.9.slot_ref, f32[8192,32]{1,0:T(8,128)S(1)} %bitcast.88), custom_call_target="tpu_custom_call" | custom-call | tf_op jit(solution)/shard_map/pallas_call | solution.py:77
  101.7 25.4 %all_to_all.34 = f32[128,16,128]{2,1,0:T(8,128)S(1)} all-to-all(f32[128,16,128]{2,1,0:T(8,128)S(1)} %bitcast.93), channel_id=1, replica_groups=mesh['iface'=4,'sub'=32] {'iface','sub'}, dimensions={0} | all-to-all | bytes 2097152 | tf_op jit(solution)/shard_map/all_to_all | solution.py:107
  127.1 10.9 %shard_map.58 = f32[8192,32]{1,0:T(8,128)S(1)} custom-call(s32[8192]{0:T(1024)S(1)} %get-tuple-element.10.src_ref, f32[8192,32]{1,0:T(8,128)} %bitcast.87, f32[2048,128]{1,0:T(8,128)S(1)} %bitcast.91), custom_call_target="tpu_custom_call" | custom-call | tf_op jit(solution)/shard_map/pallas_call | solution.py:91
  142.4 2.8 fusion.12
  145.2 10.3 %collective-permute-done.4 = bf16[32,64,128]{2,0,1:T(8,128)(2,1)S(1)} collective-permute-done((bf16[32,64,128]{2,0,1:T(8,128)(2,1)S(1)}, bf16[32,64,128]{2,0,1:T(8,128)(2,1)S(1)}, u32[]{:S(2)}, u32[]{:S(2)}) %collective-permute-start.4) | collective-permute-done | bytes 524320 | tf_op jit(solution)/shard_map/ppermute | solution.py:118
  155.5 2.8 fusion.4
  158.3 5.2 %collective-permute-done.5 = bf16[32,64,128]{2,0,1:T(8,128)(2,1)S(1)} collective-permute-done((bf16[32,64,128]{2,0,1:T(8,128)(2,1)S(1)}, bf16[32,64,128]{2,0,1:T(8,128)(2,1)S(1)}, u32[]{:S(2)}, u32[]{:S(2)}) %collective-permute-start.5) | collective-permute-done | bytes 524320 | tf_op jit(solution)/shard_map/ppermute | solution.py:118
  163.5 2.8 fusion
  166.3 2.8 fusion.28
  169.1 2.6 copy.19
  174.0 10.3 %shard_map.59 = f32[2048,128]{1,0:T(8,128)} custom-call(s32[8192]{0:T(1024)S(1)} %get-tuple-element.9.slot_ref, f32[8192,32]{1,0:T(8,128)S(1)} %bitcast.84), custom_call_target="tpu_custom_call" | custom-call | tf_op jit(solution)/shard_map/pallas_call | solution.py:77
  184.2 6.4 %all-to-all-start.2 = ((f32[128,16,128]{2,1,0:T(8,128)}), f32[128,16,128]{2,1,0:T(8,128)S(1)}, u32[]{:S(2)}, u32[]{:S(2)}) async-start(f32[128,16,128]{2,1,0:T(8,128)} %bitcast.15), calls=%async_computation.2 | async-start | bytes 2097152 | tf_op jit(solution)/shard_map/all_to_all | solution.py:107
  190.7 19.1 %all-to-all-done.2 = f32[128,16,128]{2,1,0:T(8,128)S(1)} async-done(((f32[128,16,128]{2,1,0:T(8,128)}), f32[128,16,128]{2,1,0:T(8,128)S(1)}, u32[]{:S(2)}, u32[]{:S(2)}) %all-to-all-start.2) | async-done | bytes 1048608 | tf_op jit(solution)/shard_map/all_to_all | solution.py:107
  209.8 10.9 %shard_map.60 = f32[8192,32]{1,0:T(8,128)S(1)} custom-call(s32[8192]{0:T(1024)S(1)} %get-tuple-element.10.src_ref, f32[8192,32]{1,0:T(8,128)} %bitcast.83, f32[2048,128]{1,0:T(8,128)S(1)} %bitcast.89), custom_call_target="tpu_custom_call" | custom-call | tf_op jit(solution)/shard_map/pallas_call | solution.py:91
  222.7 6.7 %fusion.66 = f32[32,32]{1,0:T(8,128)S(1)} fusion(f32[8192,32]{1,0:T(8,128)S(1)} %shard_map.60), kind=kOutput, calls=%fused_computation.93 | convolution fusion | flops 100663296 | bytes 1052672 | tf_op jit(solution)/shard_map/dot_general | solution.py:171
  229.4 2.8 gather_fusion
  232.3 22.3 %all-gather = f32[1024,64]{1,0:T(8,128)S(1)} all-gather(f32[32,64]{1,0:T(8,128)S(1)} %pad_maximum_fusion.1), channel_id=2, replica_groups=mesh['iface'=4,'sub'=32] {'sub'}, dimensions={0}, use_global_device_ids=true | all-gather | bytes 270336 | tf_op jit(solution)/shard_map/all_gather | solution.py:186
  261.5 2.9 %cholesky.44 = f32[32,32]{1,0:T(8,128)S(1)} custom-call(f32[32,32]{1,0:T(8,128)S(1)} %fusion.49), custom_call_target="Cholesky" | custom-call | tf_op jit(solution)/shard_map/jit(cholesky)/cholesky | solution.py:129
  268.9 2.9 %cholesky.55 = f32[32,32]{1,0:T(8,128)S(1)} custom-call(f32[32,32]{1,0:T(8,128)S(1)} %fusion.44), custom_call_target="Cholesky" | custom-call | tf_op jit(solution)/shard_map/jit(cholesky)/cholesky | solution.py:134
  276.0 6.0 %convolution_bitcast_fusion = f32[4,8,64,128]{3,1,2,0:T(8,128)S(1)} fusion(f32[32,32]{1,0:T(8,128)S(1)} %convolution_multiply_fusion, f32[8192,32]{1,0:T(8,128)} %copy-done), kind=kOutput, calls=%fused_computation.17 | convolution fusion | flops 100663296 | bytes 2101248 | tf_op jit(solution)/shard_map/dot_general | solution.py:200
  (61 shorter events, 31.6 us)
Async XLA Ops:
  0.0 3.6 %copy-start.5 = (s32[64,128]{1,0:T(8,128)S(1)}, s32[64,128]{1,0:T(8,128)}, u32[]{:S(2)}) copy-start(s32[64,128]{1,0:T(8,128)} %param.10) | copy-start | bytes 98308
  0.0 3.6 %copy-start.4 = (s32[64,128]{1,0:T(8,128)S(1)}, s32[64,128]{1,0:T(8,128)}, u32[]{:S(2)}) copy-start(s32[64,128]{1,0:T(8,128)} %param.11) | copy-start | bytes 98308
  3.6 2.2 copy-start.2
  57.5 16.4 %collective-permute-start.1 = (bf16[32,64,128]{2,0,1:T(8,128)(2,1)S(1)}, bf16[32,64,128]{2,0,1:T(8,128)(2,1)S(1)}, u32[]{:S(2)}, u32[]{:S(2)}) collective-permute-start(bf16[32,64,128]{2,0,1:T(8,128)(2,1)S(1)} %bitcast.96), channel_id=1, source_target_pairs={{0,64},{32,96},{64,0},{96,32},{1,65},{33,97},{65,1},{97,33},{2,66}... | collective-permute-start | bytes 1572872 | tf_op jit(solution)/shard_map/ppermute | solution.py:118
  58.2 23.7 %collective-permute-start.2 = (bf16[32,64,128]{2,0,1:T(8,128)(2,1)S(1)}, bf16[32,64,128]{2,0,1:T(8,128)(2,1)S(1)}, u32[]{:S(2)}, u32[]{:S(2)}) collective-permute-start(bf16[32,64,128]{2,0,1:T(8,128)(2,1)S(1)} %bitcast.97), channel_id=1, source_target_pairs={{0,96},{32,0},{64,32},{96,64},{1,97},{33,1},{65,33},{97,65},{2,98}... | collective-permute-start | bytes 1572872 | tf_op jit(solution)/shard_map/ppermute | solution.py:118
  60.9 23.9 %collective-permute-start = (bf16[32,64,128]{2,0,1:T(8,128)(2,1)S(1)}, bf16[32,64,128]{2,0,1:T(8,128)(2,1)S(1)}, u32[]{:S(2)}, u32[]{:S(2)}) collective-permute-start(bf16[32,64,128]{2,0,1:T(8,128)(2,1)S(1)} %bitcast.98), channel_id=1, source_target_pairs={{0,32},{32,64},{64,96},{96,0},{1,33},{33,65},{65,97},{97,1},{2,34}... | collective-permute-start | bytes 1572872 | tf_op jit(solution)/shard_map/ppermute | solution.py:118
  90.2 2.2 copy-start.3
  139.1 16.4 %collective-permute-start.4 = (bf16[32,64,128]{2,0,1:T(8,128)(2,1)S(1)}, bf16[32,64,128]{2,0,1:T(8,128)(2,1)S(1)}, u32[]{:S(2)}, u32[]{:S(2)}) collective-permute-start(bf16[32,64,128]{2,0,1:T(8,128)(2,1)S(1)} %bitcast.99), channel_id=1, source_target_pairs={{0,64},{32,96},{64,0},{96,32},{1,65},{33,97},{65,1},{97,33},{2,66}... | collective-permute-start | bytes 1572872 | tf_op jit(solution)/shard_map/ppermute | solution.py:118
  139.8 23.7 %collective-permute-start.5 = (bf16[32,64,128]{2,0,1:T(8,128)(2,1)S(1)}, bf16[32,64,128]{2,0,1:T(8,128)(2,1)S(1)}, u32[]{:S(2)}, u32[]{:S(2)}) collective-permute-start(bf16[32,64,128]{2,0,1:T(8,128)(2,1)S(1)} %bitcast.100), channel_id=1, source_target_pairs={{0,96},{32,0},{64,32},{96,64},{1,97},{33,1},{65,33},{97,65},{2,98}... | collective-permute-start | bytes 1572872 | tf_op jit(solution)/shard_map/ppermute | solution.py:118
  142.4 23.9 %collective-permute-start.3 = (bf16[32,64,128]{2,0,1:T(8,128)(2,1)S(1)}, bf16[32,64,128]{2,0,1:T(8,128)(2,1)S(1)}, u32[]{:S(2)}, u32[]{:S(2)}) collective-permute-start(bf16[32,64,128]{2,0,1:T(8,128)(2,1)S(1)} %bitcast.101), channel_id=1, source_target_pairs={{0,32},{32,64},{64,96},{96,0},{1,33},{33,65},{65,97},{97,1},{2,34}... | collective-permute-start | bytes 1572872 | tf_op jit(solution)/shard_map/ppermute | solution.py:118
  171.8 18.9 %copy-start.6 = (s32[32]{0:T(128)S(1)}, s32[32]{0:T(128)}, u32[]{:S(2)}) copy-start(s32[32]{0:T(128)} %param.12) | copy-start | bytes 388
  171.8 2.2 copy-start.1
  184.2 25.6 %all-to-all-start.2 = ((f32[128,16,128]{2,1,0:T(8,128)}), f32[128,16,128]{2,1,0:T(8,128)S(1)}, u32[]{:S(2)}, u32[]{:S(2)}) async-start(f32[128,16,128]{2,1,0:T(8,128)} %bitcast.15), calls=%async_computation.2 | async-start | bytes 2097152 | tf_op jit(solution)/shard_map/all_to_all | solution.py:107
  220.8 1.9 copy-start
  254.7 5.5 %collective-permute-start.6 = (f32[32,64]{0,1:T(8,128)S(1)}, f32[32,64]{0,1:T(8,128)S(1)}, u32[]{:S(2)}, u32[]{:S(2)}) collective-permute-start(f32[32,64]{0,1:T(8,128)S(1)} %copy.21), channel_id=1, source_target_pairs={{0,32},{32,64},{64,96},{96,0},{1,33},{33,65},{65,97},{97,1},{2,34}... | collective-permute-start | bytes 24584 | tf_op jit(solution)/shard_map/ppermute | solution.py:188
  255.4 5.4 %collective-permute-start.7 = (f32[32,64]{0,1:T(8,128)S(1)}, f32[32,64]{0,1:T(8,128)S(1)}, u32[]{:S(2)}, u32[]{:S(2)}) collective-permute-start(f32[32,64]{0,1:T(8,128)S(1)} %copy.21), channel_id=1, source_target_pairs={{0,64},{32,96},{64,0},{96,32},{1,65},{33,97},{65,1},{97,33},{2,66}... | collective-permute-start | bytes 24584 | tf_op jit(solution)/shard_map/ppermute | solution.py:188
  257.5 3.9 %collective-permute-start.8 = (f32[32,64]{0,1:T(8,128)S(1)}, f32[32,64]{0,1:T(8,128)S(1)}, u32[]{:S(2)}, u32[]{:S(2)}) collective-permute-start(f32[32,64]{0,1:T(8,128)S(1)} %copy.21), channel_id=1, source_target_pairs={{0,96},{32,0},{64,32},{96,64},{1,97},{33,1},{65,33},{97,65},{2,98}... | collective-permute-start | bytes 24584 | tf_op jit(solution)/shard_map/ppermute | solution.py:188

commit v4 on v3

--- a/solution.py
+++ b/solution.py
@@ -183,7 +183,13 @@
         jnp.float32
     )
     partial = jnp.concatenate((gram_part, picked_part), axis=1)[None]
-    over_sub = jnp.sum(lax.all_gather(partial, "sub", axis=0, tiled=True), axis=0)
+    over_sub = partial[0]
+    span = 1
+    while span < sub_count:
+        over_sub = over_sub + lax.ppermute(
+            over_sub, "sub", [(i, i ^ span) for i in range(sub_count)]
+        )
+        span *= 2
     arrived = [over_sub] + [
         lax.ppermute(over_sub, "iface", [(i, (i + shift) % iface_count) for i in range(iface_count)])
         for shift in range(1, iface_count)

time: 284 us -> 281 us (0.989)
  blocking collectives: 78 us -> 55.7 us
  waiting for transfers between devices: 53 us -> 72.3 us
    all_gather x1 -> x0, blocking collectives: 22.3 us -> none  [shards(): lax.all_gather(partial, 'sub', axis=0, tiled=True)]
    ppermute x0 -> x5, waiting for transfers between devices: none -> 19 us  [shards(): lax.ppermute(over_sub, 'sub', [(i, i ^ span) for i in range(sub_count)])]
  transfers between devices with their start and end apart: 10 -> 15, of which waited for: 8 -> 13; matrix products, arithmetic and copies ran while one was open for 6% -> 6% of each run, Pallas kernels for 0% -> 0%
where the time goes in v4:
time: 281 us
  waiting for transfers between devices  72.3 us (26%)
  Pallas kernels  61.7 us (22%)
  blocking collectives  55.7 us (20%)
  matrix products  36 us (13%)
  local copies, waits for them, and re-layouts  23.3 us (8%)
  starting transfers between devices  17.5 us (6%)
  other arithmetic  14 us (5%)
    all_to_all x2, blocking collectives, exchange(): lax.all_to_all(outgoing, ('iface', 'sub'), split_axis=0, concat_axis=0, t...  55.7 us
    pallas_call x3, Pallas kernels, unpack_jump(): pl.pallas_call(functools.partial(_unpack_kernel, first, count), in_specs=...  32.8 us
    ppermute x6, waiting for transfers between devices, apply_blocks(): lax.ppermute(half, 'iface', [(i, (i + shift) % ring) for i in range(ring)])  31.1 us
    pallas_call x3, Pallas kernels, pack_rows(): pl.pallas_call(_pack_kernel, in_specs=[pl.BlockSpec(memory_space=pltpu.SM...  28.9 us
    dot_general x8, matrix products, apply_blocks(): jnp.einsum('src,ksc->srk', columns, block, preferred_element_type=jnp.flo...  22.3 us
    all_to_all x1, waiting for transfers between devices, exchange(): lax.all_to_all(outgoing, ('iface', 'sub'), split_axis=0, concat_axis=0, t...  19.1 us
    ppermute x5, waiting for transfers between devices, shards(): lax.ppermute(over_sub, 'sub', [(i, i ^ span) for i in range(sub_count)])  19 us
    unnamed x15, local copies, waits for them, and re-layouts  9.68 us
  transfers between devices with their start and end apart: 15, of which 13 were waited for; matrix products, arithmetic and copies ran while one was open for 6% of the time, Pallas kernels for 0%

profile of v4, /device:TPU:0, one launch (start us, length us, event | category | flops | bytes accessed | tf_op | source)
XLA Modules:
  0.0 280.7 jit_solution(3714357580924241587)
XLA Ops:
  0.0 3.6 %copy.6 = f32[64,128,32]{2,1,0:T(8,128)} copy(f32[64,128,32]{1,0,2:T(8,128)} %bitcast.101) | data formatting | bytes 2097152 | tf_op jit(solution)/shard_map/transpose | solution.py:163
  5.8 9.3 %shard_map.55 = f32[2048,128]{1,0:T(8,128)S(1)} custom-call(s32[8192]{0:T(1024)S(1)} %get-tuple-element.9.slot_ref, f32[8192,32]{1,0:T(8,128)S(1)} %bitcast.85), custom_call_target="tpu_custom_call" | custom-call | tf_op jit(solution)/shard_map/pallas_call | solution.py:77
  15.2 30.3 %all_to_all.33 = f32[128,16,128]{2,1,0:T(8,128)S(1)} all-to-all(f32[128,16,128]{2,1,0:T(8,128)S(1)} %bitcast.91), channel_id=1, replica_groups=mesh['iface'=4,'sub'=32] {'iface','sub'}, dimensions={0} | all-to-all | bytes 2097152 | tf_op jit(solution)/shard_map/all_to_all | solution.py:107
  45.5 10.9 %shard_map.56 = f32[8192,32]{1,0:T(8,128)S(1)} custom-call(s32[8192]{0:T(1024)S(1)} %get-tuple-element.10.src_ref, f32[8192,32]{1,0:T(8,128)} %bitcast.84, f32[2048,128]{1,0:T(8,128)S(1)} %bitcast.89), custom_call_target="tpu_custom_call" | custom-call | tf_op jit(solution)/shard_map/pallas_call | solution.py:91
  60.9 2.8 fusion.14
  63.6 10.3 %collective-permute-done.1 = bf16[32,64,128]{2,0,1:T(8,128)(2,1)S(1)} collective-permute-done((bf16[32,64,128]{2,0,1:T(8,128)(2,1)S(1)}, bf16[32,64,128]{2,0,1:T(8,128)(2,1)S(1)}, u32[]{:S(2)}, u32[]{:S(2)}) %collective-permute-start.1) | collective-permute-done | bytes 524320 | tf_op jit(solution)/shard_map/ppermute | solution.py:118
  74.0 2.8 fusion.6
  76.7 5.2 %collective-permute-done.2 = bf16[32,64,128]{2,0,1:T(8,128)(2,1)S(1)} collective-permute-done((bf16[32,64,128]{2,0,1:T(8,128)(2,1)S(1)}, bf16[32,64,128]{2,0,1:T(8,128)(2,1)S(1)}, u32[]{:S(2)}, u32[]{:S(2)}) %collective-permute-start.2) | collective-permute-done | bytes 524320 | tf_op jit(solution)/shard_map/ppermute | solution.py:118
  82.0 2.8 fusion.2
  84.7 2.8 %fusion.31 = f32[64,128,32]{1,2,0:T(8,128)S(1)} fusion(f32[64,128,32]{1,2,0:T(8,128)S(1)} %fusion.2, f32[64,128,32]{1,2,0:T(8,128)S(1)} %fusion.6, f32[64,128,32]{1,2,0:T(8,128)S(1)} %fusion.14, bf16[32,64,128]{2,0,1:T(8,128)(2,1)S(1)} %collective-permute-done, bf16[64,128,512]{2,1,0:T(8,128)(2,1)} %param.8, s32[]{:T(128)S(6)} %select_n.104), kind=kOutput, calls=%fused_computation.23 | convolution fusion | flops 67895296 | bytes 6815748 | tf_op jit(solution)/shard_map/src,ksc->srk/dot_general | solution.py:123
  92.4 9.3 %shard_map.57 = f32[2048,128]{1,0:T(8,128)S(1)} custom-call(s32[8192]{0:T(1024)S(1)} %get-tuple-element.9.slot_ref, f32[8192,32]{1,0:T(8,128)S(1)} %bitcast.87), custom_call_target="tpu_custom_call" | custom-call | tf_op jit(solution)/shard_map/pallas_call | solution.py:77
  101.7 25.4 %all_to_all.34 = f32[128,16,128]{2,1,0:T(8,128)S(1)} all-to-all(f32[128,16,128]{2,1,0:T(8,128)S(1)} %bitcast.92), channel_id=1, replica_groups=mesh['iface'=4,'sub'=32] {'iface','sub'}, dimensions={0} | all-to-all | bytes 2097152 | tf_op jit(solution)/shard_map/all_to_all | solution.py:107
  127.1 10.9 %shard_map.58 = f32[8192,32]{1,0:T(8,128)S(1)} custom-call(s32[8192]{0:T(1024)S(1)} %get-tuple-element.10.src_ref, f32[8192,32]{1,0:T(8,128)} %bitcast.86, f32[2048,128]{1,0:T(8,128)S(1)} %bitcast.90), custom_call_target="tpu_custom_call" | custom-call | tf_op jit(solution)/shard_map/pallas_call | solution.py:91
  142.4 2.8 fusion.12
  145.2 10.3 %collective-permute-done.4 = bf16[32,64,128]{2,0,1:T(8,128)(2,1)S(1)} collective-permute-done((bf16[32,64,128]{2,0,1:T(8,128)(2,1)S(1)}, bf16[32,64,128]{2,0,1:T(8,128)(2,1)S(1)}, u32[]{:S(2)}, u32[]{:S(2)}) %collective-permute-start.4) | collective-permute-done | bytes 524320 | tf_op jit(solution)/shard_map/ppermute | solution.py:118
  155.5 2.8 fusion.4
  158.3 5.2 %collective-permute-done.5 = bf16[32,64,128]{2,0,1:T(8,128)(2,1)S(1)} collective-permute-done((bf16[32,64,128]{2,0,1:T(8,128)(2,1)S(1)}, bf16[32,64,128]{2,0,1:T(8,128)(2,1)S(1)}, u32[]{:S(2)}, u32[]{:S(2)}) %collective-permute-start.5) | collective-permute-done | bytes 524320 | tf_op jit(solution)/shard_map/ppermute | solution.py:118
  163.5 2.8 fusion
  166.3 2.8 %fusion.28 = f32[64,128,32]{1,2,0:T(8,128)S(1)} fusion(f32[64,128,32]{1,2,0:T(8,128)S(1)} %fusion, f32[64,128,32]{1,2,0:T(8,128)S(1)} %fusion.4, f32[64,128,32]{1,2,0:T(8,128)S(1)} %fusion.12, bf16[32,64,128]{2,0,1:T(8,128)(2,1)S(1)} %collective-permute-done.3, bf16[64,128,512]{2,1,0:T(8,128)(2,1)} %param.8, s32[]{:T(128)S(6)} %select_n.104), kind=kOutput, calls=%fused_computation.22 | convolution fusion | flops 67895296 | bytes 6815748 | tf_op jit(solution)/shard_map/src,ksc->srk/dot_general | solution.py:123
  174.0 10.3 %shard_map.59 = f32[2048,128]{1,0:T(8,128)} custom-call(s32[8192]{0:T(1024)S(1)} %get-tuple-element.9.slot_ref, f32[8192,32]{1,0:T(8,128)S(1)} %bitcast.83), custom_call_target="tpu_custom_call" | custom-call | tf_op jit(solution)/shard_map/pallas_call | solution.py:77
  184.3 6.4 %all-to-all-start.2 = ((f32[128,16,128]{2,1,0:T(8,128)}), f32[128,16,128]{2,1,0:T(8,128)S(1)}, u32[]{:S(2)}, u32[]{:S(2)}) async-start(f32[128,16,128]{2,1,0:T(8,128)} %bitcast.15), calls=%async_computation.2 | async-start | bytes 2097152 | tf_op jit(solution)/shard_map/all_to_all | solution.py:107
  190.8 19.1 %all-to-all-done.2 = f32[128,16,128]{2,1,0:T(8,128)S(1)} async-done(((f32[128,16,128]{2,1,0:T(8,128)}), f32[128,16,128]{2,1,0:T(8,128)S(1)}, u32[]{:S(2)}, u32[]{:S(2)}) %all-to-all-start.2) | async-done | bytes 1048608 | tf_op jit(solution)/shard_map/all_to_all | solution.py:107
  209.8 10.9 %shard_map.60 = f32[8192,32]{1,0:T(8,128)S(1)} custom-call(s32[8192]{0:T(1024)S(1)} %get-tuple-element.10.src_ref, f32[8192,32]{1,0:T(8,128)} %bitcast.82, f32[2048,128]{1,0:T(8,128)S(1)} %bitcast.88), custom_call_target="tpu_custom_call" | custom-call | tf_op jit(solution)/shard_map/pallas_call | solution.py:91
  222.7 6.7 %fusion.67 = f32[32,32]{0,1:T(8,128)S(1)} fusion(f32[8192,32]{1,0:T(8,128)S(1)} %shard_map.60), kind=kOutput, calls=%fused_computation.94 | convolution fusion | flops 100663296 | bytes 1052672 | tf_op jit(solution)/shard_map/dot_general | solution.py:171
  229.5 2.8 gather_fusion
  233.9 3.7 %collective-permute-done.7 = f32[32,64]{0,1:T(8,128)S(1)} collective-permute-done((f32[32,64]{0,1:T(8,128)S(1)}, f32[32,64]{0,1:T(8,128)S(1)}, u32[]{:S(2)}, u32[]{:S(2)}) %collective-permute-start.7) | collective-permute-done | bytes 8224 | tf_op jit(solution)/shard_map/ppermute | solution.py:189
  237.7 5.3 %collective-permute-done.8 = f32[32,64]{0,1:T(8,128)S(1)} collective-permute-done((f32[32,64]{0,1:T(8,128)S(1)}, f32[32,64]{0,1:T(8,128)S(1)}, u32[]{:S(2)}, u32[]{:S(2)}) %collective-permute-start.8) | collective-permute-done | bytes 8224 | tf_op jit(solution)/shard_map/ppermute | solution.py:189
  243.6 3.4 %collective-permute-done.9 = f32[32,64]{0,1:T(8,128)S(1)} collective-permute-done((f32[32,64]{0,1:T(8,128)S(1)}, f32[32,64]{0,1:T(8,128)S(1)}, u32[]{:S(2)}, u32[]{:S(2)}) %collective-permute-start.9) | collective-permute-done | bytes 8224 | tf_op jit(solution)/shard_map/ppermute | solution.py:189
  247.0 5.4 %collective-permute-done.10 = f32[32,64]{0,1:T(8,128)S(1)} collective-permute-done((f32[32,64]{0,1:T(8,128)S(1)}, f32[32,64]{0,1:T(8,128)S(1)}, u32[]{:S(2)}, u32[]{:S(2)}) %collective-permute-start.10) | collective-permute-done | bytes 8224 | tf_op jit(solution)/shard_map/ppermute | solution.py:189
  259.0 2.9 %cholesky.44 = f32[32,32]{1,0:T(8,128)S(1)} custom-call(f32[32,32]{1,0:T(8,128)S(1)} %fusion.49), custom_call_target="Cholesky" | custom-call | tf_op jit(solution)/shard_map/jit(cholesky)/cholesky | solution.py:129
  266.4 2.9 %cholesky.55 = f32[32,32]{1,0:T(8,128)S(1)} custom-call(f32[32,32]{1,0:T(8,128)S(1)} %fusion.44), custom_call_target="Cholesky" | custom-call | tf_op jit(solution)/shard_map/jit(cholesky)/cholesky | solution.py:134
  273.5 6.0 %convolution_bitcast_fusion = f32[4,8,64,128]{3,1,2,0:T(8,128)S(1)} fusion(f32[32,32]{1,0:T(8,128)S(1)} %convolution_multiply_fusion, f32[8192,32]{1,0:T(8,128)} %copy-done), kind=kOutput, calls=%fused_computation.17 | convolution fusion | flops 100663296 | bytes 2101248 | tf_op jit(solution)/shard_map/dot_general | solution.py:206
  (72 shorter events, 41.5 us)
Async XLA Ops:
  0.0 3.6 %copy-start.5 = (s32[64,128]{1,0:T(8,128)S(1)}, s32[64,128]{1,0:T(8,128)}, u32[]{:S(2)}) copy-start(s32[64,128]{1,0:T(8,128)} %param.10) | copy-start | bytes 98308
  0.0 3.6 %copy-start.4 = (s32[64,128]{1,0:T(8,128)S(1)}, s32[64,128]{1,0:T(8,128)}, u32[]{:S(2)}) copy-start(s32[64,128]{1,0:T(8,128)} %param.11) | copy-start | bytes 98308
  3.7 2.2 copy-start.2
  57.5 16.4 %collective-permute-start.1 = (bf16[32,64,128]{2,0,1:T(8,128)(2,1)S(1)}, bf16[32,64,128]{2,0,1:T(8,128)(2,1)S(1)}, u32[]{:S(2)}, u32[]{:S(2)}) collective-permute-start(bf16[32,64,128]{2,0,1:T(8,128)(2,1)S(1)} %bitcast.95), channel_id=1, source_target_pairs={{0,64},{32,96},{64,0},{96,32},{1,65},{33,97},{65,1},{97,33},{2,66}... | collective-permute-start | bytes 1572872 | tf_op jit(solution)/shard_map/ppermute | solution.py:118
  58.2 23.7 %collective-permute-start.2 = (bf16[32,64,128]{2,0,1:T(8,128)(2,1)S(1)}, bf16[32,64,128]{2,0,1:T(8,128)(2,1)S(1)}, u32[]{:S(2)}, u32[]{:S(2)}) collective-permute-start(bf16[32,64,128]{2,0,1:T(8,128)(2,1)S(1)} %bitcast.96), channel_id=1, source_target_pairs={{0,96},{32,0},{64,32},{96,64},{1,97},{33,1},{65,33},{97,65},{2,98}... | collective-permute-start | bytes 1572872 | tf_op jit(solution)/shard_map/ppermute | solution.py:118
  60.9 23.9 %collective-permute-start = (bf16[32,64,128]{2,0,1:T(8,128)(2,1)S(1)}, bf16[32,64,128]{2,0,1:T(8,128)(2,1)S(1)}, u32[]{:S(2)}, u32[]{:S(2)}) collective-permute-start(bf16[32,64,128]{2,0,1:T(8,128)(2,1)S(1)} %bitcast.97), channel_id=1, source_target_pairs={{0,32},{32,64},{64,96},{96,0},{1,33},{33,65},{65,97},{97,1},{2,34}... | collective-permute-start | bytes 1572872 | tf_op jit(solution)/shard_map/ppermute | solution.py:118
  90.2 2.2 copy-start.3
  139.1 16.4 %collective-permute-start.4 = (bf16[32,64,128]{2,0,1:T(8,128)(2,1)S(1)}, bf16[32,64,128]{2,0,1:T(8,128)(2,1)S(1)}, u32[]{:S(2)}, u32[]{:S(2)}) collective-permute-start(bf16[32,64,128]{2,0,1:T(8,128)(2,1)S(1)} %bitcast.98), channel_id=1, source_target_pairs={{0,64},{32,96},{64,0},{96,32},{1,65},{33,97},{65,1},{97,33},{2,66}... | collective-permute-start | bytes 1572872 | tf_op jit(solution)/shard_map/ppermute | solution.py:118
  139.8 23.7 %collective-permute-start.5 = (bf16[32,64,128]{2,0,1:T(8,128)(2,1)S(1)}, bf16[32,64,128]{2,0,1:T(8,128)(2,1)S(1)}, u32[]{:S(2)}, u32[]{:S(2)}) collective-permute-start(bf16[32,64,128]{2,0,1:T(8,128)(2,1)S(1)} %bitcast.99), channel_id=1, source_target_pairs={{0,96},{32,0},{64,32},{96,64},{1,97},{33,1},{65,33},{97,65},{2,98}... | collective-permute-start | bytes 1572872 | tf_op jit(solution)/shard_map/ppermute | solution.py:118
  142.4 23.9 %collective-permute-start.3 = (bf16[32,64,128]{2,0,1:T(8,128)(2,1)S(1)}, bf16[32,64,128]{2,0,1:T(8,128)(2,1)S(1)}, u32[]{:S(2)}, u32[]{:S(2)}) collective-permute-start(bf16[32,64,128]{2,0,1:T(8,128)(2,1)S(1)} %bitcast.100), channel_id=1, source_target_pairs={{0,32},{32,64},{64,96},{96,0},{1,33},{33,65},{65,97},{97,1},{2,34}... | collective-permute-start | bytes 1572872 | tf_op jit(solution)/shard_map/ppermute | solution.py:118
  171.8 18.9 %copy-start.6 = (s32[32]{0:T(128)S(1)}, s32[32]{0:T(128)}, u32[]{:S(2)}) copy-start(s32[32]{0:T(128)} %param.12) | copy-start | bytes 388
  171.8 2.2 copy-start.1
  184.3 25.6 %all-to-all-start.2 = ((f32[128,16,128]{2,1,0:T(8,128)}), f32[128,16,128]{2,1,0:T(8,128)S(1)}, u32[]{:S(2)}, u32[]{:S(2)}) async-start(f32[128,16,128]{2,1,0:T(8,128)} %bitcast.15), calls=%async_computation.2 | async-start | bytes 2097152 | tf_op jit(solution)/shard_map/all_to_all | solution.py:107
  220.8 1.9 copy-start
  232.3 1.3 collective-permute-start.6
  233.6 4.0 %collective-permute-start.7 = (f32[32,64]{0,1:T(8,128)S(1)}, f32[32,64]{0,1:T(8,128)S(1)}, u32[]{:S(2)}, u32[]{:S(2)}) collective-permute-start(f32[32,64]{0,1:T(8,128)S(1)} %fusion.66), channel_id=1, source_target_pairs={{0,2},{1,3},{2,0},{3,1},{4,6},{5,7},{6,4},{7,5},{8,10},{9,11},{10,... | collective-permute-start | bytes 24584 | tf_op jit(solution)/shard_map/ppermute | solution.py:189
  237.6 5.4 %collective-permute-start.8 = (f32[32,64]{0,1:T(8,128)S(1)}, f32[32,64]{0,1:T(8,128)S(1)}, u32[]{:S(2)}, u32[]{:S(2)}) collective-permute-start(f32[32,64]{0,1:T(8,128)S(1)} %add.172), channel_id=1, source_target_pairs={{0,4},{1,5},{2,6},{3,7},{4,0},{5,1},{6,2},{7,3},{8,12},{9,13},{10,... | collective-permute-start | bytes 24584 | tf_op jit(solution)/shard_map/ppermute | solution.py:189
  243.0 3.9 %collective-permute-start.9 = (f32[32,64]{0,1:T(8,128)S(1)}, f32[32,64]{0,1:T(8,128)S(1)}, u32[]{:S(2)}, u32[]{:S(2)}) collective-permute-start(f32[32,64]{0,1:T(8,128)S(1)} %add.173), channel_id=1, source_target_pairs={{0,8},{1,9},{2,10},{3,11},{4,12},{5,13},{6,14},{7,15},{8,0},{9,1},... | collective-permute-start | bytes 24584 | tf_op jit(solution)/shard_map/ppermute | solution.py:189
  247.0 5.4 %collective-permute-start.10 = (f32[32,64]{0,1:T(8,128)S(1)}, f32[32,64]{0,1:T(8,128)S(1)}, u32[]{:S(2)}, u32[]{:S(2)}) collective-permute-start(f32[32,64]{0,1:T(8,128)S(1)} %add.174), channel_id=1, source_target_pairs={{0,16},{1,17},{2,18},{3,19},{4,20},{5,21},{6,22},{7,23},{8,24},{9,... | collective-permute-start | bytes 24584 | tf_op jit(solution)/shard_map/ppermute | solution.py:189
  252.4 5.1 %collective-permute-start.11 = (f32[32,64]{0,1:T(8,128)S(1)}, f32[32,64]{0,1:T(8,128)S(1)}, u32[]{:S(2)}, u32[]{:S(2)}) collective-permute-start(f32[32,64]{0,1:T(8,128)S(1)} %add.175), channel_id=1, source_target_pairs={{0,32},{32,64},{64,96},{96,0},{1,33},{33,65},{65,97},{97,1},{2,34}... | collective-permute-start | bytes 24584 | tf_op jit(solution)/shard_map/ppermute | solution.py:194
  253.0 5.4 %collective-permute-start.12 = (f32[32,64]{0,1:T(8,128)S(1)}, f32[32,64]{0,1:T(8,128)S(1)}, u32[]{:S(2)}, u32[]{:S(2)}) collective-permute-start(f32[32,64]{0,1:T(8,128)S(1)} %add.175), channel_id=1, source_target_pairs={{0,64},{32,96},{64,0},{96,32},{1,65},{33,97},{65,1},{97,33},{2,66}... | collective-permute-start | bytes 24584 | tf_op jit(solution)/shard_map/ppermute | solution.py:194
  255.0 3.9 %collective-permute-start.13 = (f32[32,64]{0,1:T(8,128)S(1)}, f32[32,64]{0,1:T(8,128)S(1)}, u32[]{:S(2)}, u32[]{:S(2)}) collective-permute-start(f32[32,64]{0,1:T(8,128)S(1)} %add.175), channel_id=1, source_target_pairs={{0,96},{32,0},{64,32},{96,64},{1,97},{33,1},{65,33},{97,65},{2,98}... | collective-permute-start | bytes 24584 | tf_op jit(solution)/shard_map/ppermute | solution.py:194

commit v5 on v2

--- a/solution.py
+++ b/solution.py
@@ -8,7 +8,7 @@
 from jax.experimental.pallas import tpu as pltpu
 from jax.sharding import PartitionSpec as P
 
-UNROLL = 32
+UNROLL = 64
 
 
 def _pack_kernel(slot_ref, *refs):
@@ -135,6 +135,26 @@
     return jax.scipy.linalg.cho_solve((lower_two, True), solved.T) * (
         total_rows / math.sqrt(sample_count)
     )
+
+
+def group_sum(x, axis, size):
+    place = lax.axis_index(axis)
+    bit = 1
+    while bit < size:
+        radix = min(4, size // bit)
+        got = [x] + [
+            lax.ppermute(x, axis, [(i, i ^ (m * bit)) for i in range(size)])
+            for m in range(1, radix)
+        ]
+        stacked = jnp.stack(got)
+        digit = (place // bit) % radix
+        total = None
+        for j in range(radix):
+            term = stacked[jnp.bitwise_xor(digit, j)]
+            total = term if total is None else total + term
+        x = total
+        bit *= radix
+    return x
 
 
 def shards(schur_blocks, noise_field, peer_device, partner_slot, pivot_rows):
@@ -183,8 +203,7 @@
         jnp.float32
     )
     partial = jnp.concatenate((gram_part, picked_part), axis=1)[None]
-    over_sub = jnp.sum(lax.all_gather(partial, "sub", axis=0, tiled=True), axis=0, keepdims=True)
-    total = jnp.sum(lax.all_gather(over_sub, "iface", axis=0, tiled=True), axis=0)
+    total = group_sum(group_sum(partial[0], "sub", sub_count), "iface", iface_count)
     gram_matrix = total[:, :sample_count]
     picked = total[:, sample_count:]
     total_rows = float(sub_local * sub_count * full_width)

time: 293 us -> 280 us (0.956)
  blocking collectives: 90.1 us -> 55.7 us
  starting transfers between devices: 13.1 us -> 27.4 us
  waiting for transfers between devices: 50.1 us -> 61.2 us
  Pallas kernels: 65.1 us -> 61.7 us
    all_gather x2 -> x0, blocking collectives: 34.4 us -> none  [the longest x1 22.3 us: shards(): lax.all_gather(partial, 'sub', axis=0, tiled=True)]
    ppermute x0 -> x10, starting transfers between devices: none -> 14.3 us  [group_sum(): lax.ppermute(x, axis, [(i, i ^ m * bit) for i in range(size)])]
    ppermute x0 -> x10, waiting for transfers between devices: none -> 11.1 us  [group_sum(): lax.ppermute(x, axis, [(i, i ^ m * bit) for i in range(size)])]
    unnamed x16 -> x15, local copies, waits for them, and re-layouts: 9.73 us -> 9.7 us
  transfers between devices with their start and end apart: 7 -> 17, of which waited for: 5 -> 11; matrix products, arithmetic and copies ran while one was open for 6% -> 6% of each run, Pallas kernels for 0% -> 0%
where the time goes in v5:
time: 280 us
  Pallas kernels  61.7 us (22%)
  waiting for transfers between devices  61.2 us (22%)
  blocking collectives  55.7 us (20%)
  matrix products  36 us (13%)
  starting transfers between devices  27.4 us (10%)
  local copies, waits for them, and re-layouts  23.3 us (8%)
  other arithmetic  14.1 us (5%)
    all_to_all x2, blocking collectives, exchange(): lax.all_to_all(outgoing, ('iface', 'sub'), split_axis=0, concat_axis=0, t...  55.7 us
    pallas_call x3, Pallas kernels, unpack_jump(): pl.pallas_call(functools.partial(_unpack_kernel, first, count), in_specs=...  32.8 us
    ppermute x6, waiting for transfers between devices, apply_blocks(): lax.ppermute(half, 'iface', [(i, (i + shift) % ring) for i in range(ring)])  31.1 us
    pallas_call x3, Pallas kernels, pack_rows(): pl.pallas_call(_pack_kernel, in_specs=[pl.BlockSpec(memory_space=pltpu.SM...  28.9 us
    dot_general x8, matrix products, apply_blocks(): jnp.einsum('src,ksc->srk', columns, block, preferred_element_type=jnp.flo...  22.3 us
    all_to_all x1, waiting for transfers between devices, exchange(): lax.all_to_all(outgoing, ('iface', 'sub'), split_axis=0, concat_axis=0, t...  19.1 us
    ppermute x10, starting transfers between devices, group_sum(): lax.ppermute(x, axis, [(i, i ^ m * bit) for i in range(size)])  14.3 us
    ppermute x10, waiting for transfers between devices, group_sum(): lax.ppermute(x, axis, [(i, i ^ m * bit) for i in range(size)])  11.1 us
  transfers between devices with their start and end apart: 17, of which 11 were waited for; matrix products, arithmetic and copies ran while one was open for 6% of the time, Pallas kernels for 0%

profile of v5, /device:TPU:0, one launch (start us, length us, event | category | flops | bytes accessed | tf_op | source)
XLA Modules:
  0.0 279.7 jit_solution(2560822635087538146)
XLA Ops:
  0.0 3.6 %copy.6 = f32[64,128,32]{2,1,0:T(8,128)} copy(f32[64,128,32]{1,0,2:T(8,128)} %bitcast.114) | data formatting | bytes 2097152 | tf_op jit(solution)/shard_map/transpose | solution.py:183
  5.9 9.3 %shard_map.55 = f32[2048,128]{1,0:T(8,128)S(1)} custom-call(s32[8192]{0:T(1024)S(1)} %get-tuple-element.9.slot_ref, f32[8192,32]{1,0:T(8,128)S(1)} %bitcast.98), custom_call_target="tpu_custom_call" | custom-call | tf_op jit(solution)/shard_map/pallas_call | solution.py:77
  15.2 30.3 %all_to_all.33 = f32[128,16,128]{2,1,0:T(8,128)S(1)} all-to-all(f32[128,16,128]{2,1,0:T(8,128)S(1)} %bitcast.104), channel_id=1, replica_groups=mesh['iface'=4,'sub'=32] {'iface','sub'}, dimensions={0} | all-to-all | bytes 2097152 | tf_op jit(solution)/shard_map/all_to_all | solution.py:107
  45.5 10.9 %shard_map.56 = f32[8192,32]{1,0:T(8,128)S(1)} custom-call(s32[8192]{0:T(1024)S(1)} %get-tuple-element.10.src_ref, f32[8192,32]{1,0:T(8,128)} %bitcast.97, f32[2048,128]{1,0:T(8,128)S(1)} %bitcast.102), custom_call_target="tpu_custom_call" | custom-call | tf_op jit(solution)/shard_map/pallas_call | solution.py:91
  60.9 2.8 fusion.14
  63.7 10.3 %collective-permute-done.1 = bf16[32,64,128]{2,0,1:T(8,128)(2,1)S(1)} collective-permute-done((bf16[32,64,128]{2,0,1:T(8,128)(2,1)S(1)}, bf16[32,64,128]{2,0,1:T(8,128)(2,1)S(1)}, u32[]{:S(2)}, u32[]{:S(2)}) %collective-permute-start.1) | collective-permute-done | bytes 524320 | tf_op jit(solution)/shard_map/ppermute | solution.py:118
  74.0 2.8 fusion.6
  76.8 5.2 %collective-permute-done.2 = bf16[32,64,128]{2,0,1:T(8,128)(2,1)S(1)} collective-permute-done((bf16[32,64,128]{2,0,1:T(8,128)(2,1)S(1)}, bf16[32,64,128]{2,0,1:T(8,128)(2,1)S(1)}, u32[]{:S(2)}, u32[]{:S(2)}) %collective-permute-start.2) | collective-permute-done | bytes 524320 | tf_op jit(solution)/shard_map/ppermute | solution.py:118
  82.0 2.8 fusion.2
  84.8 2.8 %fusion.31 = f32[64,128,32]{1,2,0:T(8,128)S(1)} fusion(f32[64,128,32]{1,2,0:T(8,128)S(1)} %fusion.2, f32[64,128,32]{1,2,0:T(8,128)S(1)} %fusion.6, f32[64,128,32]{1,2,0:T(8,128)S(1)} %fusion.14, bf16[32,64,128]{2,0,1:T(8,128)(2,1)S(1)} %collective-permute-done, bf16[64,128,512]{2,1,0:T(8,128)(2,1)} %param.8, s32[]{:T(128)S(6)} %select_n.149), kind=kOutput, calls=%fused_computation.23 | convolution fusion | flops 67895296 | bytes 6815748 | tf_op jit(solution)/shard_map/src,ksc->srk/dot_general | solution.py:123
  87.6 2.7 copy.8
  92.4 9.3 %shard_map.57 = f32[2048,128]{1,0:T(8,128)S(1)} custom-call(s32[8192]{0:T(1024)S(1)} %get-tuple-element.9.slot_ref, f32[8192,32]{1,0:T(8,128)S(1)} %bitcast.100), custom_call_target="tpu_custom_call" | custom-call | tf_op jit(solution)/shard_map/pallas_call | solution.py:77
  101.8 25.4 %all_to_all.34 = f32[128,16,128]{2,1,0:T(8,128)S(1)} all-to-all(f32[128,16,128]{2,1,0:T(8,128)S(1)} %bitcast.105), channel_id=1, replica_groups=mesh['iface'=4,'sub'=32] {'iface','sub'}, dimensions={0} | all-to-all | bytes 2097152 | tf_op jit(solution)/shard_map/all_to_all | solution.py:107
  127.1 10.9 %shard_map.58 = f32[8192,32]{1,0:T(8,128)S(1)} custom-call(s32[8192]{0:T(1024)S(1)} %get-tuple-element.10.src_ref, f32[8192,32]{1,0:T(8,128)} %bitcast.99, f32[2048,128]{1,0:T(8,128)S(1)} %bitcast.103), custom_call_target="tpu_custom_call" | custom-call | tf_op jit(solution)/shard_map/pallas_call | solution.py:91
  142.5 2.8 fusion.12
  145.3 10.3 %collective-permute-done.4 = bf16[32,64,128]{2,0,1:T(8,128)(2,1)S(1)} collective-permute-done((bf16[32,64,128]{2,0,1:T(8,128)(2,1)S(1)}, bf16[32,64,128]{2,0,1:T(8,128)(2,1)S(1)}, u32[]{:S(2)}, u32[]{:S(2)}) %collective-permute-start.4) | collective-permute-done | bytes 524320 | tf_op jit(solution)/shard_map/ppermute | solution.py:118
  155.6 2.8 fusion.4
  158.4 5.2 %collective-permute-done.5 = bf16[32,64,128]{2,0,1:T(8,128)(2,1)S(1)} collective-permute-done((bf16[32,64,128]{2,0,1:T(8,128)(2,1)S(1)}, bf16[32,64,128]{2,0,1:T(8,128)(2,1)S(1)}, u32[]{:S(2)}, u32[]{:S(2)}) %collective-permute-start.5) | collective-permute-done | bytes 524320 | tf_op jit(solution)/shard_map/ppermute | solution.py:118
  163.6 2.8 fusion
  166.4 2.8 %fusion.28 = f32[64,128,32]{1,2,0:T(8,128)S(1)} fusion(f32[64,128,32]{1,2,0:T(8,128)S(1)} %fusion, f32[64,128,32]{1,2,0:T(8,128)S(1)} %fusion.4, f32[64,128,32]{1,2,0:T(8,128)S(1)} %fusion.12, bf16[32,64,128]{2,0,1:T(8,128)(2,1)S(1)} %collective-permute-done.3, bf16[64,128,512]{2,1,0:T(8,128)(2,1)} %param.8, s32[]{:T(128)S(6)} %select_n.149), kind=kOutput, calls=%fused_computation.22 | convolution fusion | flops 67895296 | bytes 6815748 | tf_op jit(solution)/shard_map/src,ksc->srk/dot_general | solution.py:123
  169.2 2.7 copy.10
  174.1 10.3 %shard_map.59 = f32[2048,128]{1,0:T(8,128)} custom-call(s32[8192]{0:T(1024)S(1)} %get-tuple-element.9.slot_ref, f32[8192,32]{1,0:T(8,128)S(1)} %bitcast.96), custom_call_target="tpu_custom_call" | custom-call | tf_op jit(solution)/shard_map/pallas_call | solution.py:77
  184.3 6.4 %all-to-all-start.2 = ((f32[128,16,128]{2,1,0:T(8,128)}), f32[128,16,128]{2,1,0:T(8,128)S(1)}, u32[]{:S(2)}, u32[]{:S(2)}) async-start(f32[128,16,128]{2,1,0:T(8,128)} %bitcast.15), calls=%async_computation.2 | async-start | bytes 2097152 | tf_op jit(solution)/shard_map/all_to_all | solution.py:107
  190.8 19.1 %all-to-all-done.2 = f32[128,16,128]{2,1,0:T(8,128)S(1)} async-done(((f32[128,16,128]{2,1,0:T(8,128)}), f32[128,16,128]{2,1,0:T(8,128)S(1)}, u32[]{:S(2)}, u32[]{:S(2)}) %all-to-all-start.2) | async-done | bytes 1048608 | tf_op jit(solution)/shard_map/all_to_all | solution.py:107
  209.9 10.9 %shard_map.60 = f32[8192,32]{1,0:T(8,128)S(1)} custom-call(s32[8192]{0:T(1024)S(1)} %get-tuple-element.10.src_ref, f32[8192,32]{1,0:T(8,128)} %bitcast.95, f32[2048,128]{1,0:T(8,128)S(1)} %bitcast.101), custom_call_target="tpu_custom_call" | custom-call | tf_op jit(solution)/shard_map/pallas_call | solution.py:91
  222.8 6.7 %fusion.70 = f32[32,32]{0,1:T(8,128)S(1)} fusion(f32[8192,32]{1,0:T(8,128)S(1)} %shard_map.60), kind=kOutput, calls=%fused_computation.105 | convolution fusion | flops 100663296 | bytes 1052672 | tf_op jit(solution)/shard_map/dot_general | solution.py:191
  229.6 2.8 gather_fusion
  238.1 3.6 %collective-permute-start.11 = (f32[32,64]{0,1:T(8,128)S(1)}, f32[32,64]{0,1:T(8,128)S(1)}, u32[]{:S(2)}, u32[]{:S(2)}) collective-permute-start(f32[32,64]{0,1:T(8,128)S(1)} %fusion.85), channel_id=1, source_target_pairs={{0,12},{1,13},{2,14},{3,15},{4,8},{5,9},{6,10},{7,11},{8,4},{9,5},... | collective-permute-start | bytes 24584 | tf_op jit(solution)/shard_map/ppermute | solution.py:146
  247.0 3.0 %collective-permute-done.12 = f32[32,64]{0,1:T(8,128)S(1)} collective-permute-done((f32[32,64]{0,1:T(8,128)S(1)}, f32[32,64]{0,1:T(8,128)S(1)}, u32[]{:S(2)}, u32[]{:S(2)}) %collective-permute-start.12) | collective-permute-done | bytes 8224 | tf_op jit(solution)/shard_map/ppermute | solution.py:146
  258.1 2.9 %cholesky.44 = f32[32,32]{1,0:T(8,128)S(1)} custom-call(f32[32,32]{1,0:T(8,128)S(1)} %fusion.52), custom_call_target="Cholesky" | custom-call | tf_op jit(solution)/shard_map/jit(cholesky)/cholesky | solution.py:129
  265.5 2.9 %cholesky.55 = f32[32,32]{1,0:T(8,128)S(1)} custom-call(f32[32,32]{1,0:T(8,128)S(1)} %fusion.47), custom_call_target="Cholesky" | custom-call | tf_op jit(solution)/shard_map/jit(cholesky)/cholesky | solution.py:134
  272.5 6.0 %convolution_bitcast_fusion = f32[4,8,64,128]{3,1,2,0:T(8,128)S(1)} fusion(f32[32,32]{1,0:T(8,128)S(1)} %convolution_multiply_fusion, f32[8192,32]{1,0:T(8,128)} %copy-done), kind=kOutput, calls=%fused_computation.17 | convolution fusion | flops 100663296 | bytes 2101248 | tf_op jit(solution)/shard_map/dot_general | solution.py:211
  (78 shorter events, 46.2 us)
Async XLA Ops:
  0.0 3.7 %copy-start.5 = (s32[64,128]{1,0:T(8,128)S(1)}, s32[64,128]{1,0:T(8,128)}, u32[]{:S(2)}) copy-start(s32[64,128]{1,0:T(8,128)} %param.10) | copy-start | bytes 98308
  0.0 3.7 %copy-start.4 = (s32[64,128]{1,0:T(8,128)S(1)}, s32[64,128]{1,0:T(8,128)}, u32[]{:S(2)}) copy-start(s32[64,128]{1,0:T(8,128)} %param.11) | copy-start | bytes 98308
  3.7 2.2 copy-start.2
  57.6 16.4 %collective-permute-start.1 = (bf16[32,64,128]{2,0,1:T(8,128)(2,1)S(1)}, bf16[32,64,128]{2,0,1:T(8,128)(2,1)S(1)}, u32[]{:S(2)}, u32[]{:S(2)}) collective-permute-start(bf16[32,64,128]{2,0,1:T(8,128)(2,1)S(1)} %bitcast.108), channel_id=1, source_target_pairs={{0,64},{32,96},{64,0},{96,32},{1,65},{33,97},{65,1},{97,33},{2,66}... | collective-permute-start | bytes 1572872 | tf_op jit(solution)/shard_map/ppermute | solution.py:118
  58.3 23.7 %collective-permute-start.2 = (bf16[32,64,128]{2,0,1:T(8,128)(2,1)S(1)}, bf16[32,64,128]{2,0,1:T(8,128)(2,1)S(1)}, u32[]{:S(2)}, u32[]{:S(2)}) collective-permute-start(bf16[32,64,128]{2,0,1:T(8,128)(2,1)S(1)} %bitcast.109), channel_id=1, source_target_pairs={{0,96},{32,0},{64,32},{96,64},{1,97},{33,1},{65,33},{97,65},{2,98}... | collective-permute-start | bytes 1572872 | tf_op jit(solution)/shard_map/ppermute | solution.py:118
  60.9 23.9 %collective-permute-start = (bf16[32,64,128]{2,0,1:T(8,128)(2,1)S(1)}, bf16[32,64,128]{2,0,1:T(8,128)(2,1)S(1)}, u32[]{:S(2)}, u32[]{:S(2)}) collective-permute-start(bf16[32,64,128]{2,0,1:T(8,128)(2,1)S(1)} %bitcast.110), channel_id=1, source_target_pairs={{0,32},{32,64},{64,96},{96,0},{1,33},{33,65},{65,97},{97,1},{2,34}... | collective-permute-start | bytes 1572872 | tf_op jit(solution)/shard_map/ppermute | solution.py:118
  90.3 2.2 copy-start.3
  139.2 16.4 %collective-permute-start.4 = (bf16[32,64,128]{2,0,1:T(8,128)(2,1)S(1)}, bf16[32,64,128]{2,0,1:T(8,128)(2,1)S(1)}, u32[]{:S(2)}, u32[]{:S(2)}) collective-permute-start(bf16[32,64,128]{2,0,1:T(8,128)(2,1)S(1)} %bitcast.111), channel_id=1, source_target_pairs={{0,64},{32,96},{64,0},{96,32},{1,65},{33,97},{65,1},{97,33},{2,66}... | collective-permute-start | bytes 1572872 | tf_op jit(solution)/shard_map/ppermute | solution.py:118
  139.9 23.7 %collective-permute-start.5 = (bf16[32,64,128]{2,0,1:T(8,128)(2,1)S(1)}, bf16[32,64,128]{2,0,1:T(8,128)(2,1)S(1)}, u32[]{:S(2)}, u32[]{:S(2)}) collective-permute-start(bf16[32,64,128]{2,0,1:T(8,128)(2,1)S(1)} %bitcast.112), channel_id=1, source_target_pairs={{0,96},{32,0},{64,32},{96,64},{1,97},{33,1},{65,33},{97,65},{2,98}... | collective-permute-start | bytes 1572872 | tf_op jit(solution)/shard_map/ppermute | solution.py:118
  142.5 23.9 %collective-permute-start.3 = (bf16[32,64,128]{2,0,1:T(8,128)(2,1)S(1)}, bf16[32,64,128]{2,0,1:T(8,128)(2,1)S(1)}, u32[]{:S(2)}, u32[]{:S(2)}) collective-permute-start(bf16[32,64,128]{2,0,1:T(8,128)(2,1)S(1)} %bitcast.113), channel_id=1, source_target_pairs={{0,32},{32,64},{64,96},{96,0},{1,33},{33,65},{65,97},{97,1},{2,34}... | collective-permute-start | bytes 1572872 | tf_op jit(solution)/shard_map/ppermute | solution.py:118
  171.9 18.9 %copy-start.6 = (s32[32]{0:T(128)S(1)}, s32[32]{0:T(128)}, u32[]{:S(2)}) copy-start(s32[32]{0:T(128)} %param.12) | copy-start | bytes 388
  171.9 2.2 copy-start.1
  184.3 25.6 %all-to-all-start.2 = ((f32[128,16,128]{2,1,0:T(8,128)}), f32[128,16,128]{2,1,0:T(8,128)S(1)}, u32[]{:S(2)}, u32[]{:S(2)}) async-start(f32[128,16,128]{2,1,0:T(8,128)} %bitcast.15), calls=%async_computation.2 | async-start | bytes 2097152 | tf_op jit(solution)/shard_map/all_to_all | solution.py:107
  220.9 2.0 copy-start
  232.4 1.9 collective-permute-start.6
  232.5 4.1 %collective-permute-start.7 = (f32[32,64]{0,1:T(8,128)S(1)}, f32[32,64]{0,1:T(8,128)S(1)}, u32[]{:S(2)}, u32[]{:S(2)}) collective-permute-start(f32[32,64]{0,1:T(8,128)S(1)} %get-tuple-element.12), channel_id=1, source_target_pairs={{0,2},{1,3},{2,0},{3,1},{4,6},{5,7},{6,4},{7,5},{8,10},{9,11},{10,... | collective-permute-start | bytes 24584 | tf_op jit(solution)/shard_map/ppermute | solution.py:146
  232.8 3.8 %collective-permute-start.8 = (f32[32,64]{0,1:T(8,128)S(1)}, f32[32,64]{0,1:T(8,128)S(1)}, u32[]{:S(2)}, u32[]{:S(2)}) collective-permute-start(f32[32,64]{0,1:T(8,128)S(1)} %get-tuple-element.12), channel_id=1, source_target_pairs={{0,3},{1,2},{2,1},{3,0},{4,7},{5,6},{6,5},{7,4},{8,11},{9,10},{10,... | collective-permute-start | bytes 24584 | tf_op jit(solution)/shard_map/ppermute | solution.py:146
  236.7 5.5 %collective-permute-start.9 = (f32[32,64]{0,1:T(8,128)S(1)}, f32[32,64]{0,1:T(8,128)S(1)}, u32[]{:S(2)}, u32[]{:S(2)}) collective-permute-start(f32[32,64]{0,1:T(8,128)S(1)} %fusion.85), channel_id=1, source_target_pairs={{0,4},{1,5},{2,6},{3,7},{4,0},{5,1},{6,2},{7,3},{8,12},{9,13},{10,... | collective-permute-start | bytes 24584 | tf_op jit(solution)/shard_map/ppermute | solution.py:146
  237.8 4.4 %collective-permute-start.10 = (f32[32,64]{0,1:T(8,128)S(1)}, f32[32,64]{0,1:T(8,128)S(1)}, u32[]{:S(2)}, u32[]{:S(2)}) collective-permute-start(f32[32,64]{0,1:T(8,128)S(1)} %fusion.85), channel_id=1, source_target_pairs={{0,8},{1,9},{2,10},{3,11},{4,12},{5,13},{6,14},{7,15},{8,0},{9,1},... | collective-permute-start | bytes 24584 | tf_op jit(solution)/shard_map/ppermute | solution.py:146
  238.1 6.3 %collective-permute-start.11 = (f32[32,64]{0,1:T(8,128)S(1)}, f32[32,64]{0,1:T(8,128)S(1)}, u32[]{:S(2)}, u32[]{:S(2)}) collective-permute-start(f32[32,64]{0,1:T(8,128)S(1)} %fusion.85), channel_id=1, source_target_pairs={{0,12},{1,13},{2,14},{3,15},{4,8},{5,9},{6,10},{7,11},{8,4},{9,5},... | collective-permute-start | bytes 24584 | tf_op jit(solution)/shard_map/ppermute | solution.py:146
  244.5 5.5 %collective-permute-start.12 = (f32[32,64]{0,1:T(8,128)S(1)}, f32[32,64]{0,1:T(8,128)S(1)}, u32[]{:S(2)}, u32[]{:S(2)}) collective-permute-start(f32[32,64]{0,1:T(8,128)S(1)} %fusion.84), channel_id=1, source_target_pairs={{0,16},{1,17},{2,18},{3,19},{4,20},{5,21},{6,22},{7,23},{8,24},{9,... | collective-permute-start | bytes 24584 | tf_op jit(solution)/shard_map/ppermute | solution.py:146
  250.0 4.8 %collective-permute-start.13 = (f32[32,64]{0,1:T(8,128)S(1)}, f32[32,64]{0,1:T(8,128)S(1)}, u32[]{:S(2)}, u32[]{:S(2)}) collective-permute-start(f32[32,64]{0,1:T(8,128)S(1)} %bitcast.115), channel_id=1, source_target_pairs={{0,32},{32,0},{64,96},{96,64},{1,33},{33,1},{65,97},{97,65},{2,34}... | collective-permute-start | bytes 24584 | tf_op jit(solution)/shard_map/ppermute | solution.py:146
  250.8 5.4 %collective-permute-start.14 = (f32[32,64]{0,1:T(8,128)S(1)}, f32[32,64]{0,1:T(8,128)S(1)}, u32[]{:S(2)}, u32[]{:S(2)}) collective-permute-start(f32[32,64]{0,1:T(8,128)S(1)} %bitcast.116), channel_id=1, source_target_pairs={{0,64},{32,96},{64,0},{96,32},{1,65},{33,97},{65,1},{97,33},{2,66}... | collective-permute-start | bytes 24584 | tf_op jit(solution)/shard_map/ppermute | solution.py:146
  252.8 5.1 %collective-permute-start.15 = (f32[32,64]{0,1:T(8,128)S(1)}, f32[32,64]{0,1:T(8,128)S(1)}, u32[]{:S(2)}, u32[]{:S(2)}) collective-permute-start(f32[32,64]{0,1:T(8,128)S(1)} %bitcast.117), channel_id=1, source_target_pairs={{0,96},{32,64},{64,32},{96,0},{1,97},{33,65},{65,33},{97,1},{2,98}... | collective-permute-start | bytes 24584 | tf_op jit(solution)/shard_map/ppermute | solution.py:146

commit v6 on v5

--- a/solution.py
+++ b/solution.py
@@ -112,16 +112,31 @@
     half = jump_rows.astype(jnp.bfloat16).reshape(sub_local, group, width).transpose(2, 0, 1)
     ring = lax.axis_size("iface")
     here = lax.axis_index("iface")
-    total = None
-    for shift in range(ring):
-        if shift:
-            block = lax.ppermute(half, "iface", [(i, (i + shift) % ring) for i in range(ring)])
-        else:
-            block = half
-        owner = (here - shift) % ring
+
+    def shifted(value, shift):
+        return lax.ppermute(value, "iface", [(i, (i + shift) % ring) for i in range(ring)])
+
+    def product(block, owner):
         columns = lax.dynamic_slice_in_dim(schur_blocks, owner * group, group, axis=2)
-        part = jnp.einsum("src,ksc->srk", columns, block, preferred_element_type=jnp.float32)
-        total = part if total is None else total + part
+        return jnp.einsum("src,ksc->srk", columns, block, preferred_element_type=jnp.float32)
+
+    if ring == 4:
+        from_left = shifted(half, 1)
+        from_right = shifted(half, ring - 1)
+        split = width // 2
+        far = jnp.concatenate(
+            (shifted(from_left[:split], 1), shifted(from_right[split:], ring - 1)), axis=0
+        )
+        total = product(half, here)
+        total = total + product(from_left, (here + ring - 1) % ring)
+        total = total + product(from_right, (here + 1) % ring)
+        total = total + product(far, (here + 2) % ring)
+    else:
+        total = None
+        for shift in range(ring):
+            block = shifted(half, shift) if shift else half
+            part = product(block, (here - shift) % ring)
+            total = part if total is None else total + part
     return total.reshape(sub_local * group, width)
 
 

time: 280 us -> 279 us (level)
  waiting for transfers between devices: 61.2 us -> 50.2 us
  starting transfers between devices: 27.4 us -> 35.3 us
    ppermute x6 -> x8, waiting for transfers between devices: 31.1 us -> 20.1 us  [shifted(): lax.ppermute(value, 'iface', [(i, (i + shift) % ring) for i in range(ring)])]
    ppermute x6 -> x8, starting transfers between devices: 6.67 us -> 13.3 us  [shifted(): lax.ppermute(value, 'iface', [(i, (i + shift) % ring) for i in range(ring)])]
  transfers between devices with their start and end apart: 17 -> 19, of which waited for: 11 -> 11; matrix products, arithmetic and copies ran while one was open for 6% -> 4% of each run, Pallas kernels for 0% -> 0%
where the time goes in v6:
time: 279 us; the launch traced here: 278 us
  Pallas kernels  61.7 us (22%)
  blocking collectives  56.9 us (20%)
  waiting for transfers between devices  50.2 us (18%)
  matrix products  36 us (13%)
  starting transfers between devices  35.3 us (13%)
  local copies, waits for them, and re-layouts  23.4 us (8%)
  other arithmetic  14.1 us (5%)
    all_to_all x2, blocking collectives, exchange(): lax.all_to_all(outgoing, ('iface', 'sub'), split_axis=0, concat_axis=0, t...  56.9 us
    pallas_call x3, Pallas kernels, unpack_jump(): pl.pallas_call(functools.partial(_unpack_kernel, first, count), in_specs=...  32.8 us
    pallas_call x3, Pallas kernels, pack_rows(): pl.pallas_call(_pack_kernel, in_specs=[pl.BlockSpec(memory_space=pltpu.SM...  28.9 us
    dot_general x8, matrix products, product(): jnp.einsum('src,ksc->srk', columns, block, preferred_element_type=jnp.flo...  22.3 us
    ppermute x8, waiting for transfers between devices, shifted(): lax.ppermute(value, 'iface', [(i, (i + shift) % ring) for i in range(ring)])  20.1 us
    all_to_all x1, waiting for transfers between devices, exchange(): lax.all_to_all(outgoing, ('iface', 'sub'), split_axis=0, concat_axis=0, t...  19.1 us
    ppermute x10, starting transfers between devices, group_sum(): lax.ppermute(x, axis, [(i, i ^ m * bit) for i in range(size)])  14.3 us
    ppermute x8, starting transfers between devices, shifted(): lax.ppermute(value, 'iface', [(i, (i + shift) % ring) for i in range(ring)])  13.3 us
  transfers between devices with their start and end apart: 19, of which 11 were waited for; matrix products, arithmetic and copies ran while one was open for 4% of the time, Pallas kernels for 0%

profile of v6, /device:TPU:0, one launch (start us, length us, event | category | flops | bytes accessed | tf_op | source)
XLA Modules:
  0.0 277.9 jit_solution(17260148017230851916)
XLA Ops:
  0.0 3.6 %copy.6 = f32[64,128,32]{2,1,0:T(8,128)} copy(f32[64,128,32]{1,0,2:T(8,128)} %bitcast.110) | data formatting | bytes 2097152 | tf_op jit(solution)/shard_map/transpose | solution.py:198
  5.9 9.3 %shard_map.55 = f32[2048,128]{1,0:T(8,128)S(1)} custom-call(s32[8192]{0:T(1024)S(1)} %get-tuple-element.9.slot_ref, f32[8192,32]{1,0:T(8,128)S(1)} %bitcast.96), custom_call_target="tpu_custom_call" | custom-call | tf_op jit(solution)/shard_map/pallas_call | solution.py:77
  15.2 30.3 %all_to_all.33 = f32[128,16,128]{2,1,0:T(8,128)S(1)} all-to-all(f32[128,16,128]{2,1,0:T(8,128)S(1)} %bitcast.102), channel_id=1, replica_groups=mesh['iface'=4,'sub'=32] {'iface','sub'}, dimensions={0} | all-to-all | bytes 2097152 | tf_op jit(solution)/shard_map/all_to_all | solution.py:107
  45.5 10.9 %shard_map.56 = f32[8192,32]{1,0:T(8,128)S(1)} custom-call(s32[8192]{0:T(1024)S(1)} %get-tuple-element.10.src_ref, f32[8192,32]{1,0:T(8,128)} %bitcast.95, f32[2048,128]{1,0:T(8,128)S(1)} %bitcast.100), custom_call_target="tpu_custom_call" | custom-call | tf_op jit(solution)/shard_map/pallas_call | solution.py:91
  60.9 2.8 fusion.14
  63.6 8.3 %collective-permute-done = bf16[32,64,128]{2,0,1:T(8,128)(2,1)S(1)} collective-permute-done((bf16[32,64,128]{2,0,1:T(8,128)(2,1)S(1)}, bf16[32,64,128]{2,0,1:T(8,128)(2,1)S(1)}, u32[]{:S(2)}, u32[]{:S(2)}) %collective-permute-start) | collective-permute-done | bytes 524320 | tf_op jit(solution)/shard_map/ppermute | solution.py:117
  72.1 3.3 %collective-permute-start.3 = (bf16[16,64,128]{2,0,1:T(8,128)(2,1)S(1)}, bf16[16,64,128]{2,0,1:T(8,128)(2,1)S(1)}, u32[]{:S(2)}, u32[]{:S(2)}) collective-permute-start(bf16[16,64,128]{2,0,1:T(8,128)(2,1)S(1)} %slice.39), channel_id=1, source_target_pairs={{0,96},{32,0},{64,32},{96,64},{1,97},{33,1},{65,33},{97,65},{2,98}... | collective-permute-start | bytes 786440 | tf_op jit(solution)/shard_map/ppermute | solution.py:117
  75.4 2.8 fusion.6
  79.9 2.8 %fusion.2 = f32[64,128,32]{1,2,0:T(8,128)S(1)} fusion(bf16[64,128,512]{2,1,0:T(8,128)(2,1)} %param.8, s32[]{:T(128)S(6)} %select_n.148, bf16[16,64,128]{2,0,1:T(8,128)(2,1)S(1)} %collective-permute-done.3, bf16[16,64,128]{2,0,1:T(8,128)(2,1)S(1)} %collective-permute-done.2), kind=kOutput, calls=%fused_computation.3 | convolution fusion | flops 68157440 | bytes 3670020 | tf_op jit(solution)/shard_map/src,ksc->srk/dot_general | solution.py:121
  82.7 2.8 %fusion.31 = f32[64,128,32]{1,2,0:T(8,128)S(1)} fusion(f32[64,128,32]{1,2,0:T(8,128)S(1)} %fusion.2, f32[64,128,32]{1,2,0:T(8,128)S(1)} %fusion.6, f32[64,128,32]{1,2,0:T(8,128)S(1)} %fusion.14, bf16[32,64,128]{2,0,1:T(8,128)(2,1)S(1)} %collective-permute-done, bf16[64,128,512]{2,1,0:T(8,128)(2,1)} %param.8, s32[]{:T(128)S(6)} %select_n.144), kind=kOutput, calls=%fused_computation.23 | convolution fusion | flops 67895296 | bytes 6815748 | tf_op jit(solution)/shard_map/src,ksc->srk/dot_general | solution.py:121
  85.5 2.7 copy.8
  90.3 9.3 %shard_map.57 = f32[2048,128]{1,0:T(8,128)S(1)} custom-call(s32[8192]{0:T(1024)S(1)} %get-tuple-element.9.slot_ref, f32[8192,32]{1,0:T(8,128)S(1)} %bitcast.98), custom_call_target="tpu_custom_call" | custom-call | tf_op jit(solution)/shard_map/pallas_call | solution.py:77
  99.6 26.6 %all_to_all.34 = f32[128,16,128]{2,1,0:T(8,128)S(1)} all-to-all(f32[128,16,128]{2,1,0:T(8,128)S(1)} %bitcast.103), channel_id=1, replica_groups=mesh['iface'=4,'sub'=32] {'iface','sub'}, dimensions={0} | all-to-all | bytes 2097152 | tf_op jit(solution)/shard_map/all_to_all | solution.py:107
  126.2 10.9 %shard_map.58 = f32[8192,32]{1,0:T(8,128)S(1)} custom-call(s32[8192]{0:T(1024)S(1)} %get-tuple-element.10.src_ref, f32[8192,32]{1,0:T(8,128)} %bitcast.97, f32[2048,128]{1,0:T(8,128)S(1)} %bitcast.101), custom_call_target="tpu_custom_call" | custom-call | tf_op jit(solution)/shard_map/pallas_call | solution.py:91
  141.5 2.8 fusion.12
  144.3 8.3 %collective-permute-done.4 = bf16[32,64,128]{2,0,1:T(8,128)(2,1)S(1)} collective-permute-done((bf16[32,64,128]{2,0,1:T(8,128)(2,1)S(1)}, bf16[32,64,128]{2,0,1:T(8,128)(2,1)S(1)}, u32[]{:S(2)}, u32[]{:S(2)}) %collective-permute-start.4) | collective-permute-done | bytes 524320 | tf_op jit(solution)/shard_map/ppermute | solution.py:117
  152.8 3.3 %collective-permute-start.7 = (bf16[16,64,128]{2,0,1:T(8,128)(2,1)S(1)}, bf16[16,64,128]{2,0,1:T(8,128)(2,1)S(1)}, u32[]{:S(2)}, u32[]{:S(2)}) collective-permute-start(bf16[16,64,128]{2,0,1:T(8,128)(2,1)S(1)} %slice.41), channel_id=1, source_target_pairs={{0,96},{32,0},{64,32},{96,64},{1,97},{33,1},{65,33},{97,65},{2,98}... | collective-permute-start | bytes 786440 | tf_op jit(solution)/shard_map/ppermute | solution.py:117
  156.1 2.8 fusion.4
  160.6 2.8 %fusion = f32[64,128,32]{1,2,0:T(8,128)S(1)} fusion(bf16[64,128,512]{2,1,0:T(8,128)(2,1)} %param.8, s32[]{:T(128)S(6)} %select_n.148, bf16[16,64,128]{2,0,1:T(8,128)(2,1)S(1)} %collective-permute-done.7, bf16[16,64,128]{2,0,1:T(8,128)(2,1)S(1)} %collective-permute-done.6), kind=kOutput, calls=%fused_computation.1 | convolution fusion | flops 68157440 | bytes 3670020 | tf_op jit(solution)/shard_map/src,ksc->srk/dot_general | solution.py:121
  163.3 2.8 %fusion.28 = f32[64,128,32]{1,2,0:T(8,128)S(1)} fusion(f32[64,128,32]{1,2,0:T(8,128)S(1)} %fusion, f32[64,128,32]{1,2,0:T(8,128)S(1)} %fusion.4, f32[64,128,32]{1,2,0:T(8,128)S(1)} %fusion.12, bf16[32,64,128]{2,0,1:T(8,128)(2,1)S(1)} %collective-permute-done.4, bf16[64,128,512]{2,1,0:T(8,128)(2,1)} %param.8, s32[]{:T(128)S(6)} %select_n.144), kind=kOutput, calls=%fused_computation.22 | convolution fusion | flops 67895296 | bytes 6815748 | tf_op jit(solution)/shard_map/src,ksc->srk/dot_general | solution.py:121
  166.2 2.7 copy.10
  171.0 10.3 %shard_map.59 = f32[2048,128]{1,0:T(8,128)} custom-call(s32[8192]{0:T(1024)S(1)} %get-tuple-element.9.slot_ref, f32[8192,32]{1,0:T(8,128)S(1)} %bitcast.94), custom_call_target="tpu_custom_call" | custom-call | tf_op jit(solution)/shard_map/pallas_call | solution.py:77
  181.3 7.6 %all-to-all-start.2 = ((f32[128,16,128]{2,1,0:T(8,128)}), f32[128,16,128]{2,1,0:T(8,128)S(1)}, u32[]{:S(2)}, u32[]{:S(2)}) async-start(f32[128,16,128]{2,1,0:T(8,128)} %bitcast.15), calls=%async_computation.2 | async-start | bytes 2097152 | tf_op jit(solution)/shard_map/all_to_all | solution.py:107
  189.0 19.1 %all-to-all-done.2 = f32[128,16,128]{2,1,0:T(8,128)S(1)} async-done(((f32[128,16,128]{2,1,0:T(8,128)}), f32[128,16,128]{2,1,0:T(8,128)S(1)}, u32[]{:S(2)}, u32[]{:S(2)}) %all-to-all-start.2) | async-done | bytes 1048608 | tf_op jit(solution)/shard_map/all_to_all | solution.py:107
  208.1 10.9 %shard_map.60 = f32[8192,32]{1,0:T(8,128)S(1)} custom-call(s32[8192]{0:T(1024)S(1)} %get-tuple-element.10.src_ref, f32[8192,32]{1,0:T(8,128)} %bitcast.93, f32[2048,128]{1,0:T(8,128)S(1)} %bitcast.99), custom_call_target="tpu_custom_call" | custom-call | tf_op jit(solution)/shard_map/pallas_call | solution.py:91
  221.0 6.7 %fusion.78 = f32[32,32]{0,1:T(8,128)S(1)} fusion(f32[8192,32]{1,0:T(8,128)S(1)} %shard_map.60), kind=kOutput, calls=%fused_computation.113 | convolution fusion | flops 100663296 | bytes 1052672 | tf_op jit(solution)/shard_map/dot_general | solution.py:206
  227.7 2.8 gather_fusion
  236.3 3.6 %collective-permute-start.13 = (f32[32,64]{0,1:T(8,128)S(1)}, f32[32,64]{0,1:T(8,128)S(1)}, u32[]{:S(2)}, u32[]{:S(2)}) collective-permute-start(f32[32,64]{0,1:T(8,128)S(1)} %fusion.91), channel_id=1, source_target_pairs={{0,12},{1,13},{2,14},{3,15},{4,8},{5,9},{6,10},{7,11},{8,4},{9,5},... | collective-permute-start | bytes 24584 | tf_op jit(solution)/shard_map/ppermute | solution.py:161
  245.2 3.0 %collective-permute-done.14 = f32[32,64]{0,1:T(8,128)S(1)} collective-permute-done((f32[32,64]{0,1:T(8,128)S(1)}, f32[32,64]{0,1:T(8,128)S(1)}, u32[]{:S(2)}, u32[]{:S(2)}) %collective-permute-start.14) | collective-permute-done | bytes 8224 | tf_op jit(solution)/shard_map/ppermute | solution.py:161
  256.2 2.9 %cholesky.44 = f32[32,32]{1,0:T(8,128)S(1)} custom-call(f32[32,32]{1,0:T(8,128)S(1)} %fusion.58), custom_call_target="Cholesky" | custom-call | tf_op jit(solution)/shard_map/jit(cholesky)/cholesky | solution.py:144
  263.6 2.9 %cholesky.55 = f32[32,32]{1,0:T(8,128)S(1)} custom-call(f32[32,32]{1,0:T(8,128)S(1)} %fusion.53), custom_call_target="Cholesky" | custom-call | tf_op jit(solution)/shard_map/jit(cholesky)/cholesky | solution.py:149
  270.7 6.0 %convolution_bitcast_fusion = f32[4,8,64,128]{3,1,2,0:T(8,128)S(1)} fusion(f32[32,32]{1,0:T(8,128)S(1)} %convolution_multiply_fusion, f32[8192,32]{1,0:T(8,128)} %copy-done), kind=kOutput, calls=%fused_computation.17 | convolution fusion | flops 100663296 | bytes 2101248 | tf_op jit(solution)/shard_map/dot_general | solution.py:226
  (86 shorter events, 49.9 us)
Async XLA Ops:
  0.0 3.6 %copy-start.5 = (s32[64,128]{1,0:T(8,128)S(1)}, s32[64,128]{1,0:T(8,128)}, u32[]{:S(2)}) copy-start(s32[64,128]{1,0:T(8,128)} %param.10) | copy-start | bytes 98308
  0.0 3.6 %copy-start.4 = (s32[64,128]{1,0:T(8,128)S(1)}, s32[64,128]{1,0:T(8,128)}, u32[]{:S(2)}) copy-start(s32[64,128]{1,0:T(8,128)} %param.11) | copy-start | bytes 98308
  3.7 2.2 copy-start.2
  57.5 14.4 %collective-permute-start = (bf16[32,64,128]{2,0,1:T(8,128)(2,1)S(1)}, bf16[32,64,128]{2,0,1:T(8,128)(2,1)S(1)}, u32[]{:S(2)}, u32[]{:S(2)}) collective-permute-start(bf16[32,64,128]{2,0,1:T(8,128)(2,1)S(1)} %bitcast.106), channel_id=1, source_target_pairs={{0,32},{32,64},{64,96},{96,0},{1,33},{33,65},{65,97},{97,1},{2,34}... | collective-permute-start | bytes 1572872 | tf_op jit(solution)/shard_map/ppermute | solution.py:117
  58.2 13.8 %collective-permute-start.1 = (bf16[32,64,128]{2,0,1:T(8,128)(2,1)S(1)}, bf16[32,64,128]{2,0,1:T(8,128)(2,1)S(1)}, u32[]{:S(2)}, u32[]{:S(2)}) collective-permute-start(bf16[32,64,128]{2,0,1:T(8,128)(2,1)S(1)} %bitcast.107), channel_id=1, source_target_pairs={{0,96},{32,0},{64,32},{96,64},{1,97},{33,1},{65,33},{97,65},{2,98}... | collective-permute-start | bytes 1572872 | tf_op jit(solution)/shard_map/ppermute | solution.py:117
  72.0 7.9 %collective-permute-start.2 = (bf16[16,64,128]{2,0,1:T(8,128)(2,1)S(1)}, bf16[16,64,128]{2,0,1:T(8,128)(2,1)S(1)}, u32[]{:S(2)}, u32[]{:S(2)}) collective-permute-start(bf16[16,64,128]{2,0,1:T(8,128)(2,1)S(1)} %slice.38), channel_id=1, source_target_pairs={{0,32},{32,64},{64,96},{96,0},{1,33},{33,65},{65,97},{97,1},{2,34}... | collective-permute-start | bytes 786440 | tf_op jit(solution)/shard_map/ppermute | solution.py:117
  72.1 7.8 %collective-permute-start.3 = (bf16[16,64,128]{2,0,1:T(8,128)(2,1)S(1)}, bf16[16,64,128]{2,0,1:T(8,128)(2,1)S(1)}, u32[]{:S(2)}, u32[]{:S(2)}) collective-permute-start(bf16[16,64,128]{2,0,1:T(8,128)(2,1)S(1)} %slice.39), channel_id=1, source_target_pairs={{0,96},{32,0},{64,32},{96,64},{1,97},{33,1},{65,33},{97,65},{2,98}... | collective-permute-start | bytes 786440 | tf_op jit(solution)/shard_map/ppermute | solution.py:117
  88.1 2.2 copy-start.3
  138.2 14.4 %collective-permute-start.4 = (bf16[32,64,128]{2,0,1:T(8,128)(2,1)S(1)}, bf16[32,64,128]{2,0,1:T(8,128)(2,1)S(1)}, u32[]{:S(2)}, u32[]{:S(2)}) collective-permute-start(bf16[32,64,128]{2,0,1:T(8,128)(2,1)S(1)} %bitcast.108), channel_id=1, source_target_pairs={{0,32},{32,64},{64,96},{96,0},{1,33},{33,65},{65,97},{97,1},{2,34}... | collective-permute-start | bytes 1572872 | tf_op jit(solution)/shard_map/ppermute | solution.py:117
  138.9 13.8 %collective-permute-start.5 = (bf16[32,64,128]{2,0,1:T(8,128)(2,1)S(1)}, bf16[32,64,128]{2,0,1:T(8,128)(2,1)S(1)}, u32[]{:S(2)}, u32[]{:S(2)}) collective-permute-start(bf16[32,64,128]{2,0,1:T(8,128)(2,1)S(1)} %bitcast.109), channel_id=1, source_target_pairs={{0,96},{32,0},{64,32},{96,64},{1,97},{33,1},{65,33},{97,65},{2,98}... | collective-permute-start | bytes 1572872 | tf_op jit(solution)/shard_map/ppermute | solution.py:117
  152.6 7.9 %collective-permute-start.6 = (bf16[16,64,128]{2,0,1:T(8,128)(2,1)S(1)}, bf16[16,64,128]{2,0,1:T(8,128)(2,1)S(1)}, u32[]{:S(2)}, u32[]{:S(2)}) collective-permute-start(bf16[16,64,128]{2,0,1:T(8,128)(2,1)S(1)} %slice.40), channel_id=1, source_target_pairs={{0,32},{32,64},{64,96},{96,0},{1,33},{33,65},{65,97},{97,1},{2,34}... | collective-permute-start | bytes 786440 | tf_op jit(solution)/shard_map/ppermute | solution.py:117
  152.8 7.8 %collective-permute-start.7 = (bf16[16,64,128]{2,0,1:T(8,128)(2,1)S(1)}, bf16[16,64,128]{2,0,1:T(8,128)(2,1)S(1)}, u32[]{:S(2)}, u32[]{:S(2)}) collective-permute-start(bf16[16,64,128]{2,0,1:T(8,128)(2,1)S(1)} %slice.41), channel_id=1, source_target_pairs={{0,96},{32,0},{64,32},{96,64},{1,97},{33,1},{65,33},{97,65},{2,98}... | collective-permute-start | bytes 786440 | tf_op jit(solution)/shard_map/ppermute | solution.py:117
  168.8 20.1 %copy-start.6 = (s32[32]{0:T(128)S(1)}, s32[32]{0:T(128)}, u32[]{:S(2)}) copy-start(s32[32]{0:T(128)} %param.12) | copy-start | bytes 388
  168.8 2.2 copy-start.1
  181.3 26.8 %all-to-all-start.2 = ((f32[128,16,128]{2,1,0:T(8,128)}), f32[128,16,128]{2,1,0:T(8,128)S(1)}, u32[]{:S(2)}, u32[]{:S(2)}) async-start(f32[128,16,128]{2,1,0:T(8,128)} %bitcast.15), calls=%async_computation.2 | async-start | bytes 2097152 | tf_op jit(solution)/shard_map/all_to_all | solution.py:107
  219.0 2.0 copy-start
  230.6 1.9 collective-permute-start.8
  230.7 4.1 %collective-permute-start.9 = (f32[32,64]{0,1:T(8,128)S(1)}, f32[32,64]{0,1:T(8,128)S(1)}, u32[]{:S(2)}, u32[]{:S(2)}) collective-permute-start(f32[32,64]{0,1:T(8,128)S(1)} %get-tuple-element.12), channel_id=1, source_target_pairs={{0,2},{1,3},{2,0},{3,1},{4,6},{5,7},{6,4},{7,5},{8,10},{9,11},{10,... | collective-permute-start | bytes 24584 | tf_op jit(solution)/shard_map/ppermute | solution.py:161
  231.0 3.8 %collective-permute-start.10 = (f32[32,64]{0,1:T(8,128)S(1)}, f32[32,64]{0,1:T(8,128)S(1)}, u32[]{:S(2)}, u32[]{:S(2)}) collective-permute-start(f32[32,64]{0,1:T(8,128)S(1)} %get-tuple-element.12), channel_id=1, source_target_pairs={{0,3},{1,2},{2,1},{3,0},{4,7},{5,6},{6,5},{7,4},{8,11},{9,10},{10,... | collective-permute-start | bytes 24584 | tf_op jit(solution)/shard_map/ppermute | solution.py:161
  234.9 5.5 %collective-permute-start.11 = (f32[32,64]{0,1:T(8,128)S(1)}, f32[32,64]{0,1:T(8,128)S(1)}, u32[]{:S(2)}, u32[]{:S(2)}) collective-permute-start(f32[32,64]{0,1:T(8,128)S(1)} %fusion.91), channel_id=1, source_target_pairs={{0,4},{1,5},{2,6},{3,7},{4,0},{5,1},{6,2},{7,3},{8,12},{9,13},{10,... | collective-permute-start | bytes 24584 | tf_op jit(solution)/shard_map/ppermute | solution.py:161
  236.0 4.4 %collective-permute-start.12 = (f32[32,64]{0,1:T(8,128)S(1)}, f32[32,64]{0,1:T(8,128)S(1)}, u32[]{:S(2)}, u32[]{:S(2)}) collective-permute-start(f32[32,64]{0,1:T(8,128)S(1)} %fusion.91), channel_id=1, source_target_pairs={{0,8},{1,9},{2,10},{3,11},{4,12},{5,13},{6,14},{7,15},{8,0},{9,1},... | collective-permute-start | bytes 24584 | tf_op jit(solution)/shard_map/ppermute | solution.py:161
  236.3 6.3 %collective-permute-start.13 = (f32[32,64]{0,1:T(8,128)S(1)}, f32[32,64]{0,1:T(8,128)S(1)}, u32[]{:S(2)}, u32[]{:S(2)}) collective-permute-start(f32[32,64]{0,1:T(8,128)S(1)} %fusion.91), channel_id=1, source_target_pairs={{0,12},{1,13},{2,14},{3,15},{4,8},{5,9},{6,10},{7,11},{8,4},{9,5},... | collective-permute-start | bytes 24584 | tf_op jit(solution)/shard_map/ppermute | solution.py:161
  242.7 5.5 %collective-permute-start.14 = (f32[32,64]{0,1:T(8,128)S(1)}, f32[32,64]{0,1:T(8,128)S(1)}, u32[]{:S(2)}, u32[]{:S(2)}) collective-permute-start(f32[32,64]{0,1:T(8,128)S(1)} %fusion.90), channel_id=1, source_target_pairs={{0,16},{1,17},{2,18},{3,19},{4,20},{5,21},{6,22},{7,23},{8,24},{9,... | collective-permute-start | bytes 24584 | tf_op jit(solution)/shard_map/ppermute | solution.py:161
  248.2 4.8 %collective-permute-start.15 = (f32[32,64]{0,1:T(8,128)S(1)}, f32[32,64]{0,1:T(8,128)S(1)}, u32[]{:S(2)}, u32[]{:S(2)}) collective-permute-start(f32[32,64]{0,1:T(8,128)S(1)} %bitcast.111), channel_id=1, source_target_pairs={{0,32},{32,0},{64,96},{96,64},{1,33},{33,1},{65,97},{97,65},{2,34}... | collective-permute-start | bytes 24584 | tf_op jit(solution)/shard_map/ppermute | solution.py:161
  249.0 5.4 %collective-permute-start.16 = (f32[32,64]{0,1:T(8,128)S(1)}, f32[32,64]{0,1:T(8,128)S(1)}, u32[]{:S(2)}, u32[]{:S(2)}) collective-permute-start(f32[32,64]{0,1:T(8,128)S(1)} %bitcast.112), channel_id=1, source_target_pairs={{0,64},{32,96},{64,0},{96,32},{1,65},{33,97},{65,1},{97,33},{2,66}... | collective-permute-start | bytes 24584 | tf_op jit(solution)/shard_map/ppermute | solution.py:161
  251.0 5.1 %collective-permute-start.17 = (f32[32,64]{0,1:T(8,128)S(1)}, f32[32,64]{0,1:T(8,128)S(1)}, u32[]{:S(2)}, u32[]{:S(2)}) collective-permute-start(f32[32,64]{0,1:T(8,128)S(1)} %bitcast.113), channel_id=1, source_target_pairs={{0,96},{32,64},{64,32},{96,0},{1,97},{33,65},{65,33},{97,1},{2,98}... | collective-permute-start | bytes 24584 | tf_op jit(solution)/shard_map/ppermute | solution.py:161

commit v7 on v6

--- a/solution.py
+++ b/solution.py
@@ -227,7 +227,7 @@
         coefficients,
         samples,
         (((1,), (1,)), ((), ())),
-        precision=lax.Precision.HIGHEST,
+        precision=lax.Precision.HIGH,
         preferred_element_type=jnp.float32,
     )
     return constraint_rows.reshape(sample_count, sub_local, group)

time: 279 us -> 277 us (level)
  no operation moved by 1% of the time
where the time goes in v7:
time: 277 us; the launch traced here: 276 us
  Pallas kernels  61.7 us (22%)
  blocking collectives  56.9 us (21%)
  waiting for transfers between devices  50.2 us (18%)
  starting transfers between devices  35.3 us (13%)
  matrix products  34.4 us (12%)
  local copies, waits for them, and re-layouts  23.4 us (8%)
  other arithmetic  14.1 us (5%)
    all_to_all x2, blocking collectives, exchange(): lax.all_to_all(outgoing, ('iface', 'sub'), split_axis=0, concat_axis=0, t...  56.9 us
    pallas_call x3, Pallas kernels, unpack_jump(): pl.pallas_call(functools.partial(_unpack_kernel, first, count), in_specs=...  32.8 us
    pallas_call x3, Pallas kernels, pack_rows(): pl.pallas_call(_pack_kernel, in_specs=[pl.BlockSpec(memory_space=pltpu.SM...  28.9 us
    dot_general x8, matrix products, product(): jnp.einsum('src,ksc->srk', columns, block, preferred_element_type=jnp.flo...  22.3 us
    ppermute x8, waiting for transfers between devices, shifted(): lax.ppermute(value, 'iface', [(i, (i + shift) % ring) for i in range(ring)])  20.1 us
    all_to_all x1, waiting for transfers between devices, exchange(): lax.all_to_all(outgoing, ('iface', 'sub'), split_axis=0, concat_axis=0, t...  19.1 us
    ppermute x10, starting transfers between devices, group_sum(): lax.ppermute(x, axis, [(i, i ^ m * bit) for i in range(size)])  14.3 us
    ppermute x8, starting transfers between devices, shifted(): lax.ppermute(value, 'iface', [(i, (i + shift) % ring) for i in range(ring)])  13.3 us
  transfers between devices with their start and end apart: 19, of which 11 were waited for; matrix products, arithmetic and copies ran while one was open for 4% of the time, Pallas kernels for 0%

profile of v7, /device:TPU:0, one launch (start us, length us, event | category | flops | bytes accessed | tf_op | source)
XLA Modules:
  0.0 276.2 jit_solution(9975400903878087705)
XLA Ops:
  0.0 3.6 %copy.6 = f32[64,128,32]{2,1,0:T(8,128)} copy(f32[64,128,32]{1,0,2:T(8,128)} %bitcast.110) | data formatting | bytes 2097152 | tf_op jit(solution)/shard_map/transpose | solution.py:198
  5.9 9.3 %shard_map.55 = f32[2048,128]{1,0:T(8,128)S(1)} custom-call(s32[8192]{0:T(1024)S(1)} %get-tuple-element.9.slot_ref, f32[8192,32]{1,0:T(8,128)S(1)} %bitcast.96), custom_call_target="tpu_custom_call" | custom-call | tf_op jit(solution)/shard_map/pallas_call | solution.py:77
  15.2 30.3 %all_to_all.33 = f32[128,16,128]{2,1,0:T(8,128)S(1)} all-to-all(f32[128,16,128]{2,1,0:T(8,128)S(1)} %bitcast.102), channel_id=1, replica_groups=mesh['iface'=4,'sub'=32] {'iface','sub'}, dimensions={0} | all-to-all | bytes 2097152 | tf_op jit(solution)/shard_map/all_to_all | solution.py:107
  45.5 10.9 %shard_map.56 = f32[8192,32]{1,0:T(8,128)S(1)} custom-call(s32[8192]{0:T(1024)S(1)} %get-tuple-element.10.src_ref, f32[8192,32]{1,0:T(8,128)} %bitcast.95, f32[2048,128]{1,0:T(8,128)S(1)} %bitcast.100), custom_call_target="tpu_custom_call" | custom-call | tf_op jit(solution)/shard_map/pallas_call | solution.py:91
  60.9 2.8 %fusion.14 = f32[64,128,32]{1,2,0:T(8,128)S(1)} fusion(bf16[64,128,512]{2,1,0:T(8,128)(2,1)} %param.8, s32[]{:T(128)S(6)} %select_n.141, bf16[64,128,32]{1,2,0:T(8,128)(2,1)S(1)} %copy.7), kind=kOutput, calls=%fused_computation.15 | convolution fusion | flops 67108864 | bytes 3670020 | tf_op jit(solution)/shard_map/src,ksc->srk/dot_general | solution.py:121
  63.6 8.3 %collective-permute-done = bf16[32,64,128]{2,0,1:T(8,128)(2,1)S(1)} collective-permute-done((bf16[32,64,128]{2,0,1:T(8,128)(2,1)S(1)}, bf16[32,64,128]{2,0,1:T(8,128)(2,1)S(1)}, u32[]{:S(2)}, u32[]{:S(2)}) %collective-permute-start) | collective-permute-done | bytes 524320 | tf_op jit(solution)/shard_map/ppermute | solution.py:117
  72.1 3.3 %collective-permute-start.3 = (bf16[16,64,128]{2,0,1:T(8,128)(2,1)S(1)}, bf16[16,64,128]{2,0,1:T(8,128)(2,1)S(1)}, u32[]{:S(2)}, u32[]{:S(2)}) collective-permute-start(bf16[16,64,128]{2,0,1:T(8,128)(2,1)S(1)} %slice.39), channel_id=1, source_target_pairs={{0,96},{32,0},{64,32},{96,64},{1,97},{33,1},{65,33},{97,65},{2,98}... | collective-permute-start | bytes 786440 | tf_op jit(solution)/shard_map/ppermute | solution.py:117
  75.4 2.8 %fusion.6 = f32[64,128,32]{1,2,0:T(8,128)S(1)} fusion(bf16[32,64,128]{2,0,1:T(8,128)(2,1)S(1)} %collective-permute-done.1, bf16[64,128,512]{2,1,0:T(8,128)(2,1)} %param.8, s32[]{:T(128)S(6)} %select_n.146), kind=kOutput, calls=%fused_computation.7 | convolution fusion | flops 67108864 | bytes 3670020 | tf_op jit(solution)/shard_map/src,ksc->srk/dot_general | solution.py:121
  79.9 2.8 %fusion.2 = f32[64,128,32]{1,2,0:T(8,128)S(1)} fusion(bf16[64,128,512]{2,1,0:T(8,128)(2,1)} %param.8, s32[]{:T(128)S(6)} %select_n.148, bf16[16,64,128]{2,0,1:T(8,128)(2,1)S(1)} %collective-permute-done.3, bf16[16,64,128]{2,0,1:T(8,128)(2,1)S(1)} %collective-permute-done.2), kind=kOutput, calls=%fused_computation.3 | convolution fusion | flops 68157440 | bytes 3670020 | tf_op jit(solution)/shard_map/src,ksc->srk/dot_general | solution.py:121
  82.7 2.8 %fusion.31 = f32[64,128,32]{1,2,0:T(8,128)S(1)} fusion(f32[64,128,32]{1,2,0:T(8,128)S(1)} %fusion.2, f32[64,128,32]{1,2,0:T(8,128)S(1)} %fusion.6, f32[64,128,32]{1,2,0:T(8,128)S(1)} %fusion.14, bf16[32,64,128]{2,0,1:T(8,128)(2,1)S(1)} %collective-permute-done, bf16[64,128,512]{2,1,0:T(8,128)(2,1)} %param.8, s32[]{:T(128)S(6)} %select_n.144), kind=kOutput, calls=%fused_computation.23 | convolution fusion | flops 67895296 | bytes 6815748 | tf_op jit(solution)/shard_map/src,ksc->srk/dot_general | solution.py:121
  85.5 2.7 copy.8
  90.3 9.3 %shard_map.57 = f32[2048,128]{1,0:T(8,128)S(1)} custom-call(s32[8192]{0:T(1024)S(1)} %get-tuple-element.9.slot_ref, f32[8192,32]{1,0:T(8,128)S(1)} %bitcast.98), custom_call_target="tpu_custom_call" | custom-call | tf_op jit(solution)/shard_map/pallas_call | solution.py:77
  99.6 26.6 %all_to_all.34 = f32[128,16,128]{2,1,0:T(8,128)S(1)} all-to-all(f32[128,16,128]{2,1,0:T(8,128)S(1)} %bitcast.103), channel_id=1, replica_groups=mesh['iface'=4,'sub'=32] {'iface','sub'}, dimensions={0} | all-to-all | bytes 2097152 | tf_op jit(solution)/shard_map/all_to_all | solution.py:107
  126.2 10.9 %shard_map.58 = f32[8192,32]{1,0:T(8,128)S(1)} custom-call(s32[8192]{0:T(1024)S(1)} %get-tuple-element.10.src_ref, f32[8192,32]{1,0:T(8,128)} %bitcast.97, f32[2048,128]{1,0:T(8,128)S(1)} %bitcast.101), custom_call_target="tpu_custom_call" | custom-call | tf_op jit(solution)/shard_map/pallas_call | solution.py:91
  141.5 2.8 %fusion.12 = f32[64,128,32]{1,2,0:T(8,128)S(1)} fusion(bf16[64,128,512]{2,1,0:T(8,128)(2,1)} %param.8, s32[]{:T(128)S(6)} %select_n.141, bf16[64,128,32]{1,2,0:T(8,128)(2,1)S(1)} %copy.9), kind=kOutput, calls=%fused_computation.13 | convolution fusion | flops 67108864 | bytes 3670020 | tf_op jit(solution)/shard_map/src,ksc->srk/dot_general | solution.py:121
  144.3 8.3 %collective-permute-done.4 = bf16[32,64,128]{2,0,1:T(8,128)(2,1)S(1)} collective-permute-done((bf16[32,64,128]{2,0,1:T(8,128)(2,1)S(1)}, bf16[32,64,128]{2,0,1:T(8,128)(2,1)S(1)}, u32[]{:S(2)}, u32[]{:S(2)}) %collective-permute-start.4) | collective-permute-done | bytes 524320 | tf_op jit(solution)/shard_map/ppermute | solution.py:117
  152.8 3.3 %collective-permute-start.7 = (bf16[16,64,128]{2,0,1:T(8,128)(2,1)S(1)}, bf16[16,64,128]{2,0,1:T(8,128)(2,1)S(1)}, u32[]{:S(2)}, u32[]{:S(2)}) collective-permute-start(bf16[16,64,128]{2,0,1:T(8,128)(2,1)S(1)} %slice.41), channel_id=1, source_target_pairs={{0,96},{32,0},{64,32},{96,64},{1,97},{33,1},{65,33},{97,65},{2,98}... | collective-permute-start | bytes 786440 | tf_op jit(solution)/shard_map/ppermute | solution.py:117
  156.1 2.8 %fusion.4 = f32[64,128,32]{1,2,0:T(8,128)S(1)} fusion(bf16[32,64,128]{2,0,1:T(8,128)(2,1)S(1)} %collective-permute-done.5, bf16[64,128,512]{2,1,0:T(8,128)(2,1)} %param.8, s32[]{:T(128)S(6)} %select_n.146), kind=kOutput, calls=%fused_computation.5 | convolution fusion | flops 67108864 | bytes 3670020 | tf_op jit(solution)/shard_map/src,ksc->srk/dot_general | solution.py:121
  160.6 2.8 %fusion = f32[64,128,32]{1,2,0:T(8,128)S(1)} fusion(bf16[64,128,512]{2,1,0:T(8,128)(2,1)} %param.8, s32[]{:T(128)S(6)} %select_n.148, bf16[16,64,128]{2,0,1:T(8,128)(2,1)S(1)} %collective-permute-done.7, bf16[16,64,128]{2,0,1:T(8,128)(2,1)S(1)} %collective-permute-done.6), kind=kOutput, calls=%fused_computation.1 | convolution fusion | flops 68157440 | bytes 3670020 | tf_op jit(solution)/shard_map/src,ksc->srk/dot_general | solution.py:121
  163.3 2.8 %fusion.28 = f32[64,128,32]{1,2,0:T(8,128)S(1)} fusion(f32[64,128,32]{1,2,0:T(8,128)S(1)} %fusion, f32[64,128,32]{1,2,0:T(8,128)S(1)} %fusion.4, f32[64,128,32]{1,2,0:T(8,128)S(1)} %fusion.12, bf16[32,64,128]{2,0,1:T(8,128)(2,1)S(1)} %collective-permute-done.4, bf16[64,128,512]{2,1,0:T(8,128)(2,1)} %param.8, s32[]{:T(128)S(6)} %select_n.144), kind=kOutput, calls=%fused_computation.22 | convolution fusion | flops 67895296 | bytes 6815748 | tf_op jit(solution)/shard_map/src,ksc->srk/dot_general | solution.py:121
  166.2 2.7 copy.10
  171.0 10.3 %shard_map.59 = f32[2048,128]{1,0:T(8,128)} custom-call(s32[8192]{0:T(1024)S(1)} %get-tuple-element.9.slot_ref, f32[8192,32]{1,0:T(8,128)S(1)} %bitcast.94), custom_call_target="tpu_custom_call" | custom-call | tf_op jit(solution)/shard_map/pallas_call | solution.py:77
  181.3 7.6 %all-to-all-start.2 = ((f32[128,16,128]{2,1,0:T(8,128)}), f32[128,16,128]{2,1,0:T(8,128)S(1)}, u32[]{:S(2)}, u32[]{:S(2)}) async-start(f32[128,16,128]{2,1,0:T(8,128)} %bitcast.15), calls=%async_computation.2 | async-start | bytes 2097152 | tf_op jit(solution)/shard_map/all_to_all | solution.py:107
  189.0 19.1 %all-to-all-done.2 = f32[128,16,128]{2,1,0:T(8,128)S(1)} async-done(((f32[128,16,128]{2,1,0:T(8,128)}), f32[128,16,128]{2,1,0:T(8,128)S(1)}, u32[]{:S(2)}, u32[]{:S(2)}) %all-to-all-start.2) | async-done | bytes 1048608 | tf_op jit(solution)/shard_map/all_to_all | solution.py:107
  208.1 10.9 %shard_map.60 = f32[8192,32]{1,0:T(8,128)S(1)} custom-call(s32[8192]{0:T(1024)S(1)} %get-tuple-element.10.src_ref, f32[8192,32]{1,0:T(8,128)} %bitcast.93, f32[2048,128]{1,0:T(8,128)S(1)} %bitcast.99), custom_call_target="tpu_custom_call" | custom-call | tf_op jit(solution)/shard_map/pallas_call | solution.py:91
  221.0 6.7 %fusion.78 = f32[32,32]{0,1:T(8,128)S(1)} fusion(f32[8192,32]{1,0:T(8,128)S(1)} %shard_map.60), kind=kOutput, calls=%fused_computation.113 | convolution fusion | flops 100663296 | bytes 1052672 | tf_op jit(solution)/shard_map/dot_general | solution.py:206
  227.7 2.8 %gather_fusion = f32[32,32]{1,0:T(8,128)S(1)} fusion(f32[8192,32]{1,0:T(8,128)} %copy-done, s32[1024]{0:T(1024)S(1)} %pad_clamp_fusion), kind=kCustom, calls=%fused_computation | custom fusion | bytes 8320 | tf_op jit(solution)/shard_map/jit(_take)/gather | solution.py:217
  236.3 3.6 %collective-permute-start.13 = (f32[32,64]{0,1:T(8,128)S(1)}, f32[32,64]{0,1:T(8,128)S(1)}, u32[]{:S(2)}, u32[]{:S(2)}) collective-permute-start(f32[32,64]{0,1:T(8,128)S(1)} %fusion.91), channel_id=1, source_target_pairs={{0,12},{1,13},{2,14},{3,15},{4,8},{5,9},{6,10},{7,11},{8,4},{9,5},... | collective-permute-start | bytes 24584 | tf_op jit(solution)/shard_map/ppermute | solution.py:161
  245.2 3.0 %collective-permute-done.14 = f32[32,64]{0,1:T(8,128)S(1)} collective-permute-done((f32[32,64]{0,1:T(8,128)S(1)}, f32[32,64]{0,1:T(8,128)S(1)}, u32[]{:S(2)}, u32[]{:S(2)}) %collective-permute-start.14) | collective-permute-done | bytes 8224 | tf_op jit(solution)/shard_map/ppermute | solution.py:161
  256.2 2.9 %cholesky.44 = f32[32,32]{1,0:T(8,128)S(1)} custom-call(f32[32,32]{1,0:T(8,128)S(1)} %fusion.58), custom_call_target="Cholesky" | custom-call | tf_op jit(solution)/shard_map/jit(cholesky)/cholesky | solution.py:144
  263.6 2.9 %cholesky.55 = f32[32,32]{1,0:T(8,128)S(1)} custom-call(f32[32,32]{1,0:T(8,128)S(1)} %fusion.53), custom_call_target="Cholesky" | custom-call | tf_op jit(solution)/shard_map/jit(cholesky)/cholesky | solution.py:149
  270.7 4.3 %convolution_bitcast_fusion = f32[4,8,64,128]{3,1,2,0:T(8,128)S(1)} fusion(f32[32,32]{1,0:T(8,128)S(1)} %convolution_multiply_fusion, f32[8192,32]{1,0:T(8,128)} %copy-done), kind=kOutput, calls=%fused_computation.17 | convolution fusion | flops 50331648 | bytes 2101248 | tf_op jit(solution)/shard_map/dot_general | solution.py:226
  (86 shorter events, 49.9 us)
Async XLA Ops:
  0.0 3.6 %copy-start.5 = (s32[64,128]{1,0:T(8,128)S(1)}, s32[64,128]{1,0:T(8,128)}, u32[]{:S(2)}) copy-start(s32[64,128]{1,0:T(8,128)} %param.10) | copy-start | bytes 98308
  0.0 3.6 %copy-start.4 = (s32[64,128]{1,0:T(8,128)S(1)}, s32[64,128]{1,0:T(8,128)}, u32[]{:S(2)}) copy-start(s32[64,128]{1,0:T(8,128)} %param.11) | copy-start | bytes 98308
  3.7 2.2 copy-start.2
  57.5 14.4 %collective-permute-start = (bf16[32,64,128]{2,0,1:T(8,128)(2,1)S(1)}, bf16[32,64,128]{2,0,1:T(8,128)(2,1)S(1)}, u32[]{:S(2)}, u32[]{:S(2)}) collective-permute-start(bf16[32,64,128]{2,0,1:T(8,128)(2,1)S(1)} %bitcast.106), channel_id=1, source_target_pairs={{0,32},{32,64},{64,96},{96,0},{1,33},{33,65},{65,97},{97,1},{2,34}... | collective-permute-start | bytes 1572872 | tf_op jit(solution)/shard_map/ppermute | solution.py:117
  58.2 13.8 %collective-permute-start.1 = (bf16[32,64,128]{2,0,1:T(8,128)(2,1)S(1)}, bf16[32,64,128]{2,0,1:T(8,128)(2,1)S(1)}, u32[]{:S(2)}, u32[]{:S(2)}) collective-permute-start(bf16[32,64,128]{2,0,1:T(8,128)(2,1)S(1)} %bitcast.107), channel_id=1, source_target_pairs={{0,96},{32,0},{64,32},{96,64},{1,97},{33,1},{65,33},{97,65},{2,98}... | collective-permute-start | bytes 1572872 | tf_op jit(solution)/shard_map/ppermute | solution.py:117
  72.0 7.9 %collective-permute-start.2 = (bf16[16,64,128]{2,0,1:T(8,128)(2,1)S(1)}, bf16[16,64,128]{2,0,1:T(8,128)(2,1)S(1)}, u32[]{:S(2)}, u32[]{:S(2)}) collective-permute-start(bf16[16,64,128]{2,0,1:T(8,128)(2,1)S(1)} %slice.38), channel_id=1, source_target_pairs={{0,32},{32,64},{64,96},{96,0},{1,33},{33,65},{65,97},{97,1},{2,34}... | collective-permute-start | bytes 786440 | tf_op jit(solution)/shard_map/ppermute | solution.py:117
  72.1 7.8 %collective-permute-start.3 = (bf16[16,64,128]{2,0,1:T(8,128)(2,1)S(1)}, bf16[16,64,128]{2,0,1:T(8,128)(2,1)S(1)}, u32[]{:S(2)}, u32[]{:S(2)}) collective-permute-start(bf16[16,64,128]{2,0,1:T(8,128)(2,1)S(1)} %slice.39), channel_id=1, source_target_pairs={{0,96},{32,0},{64,32},{96,64},{1,97},{33,1},{65,33},{97,65},{2,98}... | collective-permute-start | bytes 786440 | tf_op jit(solution)/shard_map/ppermute | solution.py:117
  88.1 2.2 copy-start.3
  138.2 14.4 %collective-permute-start.4 = (bf16[32,64,128]{2,0,1:T(8,128)(2,1)S(1)}, bf16[32,64,128]{2,0,1:T(8,128)(2,1)S(1)}, u32[]{:S(2)}, u32[]{:S(2)}) collective-permute-start(bf16[32,64,128]{2,0,1:T(8,128)(2,1)S(1)} %bitcast.108), channel_id=1, source_target_pairs={{0,32},{32,64},{64,96},{96,0},{1,33},{33,65},{65,97},{97,1},{2,34}... | collective-permute-start | bytes 1572872 | tf_op jit(solution)/shard_map/ppermute | solution.py:117
  138.9 13.8 %collective-permute-start.5 = (bf16[32,64,128]{2,0,1:T(8,128)(2,1)S(1)}, bf16[32,64,128]{2,0,1:T(8,128)(2,1)S(1)}, u32[]{:S(2)}, u32[]{:S(2)}) collective-permute-start(bf16[32,64,128]{2,0,1:T(8,128)(2,1)S(1)} %bitcast.109), channel_id=1, source_target_pairs={{0,96},{32,0},{64,32},{96,64},{1,97},{33,1},{65,33},{97,65},{2,98}... | collective-permute-start | bytes 1572872 | tf_op jit(solution)/shard_map/ppermute | solution.py:117
  152.6 7.9 %collective-permute-start.6 = (bf16[16,64,128]{2,0,1:T(8,128)(2,1)S(1)}, bf16[16,64,128]{2,0,1:T(8,128)(2,1)S(1)}, u32[]{:S(2)}, u32[]{:S(2)}) collective-permute-start(bf16[16,64,128]{2,0,1:T(8,128)(2,1)S(1)} %slice.40), channel_id=1, source_target_pairs={{0,32},{32,64},{64,96},{96,0},{1,33},{33,65},{65,97},{97,1},{2,34}... | collective-permute-start | bytes 786440 | tf_op jit(solution)/shard_map/ppermute | solution.py:117
  152.8 7.8 %collective-permute-start.7 = (bf16[16,64,128]{2,0,1:T(8,128)(2,1)S(1)}, bf16[16,64,128]{2,0,1:T(8,128)(2,1)S(1)}, u32[]{:S(2)}, u32[]{:S(2)}) collective-permute-start(bf16[16,64,128]{2,0,1:T(8,128)(2,1)S(1)} %slice.41), channel_id=1, source_target_pairs={{0,96},{32,0},{64,32},{96,64},{1,97},{33,1},{65,33},{97,65},{2,98}... | collective-permute-start | bytes 786440 | tf_op jit(solution)/shard_map/ppermute | solution.py:117
  168.8 20.1 %copy-start.6 = (s32[32]{0:T(128)S(1)}, s32[32]{0:T(128)}, u32[]{:S(2)}) copy-start(s32[32]{0:T(128)} %param.12) | copy-start | bytes 388
  168.8 2.2 copy-start.1
  181.3 26.8 %all-to-all-start.2 = ((f32[128,16,128]{2,1,0:T(8,128)}), f32[128,16,128]{2,1,0:T(8,128)S(1)}, u32[]{:S(2)}, u32[]{:S(2)}) async-start(f32[128,16,128]{2,1,0:T(8,128)} %bitcast.15), calls=%async_computation.2 | async-start | bytes 2097152 | tf_op jit(solution)/shard_map/all_to_all | solution.py:107
  219.0 2.0 copy-start
  230.6 1.9 collective-permute-start.8
  230.7 4.1 %collective-permute-start.9 = (f32[32,64]{0,1:T(8,128)S(1)}, f32[32,64]{0,1:T(8,128)S(1)}, u32[]{:S(2)}, u32[]{:S(2)}) collective-permute-start(f32[32,64]{0,1:T(8,128)S(1)} %get-tuple-element.12), channel_id=1, source_target_pairs={{0,2},{1,3},{2,0},{3,1},{4,6},{5,7},{6,4},{7,5},{8,10},{9,11},{10,... | collective-permute-start | bytes 24584 | tf_op jit(solution)/shard_map/ppermute | solution.py:161
  231.0 3.8 %collective-permute-start.10 = (f32[32,64]{0,1:T(8,128)S(1)}, f32[32,64]{0,1:T(8,128)S(1)}, u32[]{:S(2)}, u32[]{:S(2)}) collective-permute-start(f32[32,64]{0,1:T(8,128)S(1)} %get-tuple-element.12), channel_id=1, source_target_pairs={{0,3},{1,2},{2,1},{3,0},{4,7},{5,6},{6,5},{7,4},{8,11},{9,10},{10,... | collective-permute-start | bytes 24584 | tf_op jit(solution)/shard_map/ppermute | solution.py:161
  234.9 5.5 %collective-permute-start.11 = (f32[32,64]{0,1:T(8,128)S(1)}, f32[32,64]{0,1:T(8,128)S(1)}, u32[]{:S(2)}, u32[]{:S(2)}) collective-permute-start(f32[32,64]{0,1:T(8,128)S(1)} %fusion.91), channel_id=1, source_target_pairs={{0,4},{1,5},{2,6},{3,7},{4,0},{5,1},{6,2},{7,3},{8,12},{9,13},{10,... | collective-permute-start | bytes 24584 | tf_op jit(solution)/shard_map/ppermute | solution.py:161
  236.0 4.4 %collective-permute-start.12 = (f32[32,64]{0,1:T(8,128)S(1)}, f32[32,64]{0,1:T(8,128)S(1)}, u32[]{:S(2)}, u32[]{:S(2)}) collective-permute-start(f32[32,64]{0,1:T(8,128)S(1)} %fusion.91), channel_id=1, source_target_pairs={{0,8},{1,9},{2,10},{3,11},{4,12},{5,13},{6,14},{7,15},{8,0},{9,1},... | collective-permute-start | bytes 24584 | tf_op jit(solution)/shard_map/ppermute | solution.py:161
  236.3 6.3 %collective-permute-start.13 = (f32[32,64]{0,1:T(8,128)S(1)}, f32[32,64]{0,1:T(8,128)S(1)}, u32[]{:S(2)}, u32[]{:S(2)}) collective-permute-start(f32[32,64]{0,1:T(8,128)S(1)} %fusion.91), channel_id=1, source_target_pairs={{0,12},{1,13},{2,14},{3,15},{4,8},{5,9},{6,10},{7,11},{8,4},{9,5},... | collective-permute-start | bytes 24584 | tf_op jit(solution)/shard_map/ppermute | solution.py:161
  242.7 5.5 %collective-permute-start.14 = (f32[32,64]{0,1:T(8,128)S(1)}, f32[32,64]{0,1:T(8,128)S(1)}, u32[]{:S(2)}, u32[]{:S(2)}) collective-permute-start(f32[32,64]{0,1:T(8,128)S(1)} %fusion.90), channel_id=1, source_target_pairs={{0,16},{1,17},{2,18},{3,19},{4,20},{5,21},{6,22},{7,23},{8,24},{9,... | collective-permute-start | bytes 24584 | tf_op jit(solution)/shard_map/ppermute | solution.py:161
  248.2 4.8 %collective-permute-start.15 = (f32[32,64]{0,1:T(8,128)S(1)}, f32[32,64]{0,1:T(8,128)S(1)}, u32[]{:S(2)}, u32[]{:S(2)}) collective-permute-start(f32[32,64]{0,1:T(8,128)S(1)} %bitcast.111), channel_id=1, source_target_pairs={{0,32},{32,0},{64,96},{96,64},{1,33},{33,1},{65,97},{97,65},{2,34}... | collective-permute-start | bytes 24584 | tf_op jit(solution)/shard_map/ppermute | solution.py:161
  249.0 5.4 %collective-permute-start.16 = (f32[32,64]{0,1:T(8,128)S(1)}, f32[32,64]{0,1:T(8,128)S(1)}, u32[]{:S(2)}, u32[]{:S(2)}) collective-permute-start(f32[32,64]{0,1:T(8,128)S(1)} %bitcast.112), channel_id=1, source_target_pairs={{0,64},{32,96},{64,0},{96,32},{1,65},{33,97},{65,1},{97,33},{2,66}... | collective-permute-start | bytes 24584 | tf_op jit(solution)/shard_map/ppermute | solution.py:161
  251.0 5.1 %collective-permute-start.17 = (f32[32,64]{0,1:T(8,128)S(1)}, f32[32,64]{0,1:T(8,128)S(1)}, u32[]{:S(2)}, u32[]{:S(2)}) collective-permute-start(f32[32,64]{0,1:T(8,128)S(1)} %bitcast.113), channel_id=1, source_target_pairs={{0,96},{32,64},{64,32},{96,0},{1,97},{33,65},{65,33},{97,1},{2,98}... | collective-permute-start | bytes 24584 | tf_op jit(solution)/shard_map/ppermute | solution.py:161

commit v8 on v7

--- a/solution.py
+++ b/solution.py
@@ -8,7 +8,7 @@
 from jax.experimental.pallas import tpu as pltpu
 from jax.sharding import PartitionSpec as P
 
-UNROLL = 64
+UNROLL = 128
 
 
 def _pack_kernel(slot_ref, *refs):

time: 277 us -> 275 us (level)
  no operation moved by 1% of the time
where the time goes in v8:
time: 275 us; the launch traced here: 274 us
  Pallas kernels  60 us (22%)
  blocking collectives  56.9 us (21%)
  waiting for transfers between devices  50.2 us (18%)
  starting transfers between devices  35.3 us (13%)
  matrix products  34.4 us (13%)
  local copies, waits for them, and re-layouts  23.4 us (9%)
  other arithmetic  14.1 us (5%)
    all_to_all x2, blocking collectives, exchange(): lax.all_to_all(outgoing, ('iface', 'sub'), split_axis=0, concat_axis=0, t...  56.9 us
    pallas_call x3, Pallas kernels, unpack_jump(): pl.pallas_call(functools.partial(_unpack_kernel, first, count), in_specs=...  32 us
    pallas_call x3, Pallas kernels, pack_rows(): pl.pallas_call(_pack_kernel, in_specs=[pl.BlockSpec(memory_space=pltpu.SM...  28 us
    dot_general x8, matrix products, product(): jnp.einsum('src,ksc->srk', columns, block, preferred_element_type=jnp.flo...  22.3 us
    ppermute x8, waiting for transfers between devices, shifted(): lax.ppermute(value, 'iface', [(i, (i + shift) % ring) for i in range(ring)])  20.1 us
    all_to_all x1, waiting for transfers between devices, exchange(): lax.all_to_all(outgoing, ('iface', 'sub'), split_axis=0, concat_axis=0, t...  19.1 us
    ppermute x10, starting transfers between devices, group_sum(): lax.ppermute(x, axis, [(i, i ^ m * bit) for i in range(size)])  14.3 us
    ppermute x8, starting transfers between devices, shifted(): lax.ppermute(value, 'iface', [(i, (i + shift) % ring) for i in range(ring)])  13.3 us
  transfers between devices with their start and end apart: 19, of which 11 were waited for; matrix products, arithmetic and copies ran while one was open for 4% of the time, Pallas kernels for 0%

profile of v8, /device:TPU:0, one launch (start us, length us, event | category | flops | bytes accessed | tf_op | source)
XLA Modules:
  0.0 274.5 jit_solution(10733885824309075773)
XLA Ops:
  0.0 3.6 %copy.6 = f32[64,128,32]{2,1,0:T(8,128)} copy(f32[64,128,32]{1,0,2:T(8,128)} %bitcast.110) | data formatting | bytes 2097152 | tf_op jit(solution)/shard_map/transpose | solution.py:198
  5.9 9.0 %shard_map.55 = f32[2048,128]{1,0:T(8,128)S(1)} custom-call(s32[8192]{0:T(1024)S(1)} %get-tuple-element.9.slot_ref, f32[8192,32]{1,0:T(8,128)S(1)} %bitcast.96), custom_call_target="tpu_custom_call" | custom-call | tf_op jit(solution)/shard_map/pallas_call | solution.py:77
  14.9 30.3 %all_to_all.33 = f32[128,16,128]{2,1,0:T(8,128)S(1)} all-to-all(f32[128,16,128]{2,1,0:T(8,128)S(1)} %bitcast.102), channel_id=1, replica_groups=mesh['iface'=4,'sub'=32] {'iface','sub'}, dimensions={0} | all-to-all | bytes 2097152 | tf_op jit(solution)/shard_map/all_to_all | solution.py:107
  45.2 10.7 %shard_map.56 = f32[8192,32]{1,0:T(8,128)S(1)} custom-call(s32[8192]{0:T(1024)S(1)} %get-tuple-element.10.src_ref, f32[8192,32]{1,0:T(8,128)} %bitcast.95, f32[2048,128]{1,0:T(8,128)S(1)} %bitcast.100), custom_call_target="tpu_custom_call" | custom-call | tf_op jit(solution)/shard_map/pallas_call | solution.py:91
  60.3 2.8 %fusion.14 = f32[64,128,32]{1,2,0:T(8,128)S(1)} fusion(bf16[64,128,512]{2,1,0:T(8,128)(2,1)} %param.8, s32[]{:T(128)S(6)} %select_n.141, bf16[64,128,32]{1,2,0:T(8,128)(2,1)S(1)} %copy.7), kind=kOutput, calls=%fused_computation.15 | convolution fusion | flops 67108864 | bytes 3670020 | tf_op jit(solution)/shard_map/src,ksc->srk/dot_general | solution.py:121
  63.1 8.3 %collective-permute-done = bf16[32,64,128]{2,0,1:T(8,128)(2,1)S(1)} collective-permute-done((bf16[32,64,128]{2,0,1:T(8,128)(2,1)S(1)}, bf16[32,64,128]{2,0,1:T(8,128)(2,1)S(1)}, u32[]{:S(2)}, u32[]{:S(2)}) %collective-permute-start) | collective-permute-done | bytes 524320 | tf_op jit(solution)/shard_map/ppermute | solution.py:117
  71.5 3.3 %collective-permute-start.3 = (bf16[16,64,128]{2,0,1:T(8,128)(2,1)S(1)}, bf16[16,64,128]{2,0,1:T(8,128)(2,1)S(1)}, u32[]{:S(2)}, u32[]{:S(2)}) collective-permute-start(bf16[16,64,128]{2,0,1:T(8,128)(2,1)S(1)} %slice.39), channel_id=1, source_target_pairs={{0,96},{32,0},{64,32},{96,64},{1,97},{33,1},{65,33},{97,65},{2,98}... | collective-permute-start | bytes 786440 | tf_op jit(solution)/shard_map/ppermute | solution.py:117
  74.8 2.8 %fusion.6 = f32[64,128,32]{1,2,0:T(8,128)S(1)} fusion(bf16[32,64,128]{2,0,1:T(8,128)(2,1)S(1)} %collective-permute-done.1, bf16[64,128,512]{2,1,0:T(8,128)(2,1)} %param.8, s32[]{:T(128)S(6)} %select_n.146), kind=kOutput, calls=%fused_computation.7 | convolution fusion | flops 67108864 | bytes 3670020 | tf_op jit(solution)/shard_map/src,ksc->srk/dot_general | solution.py:121
  79.3 2.8 %fusion.2 = f32[64,128,32]{1,2,0:T(8,128)S(1)} fusion(bf16[64,128,512]{2,1,0:T(8,128)(2,1)} %param.8, s32[]{:T(128)S(6)} %select_n.148, bf16[16,64,128]{2,0,1:T(8,128)(2,1)S(1)} %collective-permute-done.3, bf16[16,64,128]{2,0,1:T(8,128)(2,1)S(1)} %collective-permute-done.2), kind=kOutput, calls=%fused_computation.3 | convolution fusion | flops 68157440 | bytes 3670020 | tf_op jit(solution)/shard_map/src,ksc->srk/dot_general | solution.py:121
  82.1 2.8 %fusion.31 = f32[64,128,32]{1,2,0:T(8,128)S(1)} fusion(f32[64,128,32]{1,2,0:T(8,128)S(1)} %fusion.2, f32[64,128,32]{1,2,0:T(8,128)S(1)} %fusion.6, f32[64,128,32]{1,2,0:T(8,128)S(1)} %fusion.14, bf16[32,64,128]{2,0,1:T(8,128)(2,1)S(1)} %collective-permute-done, bf16[64,128,512]{2,1,0:T(8,128)(2,1)} %param.8, s32[]{:T(128)S(6)} %select_n.144), kind=kOutput, calls=%fused_computation.23 | convolution fusion | flops 67895296 | bytes 6815748 | tf_op jit(solution)/shard_map/src,ksc->srk/dot_general | solution.py:121
  84.9 2.7 copy.8
  89.8 9.0 %shard_map.57 = f32[2048,128]{1,0:T(8,128)S(1)} custom-call(s32[8192]{0:T(1024)S(1)} %get-tuple-element.9.slot_ref, f32[8192,32]{1,0:T(8,128)S(1)} %bitcast.98), custom_call_target="tpu_custom_call" | custom-call | tf_op jit(solution)/shard_map/pallas_call | solution.py:77
  98.8 26.6 %all_to_all.34 = f32[128,16,128]{2,1,0:T(8,128)S(1)} all-to-all(f32[128,16,128]{2,1,0:T(8,128)S(1)} %bitcast.103), channel_id=1, replica_groups=mesh['iface'=4,'sub'=32] {'iface','sub'}, dimensions={0} | all-to-all | bytes 2097152 | tf_op jit(solution)/shard_map/all_to_all | solution.py:107
  125.3 10.7 %shard_map.58 = f32[8192,32]{1,0:T(8,128)S(1)} custom-call(s32[8192]{0:T(1024)S(1)} %get-tuple-element.10.src_ref, f32[8192,32]{1,0:T(8,128)} %bitcast.97, f32[2048,128]{1,0:T(8,128)S(1)} %bitcast.101), custom_call_target="tpu_custom_call" | custom-call | tf_op jit(solution)/shard_map/pallas_call | solution.py:91
  140.4 2.8 %fusion.12 = f32[64,128,32]{1,2,0:T(8,128)S(1)} fusion(bf16[64,128,512]{2,1,0:T(8,128)(2,1)} %param.8, s32[]{:T(128)S(6)} %select_n.141, bf16[64,128,32]{1,2,0:T(8,128)(2,1)S(1)} %copy.9), kind=kOutput, calls=%fused_computation.13 | convolution fusion | flops 67108864 | bytes 3670020 | tf_op jit(solution)/shard_map/src,ksc->srk/dot_general | solution.py:121
  143.2 8.3 %collective-permute-done.4 = bf16[32,64,128]{2,0,1:T(8,128)(2,1)S(1)} collective-permute-done((bf16[32,64,128]{2,0,1:T(8,128)(2,1)S(1)}, bf16[32,64,128]{2,0,1:T(8,128)(2,1)S(1)}, u32[]{:S(2)}, u32[]{:S(2)}) %collective-permute-start.4) | collective-permute-done | bytes 524320 | tf_op jit(solution)/shard_map/ppermute | solution.py:117
  151.6 3.3 %collective-permute-start.7 = (bf16[16,64,128]{2,0,1:T(8,128)(2,1)S(1)}, bf16[16,64,128]{2,0,1:T(8,128)(2,1)S(1)}, u32[]{:S(2)}, u32[]{:S(2)}) collective-permute-start(bf16[16,64,128]{2,0,1:T(8,128)(2,1)S(1)} %slice.41), channel_id=1, source_target_pairs={{0,96},{32,0},{64,32},{96,64},{1,97},{33,1},{65,33},{97,65},{2,98}... | collective-permute-start | bytes 786440 | tf_op jit(solution)/shard_map/ppermute | solution.py:117
  154.9 2.8 %fusion.4 = f32[64,128,32]{1,2,0:T(8,128)S(1)} fusion(bf16[32,64,128]{2,0,1:T(8,128)(2,1)S(1)} %collective-permute-done.5, bf16[64,128,512]{2,1,0:T(8,128)(2,1)} %param.8, s32[]{:T(128)S(6)} %select_n.146), kind=kOutput, calls=%fused_computation.5 | convolution fusion | flops 67108864 | bytes 3670020 | tf_op jit(solution)/shard_map/src,ksc->srk/dot_general | solution.py:121
  159.4 2.8 %fusion = f32[64,128,32]{1,2,0:T(8,128)S(1)} fusion(bf16[64,128,512]{2,1,0:T(8,128)(2,1)} %param.8, s32[]{:T(128)S(6)} %select_n.148, bf16[16,64,128]{2,0,1:T(8,128)(2,1)S(1)} %collective-permute-done.7, bf16[16,64,128]{2,0,1:T(8,128)(2,1)S(1)} %collective-permute-done.6), kind=kOutput, calls=%fused_computation.1 | convolution fusion | flops 68157440 | bytes 3670020 | tf_op jit(solution)/shard_map/src,ksc->srk/dot_general | solution.py:121
  162.2 2.8 %fusion.28 = f32[64,128,32]{1,2,0:T(8,128)S(1)} fusion(f32[64,128,32]{1,2,0:T(8,128)S(1)} %fusion, f32[64,128,32]{1,2,0:T(8,128)S(1)} %fusion.4, f32[64,128,32]{1,2,0:T(8,128)S(1)} %fusion.12, bf16[32,64,128]{2,0,1:T(8,128)(2,1)S(1)} %collective-permute-done.4, bf16[64,128,512]{2,1,0:T(8,128)(2,1)} %param.8, s32[]{:T(128)S(6)} %select_n.144), kind=kOutput, calls=%fused_computation.22 | convolution fusion | flops 67895296 | bytes 6815748 | tf_op jit(solution)/shard_map/src,ksc->srk/dot_general | solution.py:121
  165.0 2.7 copy.10
  169.9 10.0 %shard_map.59 = f32[2048,128]{1,0:T(8,128)} custom-call(s32[8192]{0:T(1024)S(1)} %get-tuple-element.9.slot_ref, f32[8192,32]{1,0:T(8,128)S(1)} %bitcast.94), custom_call_target="tpu_custom_call" | custom-call | tf_op jit(solution)/shard_map/pallas_call | solution.py:77
  179.9 7.6 %all-to-all-start.2 = ((f32[128,16,128]{2,1,0:T(8,128)}), f32[128,16,128]{2,1,0:T(8,128)S(1)}, u32[]{:S(2)}, u32[]{:S(2)}) async-start(f32[128,16,128]{2,1,0:T(8,128)} %bitcast.15), calls=%async_computation.2 | async-start | bytes 2097152 | tf_op jit(solution)/shard_map/all_to_all | solution.py:107
  187.6 19.1 %all-to-all-done.2 = f32[128,16,128]{2,1,0:T(8,128)S(1)} async-done(((f32[128,16,128]{2,1,0:T(8,128)}), f32[128,16,128]{2,1,0:T(8,128)S(1)}, u32[]{:S(2)}, u32[]{:S(2)}) %all-to-all-start.2) | async-done | bytes 1048608 | tf_op jit(solution)/shard_map/all_to_all | solution.py:107
  206.6 10.7 %shard_map.60 = f32[8192,32]{1,0:T(8,128)S(1)} custom-call(s32[8192]{0:T(1024)S(1)} %get-tuple-element.10.src_ref, f32[8192,32]{1,0:T(8,128)} %bitcast.93, f32[2048,128]{1,0:T(8,128)S(1)} %bitcast.99), custom_call_target="tpu_custom_call" | custom-call | tf_op jit(solution)/shard_map/pallas_call | solution.py:91
  219.3 6.7 %fusion.78 = f32[32,32]{0,1:T(8,128)S(1)} fusion(f32[8192,32]{1,0:T(8,128)S(1)} %shard_map.60), kind=kOutput, calls=%fused_computation.113 | convolution fusion | flops 100663296 | bytes 1052672 | tf_op jit(solution)/shard_map/dot_general | solution.py:206
  226.0 2.8 %gather_fusion = f32[32,32]{1,0:T(8,128)S(1)} fusion(f32[8192,32]{1,0:T(8,128)} %copy-done, s32[1024]{0:T(1024)S(1)} %pad_clamp_fusion), kind=kCustom, calls=%fused_computation | custom fusion | bytes 8320 | tf_op jit(solution)/shard_map/jit(_take)/gather | solution.py:217
  234.6 3.6 %collective-permute-start.13 = (f32[32,64]{0,1:T(8,128)S(1)}, f32[32,64]{0,1:T(8,128)S(1)}, u32[]{:S(2)}, u32[]{:S(2)}) collective-permute-start(f32[32,64]{0,1:T(8,128)S(1)} %fusion.91), channel_id=1, source_target_pairs={{0,12},{1,13},{2,14},{3,15},{4,8},{5,9},{6,10},{7,11},{8,4},{9,5},... | collective-permute-start | bytes 24584 | tf_op jit(solution)/shard_map/ppermute | solution.py:161
  243.5 3.0 %collective-permute-done.14 = f32[32,64]{0,1:T(8,128)S(1)} collective-permute-done((f32[32,64]{0,1:T(8,128)S(1)}, f32[32,64]{0,1:T(8,128)S(1)}, u32[]{:S(2)}, u32[]{:S(2)}) %collective-permute-start.14) | collective-permute-done | bytes 8224 | tf_op jit(solution)/shard_map/ppermute | solution.py:161
  254.5 2.9 %cholesky.44 = f32[32,32]{1,0:T(8,128)S(1)} custom-call(f32[32,32]{1,0:T(8,128)S(1)} %fusion.58), custom_call_target="Cholesky" | custom-call | tf_op jit(solution)/shard_map/jit(cholesky)/cholesky | solution.py:144
  261.9 2.9 %cholesky.55 = f32[32,32]{1,0:T(8,128)S(1)} custom-call(f32[32,32]{1,0:T(8,128)S(1)} %fusion.53), custom_call_target="Cholesky" | custom-call | tf_op jit(solution)/shard_map/jit(cholesky)/cholesky | solution.py:149
  269.0 4.3 %convolution_bitcast_fusion = f32[4,8,64,128]{3,1,2,0:T(8,128)S(1)} fusion(f32[32,32]{1,0:T(8,128)S(1)} %convolution_multiply_fusion, f32[8192,32]{1,0:T(8,128)} %copy-done), kind=kOutput, calls=%fused_computation.17 | convolution fusion | flops 50331648 | bytes 2101248 | tf_op jit(solution)/shard_map/dot_general | solution.py:226
  (86 shorter events, 49.9 us)
Async XLA Ops:
  0.0 3.6 %copy-start.5 = (s32[64,128]{1,0:T(8,128)S(1)}, s32[64,128]{1,0:T(8,128)}, u32[]{:S(2)}) copy-start(s32[64,128]{1,0:T(8,128)} %param.10) | copy-start | bytes 98308
  0.0 3.6 %copy-start.4 = (s32[64,128]{1,0:T(8,128)S(1)}, s32[64,128]{1,0:T(8,128)}, u32[]{:S(2)}) copy-start(s32[64,128]{1,0:T(8,128)} %param.11) | copy-start | bytes 98308
  3.7 2.2 copy-start.2
  57.0 14.4 %collective-permute-start = (bf16[32,64,128]{2,0,1:T(8,128)(2,1)S(1)}, bf16[32,64,128]{2,0,1:T(8,128)(2,1)S(1)}, u32[]{:S(2)}, u32[]{:S(2)}) collective-permute-start(bf16[32,64,128]{2,0,1:T(8,128)(2,1)S(1)} %bitcast.106), channel_id=1, source_target_pairs={{0,32},{32,64},{64,96},{96,0},{1,33},{33,65},{65,97},{97,1},{2,34}... | collective-permute-start | bytes 1572872 | tf_op jit(solution)/shard_map/ppermute | solution.py:117
  57.6 13.8 %collective-permute-start.1 = (bf16[32,64,128]{2,0,1:T(8,128)(2,1)S(1)}, bf16[32,64,128]{2,0,1:T(8,128)(2,1)S(1)}, u32[]{:S(2)}, u32[]{:S(2)}) collective-permute-start(bf16[32,64,128]{2,0,1:T(8,128)(2,1)S(1)} %bitcast.107), channel_id=1, source_target_pairs={{0,96},{32,0},{64,32},{96,64},{1,97},{33,1},{65,33},{97,65},{2,98}... | collective-permute-start | bytes 1572872 | tf_op jit(solution)/shard_map/ppermute | solution.py:117
  71.4 7.9 %collective-permute-start.2 = (bf16[16,64,128]{2,0,1:T(8,128)(2,1)S(1)}, bf16[16,64,128]{2,0,1:T(8,128)(2,1)S(1)}, u32[]{:S(2)}, u32[]{:S(2)}) collective-permute-start(bf16[16,64,128]{2,0,1:T(8,128)(2,1)S(1)} %slice.38), channel_id=1, source_target_pairs={{0,32},{32,64},{64,96},{96,0},{1,33},{33,65},{65,97},{97,1},{2,34}... | collective-permute-start | bytes 786440 | tf_op jit(solution)/shard_map/ppermute | solution.py:117
  71.5 7.8 %collective-permute-start.3 = (bf16[16,64,128]{2,0,1:T(8,128)(2,1)S(1)}, bf16[16,64,128]{2,0,1:T(8,128)(2,1)S(1)}, u32[]{:S(2)}, u32[]{:S(2)}) collective-permute-start(bf16[16,64,128]{2,0,1:T(8,128)(2,1)S(1)} %slice.39), channel_id=1, source_target_pairs={{0,96},{32,0},{64,32},{96,64},{1,97},{33,1},{65,33},{97,65},{2,98}... | collective-permute-start | bytes 786440 | tf_op jit(solution)/shard_map/ppermute | solution.py:117
  87.6 2.2 copy-start.3
  137.1 14.4 %collective-permute-start.4 = (bf16[32,64,128]{2,0,1:T(8,128)(2,1)S(1)}, bf16[32,64,128]{2,0,1:T(8,128)(2,1)S(1)}, u32[]{:S(2)}, u32[]{:S(2)}) collective-permute-start(bf16[32,64,128]{2,0,1:T(8,128)(2,1)S(1)} %bitcast.108), channel_id=1, source_target_pairs={{0,32},{32,64},{64,96},{96,0},{1,33},{33,65},{65,97},{97,1},{2,34}... | collective-permute-start | bytes 1572872 | tf_op jit(solution)/shard_map/ppermute | solution.py:117
  137.7 13.8 %collective-permute-start.5 = (bf16[32,64,128]{2,0,1:T(8,128)(2,1)S(1)}, bf16[32,64,128]{2,0,1:T(8,128)(2,1)S(1)}, u32[]{:S(2)}, u32[]{:S(2)}) collective-permute-start(bf16[32,64,128]{2,0,1:T(8,128)(2,1)S(1)} %bitcast.109), channel_id=1, source_target_pairs={{0,96},{32,0},{64,32},{96,64},{1,97},{33,1},{65,33},{97,65},{2,98}... | collective-permute-start | bytes 1572872 | tf_op jit(solution)/shard_map/ppermute | solution.py:117
  151.5 7.9 %collective-permute-start.6 = (bf16[16,64,128]{2,0,1:T(8,128)(2,1)S(1)}, bf16[16,64,128]{2,0,1:T(8,128)(2,1)S(1)}, u32[]{:S(2)}, u32[]{:S(2)}) collective-permute-start(bf16[16,64,128]{2,0,1:T(8,128)(2,1)S(1)} %slice.40), channel_id=1, source_target_pairs={{0,32},{32,64},{64,96},{96,0},{1,33},{33,65},{65,97},{97,1},{2,34}... | collective-permute-start | bytes 786440 | tf_op jit(solution)/shard_map/ppermute | solution.py:117
  151.6 7.8 %collective-permute-start.7 = (bf16[16,64,128]{2,0,1:T(8,128)(2,1)S(1)}, bf16[16,64,128]{2,0,1:T(8,128)(2,1)S(1)}, u32[]{:S(2)}, u32[]{:S(2)}) collective-permute-start(bf16[16,64,128]{2,0,1:T(8,128)(2,1)S(1)} %slice.41), channel_id=1, source_target_pairs={{0,96},{32,0},{64,32},{96,64},{1,97},{33,1},{65,33},{97,65},{2,98}... | collective-permute-start | bytes 786440 | tf_op jit(solution)/shard_map/ppermute | solution.py:117
  167.7 19.8 %copy-start.6 = (s32[32]{0:T(128)S(1)}, s32[32]{0:T(128)}, u32[]{:S(2)}) copy-start(s32[32]{0:T(128)} %param.12) | copy-start | bytes 388
  167.7 2.2 copy-start.1
  179.9 26.8 %all-to-all-start.2 = ((f32[128,16,128]{2,1,0:T(8,128)}), f32[128,16,128]{2,1,0:T(8,128)S(1)}, u32[]{:S(2)}, u32[]{:S(2)}) async-start(f32[128,16,128]{2,1,0:T(8,128)} %bitcast.15), calls=%async_computation.2 | async-start | bytes 2097152 | tf_op jit(solution)/shard_map/all_to_all | solution.py:107
  217.3 2.0 copy-start
  228.9 1.9 collective-permute-start.8
  229.0 4.1 %collective-permute-start.9 = (f32[32,64]{0,1:T(8,128)S(1)}, f32[32,64]{0,1:T(8,128)S(1)}, u32[]{:S(2)}, u32[]{:S(2)}) collective-permute-start(f32[32,64]{0,1:T(8,128)S(1)} %get-tuple-element.12), channel_id=1, source_target_pairs={{0,2},{1,3},{2,0},{3,1},{4,6},{5,7},{6,4},{7,5},{8,10},{9,11},{10,... | collective-permute-start | bytes 24584 | tf_op jit(solution)/shard_map/ppermute | solution.py:161
  229.3 3.8 %collective-permute-start.10 = (f32[32,64]{0,1:T(8,128)S(1)}, f32[32,64]{0,1:T(8,128)S(1)}, u32[]{:S(2)}, u32[]{:S(2)}) collective-permute-start(f32[32,64]{0,1:T(8,128)S(1)} %get-tuple-element.12), channel_id=1, source_target_pairs={{0,3},{1,2},{2,1},{3,0},{4,7},{5,6},{6,5},{7,4},{8,11},{9,10},{10,... | collective-permute-start | bytes 24584 | tf_op jit(solution)/shard_map/ppermute | solution.py:161
  233.1 5.5 %collective-permute-start.11 = (f32[32,64]{0,1:T(8,128)S(1)}, f32[32,64]{0,1:T(8,128)S(1)}, u32[]{:S(2)}, u32[]{:S(2)}) collective-permute-start(f32[32,64]{0,1:T(8,128)S(1)} %fusion.91), channel_id=1, source_target_pairs={{0,4},{1,5},{2,6},{3,7},{4,0},{5,1},{6,2},{7,3},{8,12},{9,13},{10,... | collective-permute-start | bytes 24584 | tf_op jit(solution)/shard_map/ppermute | solution.py:161
  234.3 4.4 %collective-permute-start.12 = (f32[32,64]{0,1:T(8,128)S(1)}, f32[32,64]{0,1:T(8,128)S(1)}, u32[]{:S(2)}, u32[]{:S(2)}) collective-permute-start(f32[32,64]{0,1:T(8,128)S(1)} %fusion.91), channel_id=1, source_target_pairs={{0,8},{1,9},{2,10},{3,11},{4,12},{5,13},{6,14},{7,15},{8,0},{9,1},... | collective-permute-start | bytes 24584 | tf_op jit(solution)/shard_map/ppermute | solution.py:161
  234.6 6.3 %collective-permute-start.13 = (f32[32,64]{0,1:T(8,128)S(1)}, f32[32,64]{0,1:T(8,128)S(1)}, u32[]{:S(2)}, u32[]{:S(2)}) collective-permute-start(f32[32,64]{0,1:T(8,128)S(1)} %fusion.91), channel_id=1, source_target_pairs={{0,12},{1,13},{2,14},{3,15},{4,8},{5,9},{6,10},{7,11},{8,4},{9,5},... | collective-permute-start | bytes 24584 | tf_op jit(solution)/shard_map/ppermute | solution.py:161
  240.9 5.5 %collective-permute-start.14 = (f32[32,64]{0,1:T(8,128)S(1)}, f32[32,64]{0,1:T(8,128)S(1)}, u32[]{:S(2)}, u32[]{:S(2)}) collective-permute-start(f32[32,64]{0,1:T(8,128)S(1)} %fusion.90), channel_id=1, source_target_pairs={{0,16},{1,17},{2,18},{3,19},{4,20},{5,21},{6,22},{7,23},{8,24},{9,... | collective-permute-start | bytes 24584 | tf_op jit(solution)/shard_map/ppermute | solution.py:161
  246.5 4.8 %collective-permute-start.15 = (f32[32,64]{0,1:T(8,128)S(1)}, f32[32,64]{0,1:T(8,128)S(1)}, u32[]{:S(2)}, u32[]{:S(2)}) collective-permute-start(f32[32,64]{0,1:T(8,128)S(1)} %bitcast.111), channel_id=1, source_target_pairs={{0,32},{32,0},{64,96},{96,64},{1,33},{33,1},{65,97},{97,65},{2,34}... | collective-permute-start | bytes 24584 | tf_op jit(solution)/shard_map/ppermute | solution.py:161
  247.3 5.4 %collective-permute-start.16 = (f32[32,64]{0,1:T(8,128)S(1)}, f32[32,64]{0,1:T(8,128)S(1)}, u32[]{:S(2)}, u32[]{:S(2)}) collective-permute-start(f32[32,64]{0,1:T(8,128)S(1)} %bitcast.112), channel_id=1, source_target_pairs={{0,64},{32,96},{64,0},{96,32},{1,65},{33,97},{65,1},{97,33},{2,66}... | collective-permute-start | bytes 24584 | tf_op jit(solution)/shard_map/ppermute | solution.py:161
  249.3 5.1 %collective-permute-start.17 = (f32[32,64]{0,1:T(8,128)S(1)}, f32[32,64]{0,1:T(8,128)S(1)}, u32[]{:S(2)}, u32[]{:S(2)}) collective-permute-start(f32[32,64]{0,1:T(8,128)S(1)} %bitcast.113), channel_id=1, source_target_pairs={{0,96},{32,64},{64,32},{96,0},{1,97},{33,65},{65,33},{97,1},{2,98}... | collective-permute-start | bytes 24584 | tf_op jit(solution)/shard_map/ppermute | solution.py:161

commit v9 on v8

--- a/solution.py
+++ b/solution.py
@@ -13,7 +13,6 @@
 
 def _pack_kernel(slot_ref, *refs):
     x_refs, o_ref, buf = refs[:-2], refs[-2], refs[-1]
-    buf[...] = jnp.zeros_like(buf)
     offset = 0
     for x_ref in x_refs:
         def body(j, carry, x_ref=x_ref, offset=offset):

time: 275 us -> 274 us (level)
  no operation moved by 1% of the time
where the time goes in v9:
time: 274 us
  Pallas kernels  59.2 us (22%)
  blocking collectives  56.9 us (21%)
  waiting for transfers between devices  50.2 us (18%)
  starting transfers between devices  35.3 us (13%)
  matrix products  34.4 us (13%)
  local copies, waits for them, and re-layouts  23.4 us (9%)
  other arithmetic  14.1 us (5%)
    all_to_all x2, blocking collectives, exchange(): lax.all_to_all(outgoing, ('iface', 'sub'), split_axis=0, concat_axis=0, t...  56.9 us
    pallas_call x3, Pallas kernels, unpack_jump(): pl.pallas_call(functools.partial(_unpack_kernel, first, count), in_specs=...  32 us
    pallas_call x3, Pallas kernels, pack_rows(): pl.pallas_call(_pack_kernel, in_specs=[pl.BlockSpec(memory_space=pltpu.SM...  27.2 us
    dot_general x8, matrix products, product(): jnp.einsum('src,ksc->srk', columns, block, preferred_element_type=jnp.flo...  22.3 us
    ppermute x8, waiting for transfers between devices, shifted(): lax.ppermute(value, 'iface', [(i, (i + shift) % ring) for i in range(ring)])  20.1 us
    all_to_all x1, waiting for transfers between devices, exchange(): lax.all_to_all(outgoing, ('iface', 'sub'), split_axis=0, concat_axis=0, t...  19.1 us
    ppermute x10, starting transfers between devices, group_sum(): lax.ppermute(x, axis, [(i, i ^ m * bit) for i in range(size)])  14.3 us
    ppermute x8, starting transfers between devices, shifted(): lax.ppermute(value, 'iface', [(i, (i + shift) % ring) for i in range(ring)])  13.3 us
  transfers between devices with their start and end apart: 19, of which 11 were waited for; matrix products, arithmetic and copies ran while one was open for 4% of the time, Pallas kernels for 0%

profile of v9, /device:TPU:0, one launch (start us, length us, event | category | flops | bytes accessed | tf_op | source)
XLA Modules:
  0.0 273.7 jit_solution(12805100400700397122)
XLA Ops:
  0.0 3.6 %copy.6 = f32[64,128,32]{2,1,0:T(8,128)} copy(f32[64,128,32]{1,0,2:T(8,128)} %bitcast.110) | data formatting | bytes 2097152 | tf_op jit(solution)/shard_map/transpose | solution.py:197
  5.9 8.7 %shard_map.55 = f32[2048,128]{1,0:T(8,128)S(1)} custom-call(s32[8192]{0:T(1024)S(1)} %get-tuple-element.9.slot_ref, f32[8192,32]{1,0:T(8,128)S(1)} %bitcast.96), custom_call_target="tpu_custom_call" | custom-call | tf_op jit(solution)/shard_map/pallas_call | solution.py:76
  14.6 30.3 %all_to_all.33 = f32[128,16,128]{2,1,0:T(8,128)S(1)} all-to-all(f32[128,16,128]{2,1,0:T(8,128)S(1)} %bitcast.102), channel_id=1, replica_groups=mesh['iface'=4,'sub'=32] {'iface','sub'}, dimensions={0} | all-to-all | bytes 2097152 | tf_op jit(solution)/shard_map/all_to_all | solution.py:106
  44.9 10.7 %shard_map.56 = f32[8192,32]{1,0:T(8,128)S(1)} custom-call(s32[8192]{0:T(1024)S(1)} %get-tuple-element.10.src_ref, f32[8192,32]{1,0:T(8,128)} %bitcast.95, f32[2048,128]{1,0:T(8,128)S(1)} %bitcast.100), custom_call_target="tpu_custom_call" | custom-call | tf_op jit(solution)/shard_map/pallas_call | solution.py:90
  60.0 2.8 %fusion.14 = f32[64,128,32]{1,2,0:T(8,128)S(1)} fusion(bf16[64,128,512]{2,1,0:T(8,128)(2,1)} %param.8, s32[]{:T(128)S(6)} %select_n.141, bf16[64,128,32]{1,2,0:T(8,128)(2,1)S(1)} %copy.7), kind=kOutput, calls=%fused_computation.15 | convolution fusion | flops 67108864 | bytes 3670020 | tf_op jit(solution)/shard_map/src,ksc->srk/dot_general | solution.py:120
  62.8 8.3 %collective-permute-done = bf16[32,64,128]{2,0,1:T(8,128)(2,1)S(1)} collective-permute-done((bf16[32,64,128]{2,0,1:T(8,128)(2,1)S(1)}, bf16[32,64,128]{2,0,1:T(8,128)(2,1)S(1)}, u32[]{:S(2)}, u32[]{:S(2)}) %collective-permute-start) | collective-permute-done | bytes 524320 | tf_op jit(solution)/shard_map/ppermute | solution.py:116
  71.2 3.3 %collective-permute-start.3 = (bf16[16,64,128]{2,0,1:T(8,128)(2,1)S(1)}, bf16[16,64,128]{2,0,1:T(8,128)(2,1)S(1)}, u32[]{:S(2)}, u32[]{:S(2)}) collective-permute-start(bf16[16,64,128]{2,0,1:T(8,128)(2,1)S(1)} %slice.39), channel_id=1, source_target_pairs={{0,96},{32,0},{64,32},{96,64},{1,97},{33,1},{65,33},{97,65},{2,98}... | collective-permute-start | bytes 786440 | tf_op jit(solution)/shard_map/ppermute | solution.py:116
  74.5 2.8 %fusion.6 = f32[64,128,32]{1,2,0:T(8,128)S(1)} fusion(bf16[32,64,128]{2,0,1:T(8,128)(2,1)S(1)} %collective-permute-done.1, bf16[64,128,512]{2,1,0:T(8,128)(2,1)} %param.8, s32[]{:T(128)S(6)} %select_n.146), kind=kOutput, calls=%fused_computation.7 | convolution fusion | flops 67108864 | bytes 3670020 | tf_op jit(solution)/shard_map/src,ksc->srk/dot_general | solution.py:120
  79.0 2.8 %fusion.2 = f32[64,128,32]{1,2,0:T(8,128)S(1)} fusion(bf16[64,128,512]{2,1,0:T(8,128)(2,1)} %param.8, s32[]{:T(128)S(6)} %select_n.148, bf16[16,64,128]{2,0,1:T(8,128)(2,1)S(1)} %collective-permute-done.3, bf16[16,64,128]{2,0,1:T(8,128)(2,1)S(1)} %collective-permute-done.2), kind=kOutput, calls=%fused_computation.3 | convolution fusion | flops 68157440 | bytes 3670020 | tf_op jit(solution)/shard_map/src,ksc->srk/dot_general | solution.py:120
  81.8 2.8 %fusion.31 = f32[64,128,32]{1,2,0:T(8,128)S(1)} fusion(f32[64,128,32]{1,2,0:T(8,128)S(1)} %fusion.2, f32[64,128,32]{1,2,0:T(8,128)S(1)} %fusion.6, f32[64,128,32]{1,2,0:T(8,128)S(1)} %fusion.14, bf16[32,64,128]{2,0,1:T(8,128)(2,1)S(1)} %collective-permute-done, bf16[64,128,512]{2,1,0:T(8,128)(2,1)} %param.8, s32[]{:T(128)S(6)} %select_n.144), kind=kOutput, calls=%fused_computation.23 | convolution fusion | flops 67895296 | bytes 6815748 | tf_op jit(solution)/shard_map/src,ksc->srk/dot_general | solution.py:120
  84.6 2.7 copy.8
  89.5 8.7 %shard_map.57 = f32[2048,128]{1,0:T(8,128)S(1)} custom-call(s32[8192]{0:T(1024)S(1)} %get-tuple-element.9.slot_ref, f32[8192,32]{1,0:T(8,128)S(1)} %bitcast.98), custom_call_target="tpu_custom_call" | custom-call | tf_op jit(solution)/shard_map/pallas_call | solution.py:76
  98.2 26.6 %all_to_all.34 = f32[128,16,128]{2,1,0:T(8,128)S(1)} all-to-all(f32[128,16,128]{2,1,0:T(8,128)S(1)} %bitcast.103), channel_id=1, replica_groups=mesh['iface'=4,'sub'=32] {'iface','sub'}, dimensions={0} | all-to-all | bytes 2097152 | tf_op jit(solution)/shard_map/all_to_all | solution.py:106
  124.8 10.7 %shard_map.58 = f32[8192,32]{1,0:T(8,128)S(1)} custom-call(s32[8192]{0:T(1024)S(1)} %get-tuple-element.10.src_ref, f32[8192,32]{1,0:T(8,128)} %bitcast.97, f32[2048,128]{1,0:T(8,128)S(1)} %bitcast.101), custom_call_target="tpu_custom_call" | custom-call | tf_op jit(solution)/shard_map/pallas_call | solution.py:90
  139.9 2.8 %fusion.12 = f32[64,128,32]{1,2,0:T(8,128)S(1)} fusion(bf16[64,128,512]{2,1,0:T(8,128)(2,1)} %param.8, s32[]{:T(128)S(6)} %select_n.141, bf16[64,128,32]{1,2,0:T(8,128)(2,1)S(1)} %copy.9), kind=kOutput, calls=%fused_computation.13 | convolution fusion | flops 67108864 | bytes 3670020 | tf_op jit(solution)/shard_map/src,ksc->srk/dot_general | solution.py:120
  142.6 8.3 %collective-permute-done.4 = bf16[32,64,128]{2,0,1:T(8,128)(2,1)S(1)} collective-permute-done((bf16[32,64,128]{2,0,1:T(8,128)(2,1)S(1)}, bf16[32,64,128]{2,0,1:T(8,128)(2,1)S(1)}, u32[]{:S(2)}, u32[]{:S(2)}) %collective-permute-start.4) | collective-permute-done | bytes 524320 | tf_op jit(solution)/shard_map/ppermute | solution.py:116
  151.1 3.3 %collective-permute-start.7 = (bf16[16,64,128]{2,0,1:T(8,128)(2,1)S(1)}, bf16[16,64,128]{2,0,1:T(8,128)(2,1)S(1)}, u32[]{:S(2)}, u32[]{:S(2)}) collective-permute-start(bf16[16,64,128]{2,0,1:T(8,128)(2,1)S(1)} %slice.41), channel_id=1, source_target_pairs={{0,96},{32,0},{64,32},{96,64},{1,97},{33,1},{65,33},{97,65},{2,98}... | collective-permute-start | bytes 786440 | tf_op jit(solution)/shard_map/ppermute | solution.py:116
  154.4 2.8 %fusion.4 = f32[64,128,32]{1,2,0:T(8,128)S(1)} fusion(bf16[32,64,128]{2,0,1:T(8,128)(2,1)S(1)} %collective-permute-done.5, bf16[64,128,512]{2,1,0:T(8,128)(2,1)} %param.8, s32[]{:T(128)S(6)} %select_n.146), kind=kOutput, calls=%fused_computation.5 | convolution fusion | flops 67108864 | bytes 3670020 | tf_op jit(solution)/shard_map/src,ksc->srk/dot_general | solution.py:120
  158.9 2.8 %fusion = f32[64,128,32]{1,2,0:T(8,128)S(1)} fusion(bf16[64,128,512]{2,1,0:T(8,128)(2,1)} %param.8, s32[]{:T(128)S(6)} %select_n.148, bf16[16,64,128]{2,0,1:T(8,128)(2,1)S(1)} %collective-permute-done.7, bf16[16,64,128]{2,0,1:T(8,128)(2,1)S(1)} %collective-permute-done.6), kind=kOutput, calls=%fused_computation.1 | convolution fusion | flops 68157440 | bytes 3670020 | tf_op jit(solution)/shard_map/src,ksc->srk/dot_general | solution.py:120
  161.7 2.8 %fusion.28 = f32[64,128,32]{1,2,0:T(8,128)S(1)} fusion(f32[64,128,32]{1,2,0:T(8,128)S(1)} %fusion, f32[64,128,32]{1,2,0:T(8,128)S(1)} %fusion.4, f32[64,128,32]{1,2,0:T(8,128)S(1)} %fusion.12, bf16[32,64,128]{2,0,1:T(8,128)(2,1)S(1)} %collective-permute-done.4, bf16[64,128,512]{2,1,0:T(8,128)(2,1)} %param.8, s32[]{:T(128)S(6)} %select_n.144), kind=kOutput, calls=%fused_computation.22 | convolution fusion | flops 67895296 | bytes 6815748 | tf_op jit(solution)/shard_map/src,ksc->srk/dot_general | solution.py:120
  164.5 2.7 copy.10
  169.4 9.7 %shard_map.59 = f32[2048,128]{1,0:T(8,128)} custom-call(s32[8192]{0:T(1024)S(1)} %get-tuple-element.9.slot_ref, f32[8192,32]{1,0:T(8,128)S(1)} %bitcast.94), custom_call_target="tpu_custom_call" | custom-call | tf_op jit(solution)/shard_map/pallas_call | solution.py:76
  179.1 7.6 %all-to-all-start.2 = ((f32[128,16,128]{2,1,0:T(8,128)}), f32[128,16,128]{2,1,0:T(8,128)S(1)}, u32[]{:S(2)}, u32[]{:S(2)}) async-start(f32[128,16,128]{2,1,0:T(8,128)} %bitcast.15), calls=%async_computation.2 | async-start | bytes 2097152 | tf_op jit(solution)/shard_map/all_to_all | solution.py:106
  186.8 19.1 %all-to-all-done.2 = f32[128,16,128]{2,1,0:T(8,128)S(1)} async-done(((f32[128,16,128]{2,1,0:T(8,128)}), f32[128,16,128]{2,1,0:T(8,128)S(1)}, u32[]{:S(2)}, u32[]{:S(2)}) %all-to-all-start.2) | async-done | bytes 1048608 | tf_op jit(solution)/shard_map/all_to_all | solution.py:106
  205.8 10.7 %shard_map.60 = f32[8192,32]{1,0:T(8,128)S(1)} custom-call(s32[8192]{0:T(1024)S(1)} %get-tuple-element.10.src_ref, f32[8192,32]{1,0:T(8,128)} %bitcast.93, f32[2048,128]{1,0:T(8,128)S(1)} %bitcast.99), custom_call_target="tpu_custom_call" | custom-call | tf_op jit(solution)/shard_map/pallas_call | solution.py:90
  218.5 6.7 %fusion.78 = f32[32,32]{0,1:T(8,128)S(1)} fusion(f32[8192,32]{1,0:T(8,128)S(1)} %shard_map.60), kind=kOutput, calls=%fused_computation.113 | convolution fusion | flops 100663296 | bytes 1052672 | tf_op jit(solution)/shard_map/dot_general | solution.py:205
  225.2 2.8 %gather_fusion = f32[32,32]{1,0:T(8,128)S(1)} fusion(f32[8192,32]{1,0:T(8,128)} %copy-done, s32[1024]{0:T(1024)S(1)} %pad_clamp_fusion), kind=kCustom, calls=%fused_computation | custom fusion | bytes 8320 | tf_op jit(solution)/shard_map/jit(_take)/gather | solution.py:216
  233.8 3.6 %collective-permute-start.13 = (f32[32,64]{0,1:T(8,128)S(1)}, f32[32,64]{0,1:T(8,128)S(1)}, u32[]{:S(2)}, u32[]{:S(2)}) collective-permute-start(f32[32,64]{0,1:T(8,128)S(1)} %fusion.91), channel_id=1, source_target_pairs={{0,12},{1,13},{2,14},{3,15},{4,8},{5,9},{6,10},{7,11},{8,4},{9,5},... | collective-permute-start | bytes 24584 | tf_op jit(solution)/shard_map/ppermute | solution.py:160
  242.7 3.0 %collective-permute-done.14 = f32[32,64]{0,1:T(8,128)S(1)} collective-permute-done((f32[32,64]{0,1:T(8,128)S(1)}, f32[32,64]{0,1:T(8,128)S(1)}, u32[]{:S(2)}, u32[]{:S(2)}) %collective-permute-start.14) | collective-permute-done | bytes 8224 | tf_op jit(solution)/shard_map/ppermute | solution.py:160
  253.7 2.9 %cholesky.44 = f32[32,32]{1,0:T(8,128)S(1)} custom-call(f32[32,32]{1,0:T(8,128)S(1)} %fusion.58), custom_call_target="Cholesky" | custom-call | tf_op jit(solution)/shard_map/jit(cholesky)/cholesky | solution.py:143
  261.1 2.9 %cholesky.55 = f32[32,32]{1,0:T(8,128)S(1)} custom-call(f32[32,32]{1,0:T(8,128)S(1)} %fusion.53), custom_call_target="Cholesky" | custom-call | tf_op jit(solution)/shard_map/jit(cholesky)/cholesky | solution.py:148
  268.2 4.3 %convolution_bitcast_fusion = f32[4,8,64,128]{3,1,2,0:T(8,128)S(1)} fusion(f32[32,32]{1,0:T(8,128)S(1)} %convolution_multiply_fusion, f32[8192,32]{1,0:T(8,128)} %copy-done), kind=kOutput, calls=%fused_computation.17 | convolution fusion | flops 50331648 | bytes 2101248 | tf_op jit(solution)/shard_map/dot_general | solution.py:225
  (86 shorter events, 49.9 us)
Async XLA Ops:
  0.0 3.6 %copy-start.5 = (s32[64,128]{1,0:T(8,128)S(1)}, s32[64,128]{1,0:T(8,128)}, u32[]{:S(2)}) copy-start(s32[64,128]{1,0:T(8,128)} %param.10) | copy-start | bytes 98308
  0.0 3.6 %copy-start.4 = (s32[64,128]{1,0:T(8,128)S(1)}, s32[64,128]{1,0:T(8,128)}, u32[]{:S(2)}) copy-start(s32[64,128]{1,0:T(8,128)} %param.11) | copy-start | bytes 98308
  3.7 2.2 copy-start.2
  56.7 14.4 %collective-permute-start = (bf16[32,64,128]{2,0,1:T(8,128)(2,1)S(1)}, bf16[32,64,128]{2,0,1:T(8,128)(2,1)S(1)}, u32[]{:S(2)}, u32[]{:S(2)}) collective-permute-start(bf16[32,64,128]{2,0,1:T(8,128)(2,1)S(1)} %bitcast.106), channel_id=1, source_target_pairs={{0,32},{32,64},{64,96},{96,0},{1,33},{33,65},{65,97},{97,1},{2,34}... | collective-permute-start | bytes 1572872 | tf_op jit(solution)/shard_map/ppermute | solution.py:116
  57.4 13.8 %collective-permute-start.1 = (bf16[32,64,128]{2,0,1:T(8,128)(2,1)S(1)}, bf16[32,64,128]{2,0,1:T(8,128)(2,1)S(1)}, u32[]{:S(2)}, u32[]{:S(2)}) collective-permute-start(bf16[32,64,128]{2,0,1:T(8,128)(2,1)S(1)} %bitcast.107), channel_id=1, source_target_pairs={{0,96},{32,0},{64,32},{96,64},{1,97},{33,1},{65,33},{97,65},{2,98}... | collective-permute-start | bytes 1572872 | tf_op jit(solution)/shard_map/ppermute | solution.py:116
  71.1 7.9 %collective-permute-start.2 = (bf16[16,64,128]{2,0,1:T(8,128)(2,1)S(1)}, bf16[16,64,128]{2,0,1:T(8,128)(2,1)S(1)}, u32[]{:S(2)}, u32[]{:S(2)}) collective-permute-start(bf16[16,64,128]{2,0,1:T(8,128)(2,1)S(1)} %slice.38), channel_id=1, source_target_pairs={{0,32},{32,64},{64,96},{96,0},{1,33},{33,65},{65,97},{97,1},{2,34}... | collective-permute-start | bytes 786440 | tf_op jit(solution)/shard_map/ppermute | solution.py:116
  71.2 7.8 %collective-permute-start.3 = (bf16[16,64,128]{2,0,1:T(8,128)(2,1)S(1)}, bf16[16,64,128]{2,0,1:T(8,128)(2,1)S(1)}, u32[]{:S(2)}, u32[]{:S(2)}) collective-permute-start(bf16[16,64,128]{2,0,1:T(8,128)(2,1)S(1)} %slice.39), channel_id=1, source_target_pairs={{0,96},{32,0},{64,32},{96,64},{1,97},{33,1},{65,33},{97,65},{2,98}... | collective-permute-start | bytes 786440 | tf_op jit(solution)/shard_map/ppermute | solution.py:116
  87.3 2.2 copy-start.3
  136.6 14.4 %collective-permute-start.4 = (bf16[32,64,128]{2,0,1:T(8,128)(2,1)S(1)}, bf16[32,64,128]{2,0,1:T(8,128)(2,1)S(1)}, u32[]{:S(2)}, u32[]{:S(2)}) collective-permute-start(bf16[32,64,128]{2,0,1:T(8,128)(2,1)S(1)} %bitcast.108), channel_id=1, source_target_pairs={{0,32},{32,64},{64,96},{96,0},{1,33},{33,65},{65,97},{97,1},{2,34}... | collective-permute-start | bytes 1572872 | tf_op jit(solution)/shard_map/ppermute | solution.py:116
  137.2 13.8 %collective-permute-start.5 = (bf16[32,64,128]{2,0,1:T(8,128)(2,1)S(1)}, bf16[32,64,128]{2,0,1:T(8,128)(2,1)S(1)}, u32[]{:S(2)}, u32[]{:S(2)}) collective-permute-start(bf16[32,64,128]{2,0,1:T(8,128)(2,1)S(1)} %bitcast.109), channel_id=1, source_target_pairs={{0,96},{32,0},{64,32},{96,64},{1,97},{33,1},{65,33},{97,65},{2,98}... | collective-permute-start | bytes 1572872 | tf_op jit(solution)/shard_map/ppermute | solution.py:116
  151.0 7.9 %collective-permute-start.6 = (bf16[16,64,128]{2,0,1:T(8,128)(2,1)S(1)}, bf16[16,64,128]{2,0,1:T(8,128)(2,1)S(1)}, u32[]{:S(2)}, u32[]{:S(2)}) collective-permute-start(bf16[16,64,128]{2,0,1:T(8,128)(2,1)S(1)} %slice.40), channel_id=1, source_target_pairs={{0,32},{32,64},{64,96},{96,0},{1,33},{33,65},{65,97},{97,1},{2,34}... | collective-permute-start | bytes 786440 | tf_op jit(solution)/shard_map/ppermute | solution.py:116
  151.1 7.8 %collective-permute-start.7 = (bf16[16,64,128]{2,0,1:T(8,128)(2,1)S(1)}, bf16[16,64,128]{2,0,1:T(8,128)(2,1)S(1)}, u32[]{:S(2)}, u32[]{:S(2)}) collective-permute-start(bf16[16,64,128]{2,0,1:T(8,128)(2,1)S(1)} %slice.41), channel_id=1, source_target_pairs={{0,96},{32,0},{64,32},{96,64},{1,97},{33,1},{65,33},{97,65},{2,98}... | collective-permute-start | bytes 786440 | tf_op jit(solution)/shard_map/ppermute | solution.py:116
  167.2 19.5 %copy-start.6 = (s32[32]{0:T(128)S(1)}, s32[32]{0:T(128)}, u32[]{:S(2)}) copy-start(s32[32]{0:T(128)} %param.12) | copy-start | bytes 388
  167.2 2.2 copy-start.1
  179.1 26.8 %all-to-all-start.2 = ((f32[128,16,128]{2,1,0:T(8,128)}), f32[128,16,128]{2,1,0:T(8,128)S(1)}, u32[]{:S(2)}, u32[]{:S(2)}) async-start(f32[128,16,128]{2,1,0:T(8,128)} %bitcast.15), calls=%async_computation.2 | async-start | bytes 2097152 | tf_op jit(solution)/shard_map/all_to_all | solution.py:106
  216.5 2.0 copy-start
  228.1 1.9 collective-permute-start.8
  228.1 4.1 %collective-permute-start.9 = (f32[32,64]{0,1:T(8,128)S(1)}, f32[32,64]{0,1:T(8,128)S(1)}, u32[]{:S(2)}, u32[]{:S(2)}) collective-permute-start(f32[32,64]{0,1:T(8,128)S(1)} %get-tuple-element.12), channel_id=1, source_target_pairs={{0,2},{1,3},{2,0},{3,1},{4,6},{5,7},{6,4},{7,5},{8,10},{9,11},{10,... | collective-permute-start | bytes 24584 | tf_op jit(solution)/shard_map/ppermute | solution.py:160
  228.5 3.8 %collective-permute-start.10 = (f32[32,64]{0,1:T(8,128)S(1)}, f32[32,64]{0,1:T(8,128)S(1)}, u32[]{:S(2)}, u32[]{:S(2)}) collective-permute-start(f32[32,64]{0,1:T(8,128)S(1)} %get-tuple-element.12), channel_id=1, source_target_pairs={{0,3},{1,2},{2,1},{3,0},{4,7},{5,6},{6,5},{7,4},{8,11},{9,10},{10,... | collective-permute-start | bytes 24584 | tf_op jit(solution)/shard_map/ppermute | solution.py:160
  232.3 5.5 %collective-permute-start.11 = (f32[32,64]{0,1:T(8,128)S(1)}, f32[32,64]{0,1:T(8,128)S(1)}, u32[]{:S(2)}, u32[]{:S(2)}) collective-permute-start(f32[32,64]{0,1:T(8,128)S(1)} %fusion.91), channel_id=1, source_target_pairs={{0,4},{1,5},{2,6},{3,7},{4,0},{5,1},{6,2},{7,3},{8,12},{9,13},{10,... | collective-permute-start | bytes 24584 | tf_op jit(solution)/shard_map/ppermute | solution.py:160
  233.5 4.4 %collective-permute-start.12 = (f32[32,64]{0,1:T(8,128)S(1)}, f32[32,64]{0,1:T(8,128)S(1)}, u32[]{:S(2)}, u32[]{:S(2)}) collective-permute-start(f32[32,64]{0,1:T(8,128)S(1)} %fusion.91), channel_id=1, source_target_pairs={{0,8},{1,9},{2,10},{3,11},{4,12},{5,13},{6,14},{7,15},{8,0},{9,1},... | collective-permute-start | bytes 24584 | tf_op jit(solution)/shard_map/ppermute | solution.py:160
  233.8 6.3 %collective-permute-start.13 = (f32[32,64]{0,1:T(8,128)S(1)}, f32[32,64]{0,1:T(8,128)S(1)}, u32[]{:S(2)}, u32[]{:S(2)}) collective-permute-start(f32[32,64]{0,1:T(8,128)S(1)} %fusion.91), channel_id=1, source_target_pairs={{0,12},{1,13},{2,14},{3,15},{4,8},{5,9},{6,10},{7,11},{8,4},{9,5},... | collective-permute-start | bytes 24584 | tf_op jit(solution)/shard_map/ppermute | solution.py:160
  240.1 5.5 %collective-permute-start.14 = (f32[32,64]{0,1:T(8,128)S(1)}, f32[32,64]{0,1:T(8,128)S(1)}, u32[]{:S(2)}, u32[]{:S(2)}) collective-permute-start(f32[32,64]{0,1:T(8,128)S(1)} %fusion.90), channel_id=1, source_target_pairs={{0,16},{1,17},{2,18},{3,19},{4,20},{5,21},{6,22},{7,23},{8,24},{9,... | collective-permute-start | bytes 24584 | tf_op jit(solution)/shard_map/ppermute | solution.py:160
  245.7 4.8 %collective-permute-start.15 = (f32[32,64]{0,1:T(8,128)S(1)}, f32[32,64]{0,1:T(8,128)S(1)}, u32[]{:S(2)}, u32[]{:S(2)}) collective-permute-start(f32[32,64]{0,1:T(8,128)S(1)} %bitcast.111), channel_id=1, source_target_pairs={{0,32},{32,0},{64,96},{96,64},{1,33},{33,1},{65,97},{97,65},{2,34}... | collective-permute-start | bytes 24584 | tf_op jit(solution)/shard_map/ppermute | solution.py:160
  246.5 5.4 %collective-permute-start.16 = (f32[32,64]{0,1:T(8,128)S(1)}, f32[32,64]{0,1:T(8,128)S(1)}, u32[]{:S(2)}, u32[]{:S(2)}) collective-permute-start(f32[32,64]{0,1:T(8,128)S(1)} %bitcast.112), channel_id=1, source_target_pairs={{0,64},{32,96},{64,0},{96,32},{1,65},{33,97},{65,1},{97,33},{2,66}... | collective-permute-start | bytes 24584 | tf_op jit(solution)/shard_map/ppermute | solution.py:160
  248.4 5.1 %collective-permute-start.17 = (f32[32,64]{0,1:T(8,128)S(1)}, f32[32,64]{0,1:T(8,128)S(1)}, u32[]{:S(2)}, u32[]{:S(2)}) collective-permute-start(f32[32,64]{0,1:T(8,128)S(1)} %bitcast.113), channel_id=1, source_target_pairs={{0,96},{32,64},{64,32},{96,0},{1,97},{33,65},{65,33},{97,1},{2,98}... | collective-permute-start | bytes 24584 | tf_op jit(solution)/shard_map/ppermute | solution.py:160
